TPU v7x, 512 devices: a whole 4x4x16 slice. The times are simulated.
512 devices in a mesh: expert: 64 (over x_hi, z, core), dp: 8 (over x_lo, y).
Axes of the slice: x: 4 (x_hi: 2, x_lo: 2; x = x_hi * 2 + x_lo), y: 4, z: 16, core: 2. Of those that a mesh axis runs over, the one named last changes fastest.
Arguments:
- skip_stream: bfloat16 [4096, 4096], P(('expert', 'dp')), may hold values from -6 to 6
- attention_probes: bfloat16 [4096, 4096], P(('expert', 'dp')), may hold values from -5 to 5
- stored_attention_lookups: bfloat16 [4096, 16, 512], P(('expert', 'dp')), may hold values from -5 to 5
- stored_attention_contents: bfloat16 [4096, 16, 512], P(('expert', 'dp')), may hold values from -6 to 6
- incoming_lookup_entries: bfloat16 [4096, 512], P(('expert', 'dp')), may hold values from -6 to 6
- incoming_content_entries: bfloat16 [4096, 512], P(('expert', 'dp')), may hold values from -6 to 6
- filled_slot_spans: int32 [4096], P(('expert', 'dp')), may hold values from 2 to 16, as said below
- layernorm_gain: float32 [4096], replicated, may hold values from 0.1 to 1.9
- routed_specialist_indices: int32 [4096, 8], P(('expert', 'dp')), may hold values from 0 to 63, all different within a row; in each aligned block of 8 rows (0 to 7, 8 to 15, ...) at most 2 rows name the same one
- routing_probabilities: float32 [4096, 8], P(('expert', 'dp')), may hold values from 0.05 to 1
- admission_limits: int32 [64], replicated, may hold values from 256 to 1024
- swap_indicator: int32 [64], replicated, may hold values from 0 to 1, as said below
- gating_projection_matrix: bfloat16 [64, 768, 4096], P('expert', 'dp'), may hold values from -0.09375 to 0.09375
- widening_projection_matrix: bfloat16 [64, 768, 4096], P('expert', 'dp'), may hold values from -0.09375 to 0.09375
- output_projection_matrix: bfloat16 [64, 768, 4096], P('expert', None, 'dp'), may hold values from -0.21875 to 0.21875
Outputs:
- layer_out: bfloat16 [4096, 4096], P(('expert', 'dp'))
- device_share: float32 [64], P('expert')
- held_gate: bfloat16 [64, 768, 4096], P('expert', 'dp')
- held_up: bfloat16 [64, 768, 4096], P('expert', 'dp')
- held_down: bfloat16 [64, 768, 4096], P('expert', None, 'dp')
Inputs may be any that keep to these rules, and one draw needn't show every extreme that they name: `filled_slot_spans`: each sequence has 2 or more valid slots and some sequence has all 16. `routed_specialist_indices`: in each aligned block of 8 rows (the rows of one device) no expert is named by more than 2 rows; the entries of a row differ. swap_indicator[i] equals swap_indicator[i + 32].
All inputs are finite; a program needn't handle non-finite values.
Results may differ from a plain program's by a relative error of at most 0.017.
Values may be sent and summed in bfloat16 or wider, within the bound.
No kernel may reach another device: no remote copies, remote signals or barrier semaphores. Data moves between devices by JAX's collectives and lax.ppermute only.
A program may use at most 64 MiB of HBM per device.

v0:
```python
import jax
import jax.numpy as jnp
from jax import lax
from jax.sharding import PartitionSpec as P

QH = 32
KVH = 4
HEAD = 128


def swapped(value, axis, stride):
    mask = 2**stride
    pairs = [(source, source ^ mask) for source in range(lax.axis_size(axis))]
    return lax.ppermute(value, axis, pairs)


def attention(query_rows, key_rows, value_rows, new_key, new_value, valid_len):
    seq_count = query_rows.shape[0]
    cache_len = key_rows.shape[1]
    group = QH // KVH
    scale = HEAD ** (-0.5)
    query_view = query_rows.reshape(seq_count, KVH, group, HEAD)
    key_view = key_rows.reshape(seq_count, cache_len, KVH, HEAD)
    value_view = value_rows.reshape(seq_count, cache_len, KVH, HEAD)
    scores = (
        jnp.einsum("skgd,slkd->skgl", query_view, key_view, preferred_element_type=jnp.float32)
        * scale
    )
    valid = lax.broadcasted_iota(jnp.int32, (seq_count, cache_len), 1) < valid_len[:, None]
    scores = jnp.where(valid[:, None, None, :], scores, -1e30)
    own_score = (
        jnp.einsum(
            "skgd,skd->skg",
            query_view,
            new_key.reshape(seq_count, KVH, HEAD),
            preferred_element_type=jnp.float32,
        )
        * scale
    )
    highest = jnp.maximum(jnp.max(scores, axis=-1), own_score)
    weights = jnp.exp(scores - highest[..., None])
    own_weight = jnp.exp(own_score - highest)
    denom = jnp.sum(weights, axis=-1) + own_weight
    probs = (weights / denom[..., None]).astype(jnp.bfloat16)
    own_prob = (own_weight / denom).astype(jnp.bfloat16)
    mixed = jnp.einsum("skgl,slkd->skgd", probs, value_view, preferred_element_type=jnp.float32)
    mixed = mixed + own_prob.astype(jnp.float32)[..., None] * new_value.reshape(
        seq_count, KVH, 1, HEAD
    ).astype(jnp.float32)
    return mixed.reshape(seq_count, QH * HEAD).astype(jnp.bfloat16)


def per_device(
    skip_stream,
    attention_probes,
    stored_attention_lookups,
    stored_attention_contents,
    incoming_lookup_entries,
    incoming_content_entries,
    filled_slot_spans,
    layernorm_gain,
    routed_specialist_indices,
    routing_probabilities,
    admission_limits,
    swap_indicator,
    gating_projection_matrix,
    widening_projection_matrix,
    output_projection_matrix,
):
    experts = lax.axis_size("expert")
    groups = lax.axis_size("dp")
    half_axis = experts // 2
    far_bit = experts.bit_length() - 2
    my_index = lax.axis_index("expert")
    own_weights = (
        gating_projection_matrix[0],
        widening_projection_matrix[0],
        output_projection_matrix[0],
    )
    partner = swapped((own_weights[0], own_weights[1], own_weights[2]), "expert", far_bit)
    take_other = swap_indicator[my_index] == 1
    gate_held = jnp.where(take_other, partner[0], own_weights[0])
    up_held = jnp.where(take_other, partner[1], own_weights[1])
    down_held = jnp.where(take_other, partner[2], own_weights[2])
    retained_specialist = jnp.where(take_other, (my_index + half_axis) % experts, my_index)
    attn = attention(
        attention_probes,
        stored_attention_lookups,
        stored_attention_contents,
        incoming_lookup_entries,
        incoming_content_entries,
        filled_slot_spans,
    )
    stream = skip_stream.astype(jnp.float32) + attn.astype(jnp.float32)
    normed = (
        stream
        * lax.rsqrt(jnp.mean(stream * stream, axis=-1, keepdims=True) + 1e-06)
        * layernorm_gain
    ).astype(jnp.bfloat16)
    seq_rows = skip_stream.shape[0]
    top_count = routed_specialist_indices.shape[1]
    width = skip_stream.shape[1]
    slot_cap = max(2, (seq_rows * top_count + experts - 1) // experts)
    expert_range = lax.broadcasted_iota(jnp.int32, (experts,), 0)
    owner_table = jnp.where(swap_indicator == 1, (expert_range + half_axis) % experts, expert_range)
    gate_used, up_used, down_used = (gate_held, up_held, down_held)
    route_hot = (routed_specialist_indices[:, :, None] == expert_range[None, None, :]).astype(
        jnp.int32
    )
    row_hot = jnp.sum(route_hot, axis=1)
    earlier = jnp.cumsum(row_hot, axis=0) - row_hot
    local_rank = jnp.sum(route_hot * earlier[:, None, :], axis=-1)
    dest_device = jnp.sum(route_hot * owner_table[None, None, :], axis=-1)
    slot_code = dest_device * slot_cap + local_rank
    targets = lax.broadcasted_iota(jnp.int32, (experts * slot_cap,), 0)
    slot_hits = jnp.any(slot_code[:, :, None] == targets[None, None, :], axis=1)
    occupied = jnp.any(slot_hits, axis=0)
    row_range = lax.broadcasted_iota(jnp.int32, (seq_rows, 1), 0)
    source_row = jnp.sum(jnp.where(slot_hits, row_range, 0), axis=0) + jnp.where(
        occupied, 0, seq_rows
    )
    padded_rows = jnp.concatenate([normed, jnp.zeros((1, width), jnp.bfloat16)], axis=0)
    outgoing = padded_rows[source_row].reshape(experts, slot_cap, width)
    marks_out = occupied.astype(jnp.bfloat16).reshape(experts, slot_cap)
    arrived_rows, arrived_marks = (
        lax.all_to_all(outgoing, "expert", split_axis=0, concat_axis=0, tiled=True),
        lax.all_to_all(marks_out, "expert", split_axis=0, concat_axis=0, tiled=True),
    )
    column_rows, column_marks = (
        lax.all_gather(arrived_rows, "dp", axis=1, tiled=True),
        lax.all_gather(arrived_marks, "dp", axis=1, tiled=True),
    )
    gate_val = jnp.einsum("esf,hf->esh", column_rows, gate_used, preferred_element_type=jnp.float32)
    up_val = jnp.einsum("esf,hf->esh", column_rows, up_used, preferred_element_type=jnp.float32)
    hidden = (jax.nn.silu(gate_val) * up_val).astype(jnp.bfloat16)
    occupied_flat = column_marks.astype(jnp.float32).reshape(-1)
    before_count = jnp.cumsum(occupied_flat) - occupied_flat
    limit_offered = admission_limits[retained_specialist].astype(jnp.float32)
    kept_mask = occupied_flat * (before_count < limit_offered).astype(jnp.float32)
    hidden_kept = hidden * kept_mask.reshape(experts, groups * slot_cap, 1).astype(jnp.bfloat16)
    arrived_total = jnp.sum(occupied_flat)
    limit_retained = admission_limits[retained_specialist].astype(jnp.float32)
    device_share = jnp.minimum(arrived_total, limit_retained) / (seq_rows * top_count * groups)
    feature_cols = down_used.shape[1]
    summed = jnp.einsum(
        "esn,nf->esf",
        lax.all_gather(hidden_kept, "dp", axis=2, tiled=True),
        down_used,
        preferred_element_type=jnp.float32,
    )
    results = summed.astype(jnp.bfloat16).reshape(experts, groups, slot_cap, feature_cols)
    returned = lax.all_to_all(
        lax.all_to_all(results, "expert", split_axis=0, concat_axis=0, tiled=True),
        "dp",
        split_axis=1,
        concat_axis=3,
        tiled=True,
    )
    returned_flat = returned.reshape(experts * slot_cap, width)
    picked = returned_flat[slot_code]
    expert_mix = jnp.sum(routing_probabilities[:, :, None] * picked.astype(jnp.float32), axis=1)
    layer_out = (stream + expert_mix).astype(jnp.bfloat16)
    return (layer_out, device_share.reshape(1), gate_held[None], up_held[None], down_held[None])


def solution(mesh):
    in_specs = (
        P(("expert", "dp"), None),
        P(("expert", "dp"), None),
        P(("expert", "dp"), None, None),
        P(("expert", "dp"), None, None),
        P(("expert", "dp"), None),
        P(("expert", "dp"), None),
        P(("expert", "dp")),
        P(),
        P(("expert", "dp"), None),
        P(("expert", "dp"), None),
        P(),
        P(),
        P("expert", "dp", None),
        P("expert", "dp", None),
        P("expert", None, "dp"),
    )
    out_specs = (
        P(("expert", "dp"), None),
        P("expert"),
        P("expert", "dp", None),
        P("expert", "dp", None),
        P("expert", None, "dp"),
    )
    return jax.shard_map(
        per_device, mesh=mesh, in_specs=in_specs, out_specs=out_specs, check_vma=False
    )
```

profile of v0, /device:TPU:1, one launch (start us, length us, event | category | flops | bytes accessed | tf_op | source)
XLA Modules:
  0.0 378.4 jit_solution(7675521622634766968)
XLA Ops:
  7.2 0.8 convert_reduce_fusion
  8.1 0.7 compare_select_fusion.4
  8.7 1.1 select_reduce_fusion.1
  9.9 0.7 iota_compare_fusion.2
  10.7 1.0 fusion.25
  11.7 1.2 fusion.41
  12.9 0.2 fusion.22
  13.2 0.7 bitcast_convert_fusion
  13.9 0.3 fusion.3
  14.1 1.0 multiply_reduce_fusion
  15.2 0.9 multiply_convert_fusion.1
  16.2 1.2 gather_fusion
  17.4 0.7 reshape.194
  18.1 71.3 %all_to_all.34 = bf16[64,2,4096]{2,1,0:T(2,128)(2,1)S(1)} all-to-all(bf16[64,2,4096]{2,1,0:T(2,128)(2,1)S(1)} %reshape.194), channel_id=1, replica_groups=mesh['expert'=64,'dp'=8] {'expert'}, dimensions={0} | all-to-all | bytes 2097152 | tf_op jit(solution)/shard_map/all_to_all | solution.py:126
  89.4 1.7 copy.74
  91.1 2.9 collective-permute-start
  94.1 0.8 reshape.231
  94.9 11.7 %all-to-all-start.1 = ((bf16[64,1,2]{2,1,0:T(2,128)(2,1)}), bf16[64,1,2]{2,1,0:T(2,128)(2,1)S(1)}, u32[]{:S(2)}, u32[]{:S(2)}) async-start(bf16[64,1,2]{2,1,0:T(2,128)(2,1)} %reshape.231), calls=%async_computation.1 | async-start | bytes 65536 | tf_op jit(solution)/shard_map/all_to_all | solution.py:127
  106.6 4.9 %collective-permute-start.1 = (bf16[96,4096]{1,0:T(8,128)(2,1)}, bf16[96,4096]{1,0:T(8,128)(2,1)}, u32[]{:S(2)}, u32[]{:S(2)}) collective-permute-start(bf16[96,4096]{1,0:T(8,128)(2,1)} %bitcast.113), channel_id=1, source_target_pairs={{0,256},{8,264},{16,272},{24,280},{32,288},{40,296},{48,304},{56,3... | collective-permute-start | bytes 2359304 | tf_op jit(solution)/shard_map/ppermute | solution.py:14
  111.5 0.6 dynamic_slice.7
  112.8 0.6 dynamic_slice.8
  114.0 10.8 %all-to-all-done.1 = bf16[64,1,2]{2,1,0:T(2,128)(2,1)S(1)} async-done(((bf16[64,1,2]{2,1,0:T(2,128)(2,1)}), bf16[64,1,2]{2,1,0:T(2,128)(2,1)S(1)}, u32[]{:S(2)}, u32[]{:S(2)}) %all-to-all-start.1) | async-done | bytes 288 | tf_op jit(solution)/shard_map/all_to_all | solution.py:127
  124.9 34.3 %all-gather = bf16[64,1,16]{0,1,2:T(2,128)(2,1)S(1)} all-gather(bf16[64,1,2]{0,1,2:T(2,128)(2,1)S(1)} %copy.76), channel_id=2, replica_groups=mesh['expert'=64,'dp'=8] {'dp'}, dimensions={2}, use_global_device_ids=true | all-gather | bytes 2304 | tf_op jit(solution)/shard_map/all_gather | solution.py:131
  159.3 0.3 reduce-window.9
  159.8 0.1 slice_reduce_fusion
  160.1 51.3 %all-gather.4.cloned.1.call-done = bf16[64,16,4096]{2,0,1:T(8,128)(2,1)} async-done(((bf16[64,2,4096]{2,0,1:T(8,128)(2,1)}), bf16[64,16,4096]{2,0,1:T(8,128)(2,1)}) %all-gather.4.cloned.1.call-update) | async-done | bytes 8388624 | tf_op jit(solution)/shard_map/all_gather | solution.py:130
  211.4 5.9 %fusion.8 = f32[64,16,96]{2,0,1:T(8,128)S(1)} fusion(bf16[64,16,4096]{2,0,1:T(8,128)(2,1)} %all-gather.4.cloned.1.call-done, bf16[96,4096]{1,0:T(8,128)(2,1)S(1)} %collective-permute-done, pred[]{:T(512)} %bitcast.8, bf16[1,96,4096]{2,1,0:T(8,128)(2,1)S(1)} %copy-done.2), kind=kOutput, calls=%fused_computation.14 | convolution fusion | flops 805699584 | bytes 10354689 | tf_op jit(solution)/shard_map/esf,hf->esh/dot_general | solution.py:133
  217.3 2.4 fusion.14
  219.7 1.1 copy.80
  220.8 4.8 %collective-permute-start.2 = (bf16[768,512]{1,0:T(8,128)(2,1)S(1)}, bf16[768,512]{1,0:T(8,128)(2,1)}, u32[]{:S(2)}, u32[]{:S(2)}) collective-permute-start(bf16[768,512]{1,0:T(8,128)(2,1)S(1)} %bitcast.111), channel_id=1, source_target_pairs={{0,256},{8,264},{16,272},{24,280},{32,288},{40,296},{48,304},{56,3... | collective-permute-start | bytes 2359304 | tf_op jit(solution)/shard_map/ppermute | solution.py:14
  225.6 47.9 %all-gather.6.cloned.1.call-done = bf16[64,16,768]{0,1,2:T(8,128)(2,1)} async-done(((bf16[64,16,96]{0,1,2:T(8,128)(2,1)}), bf16[64,16,768]{0,1,2:T(8,128)(2,1)}) %all-gather.6.cloned.1.call-update) | async-done | bytes 1572880 | tf_op jit(solution)/shard_map/all_gather | solution.py:147
  273.5 5.5 %copy.81 = bf16[64,16,768]{2,1,0:T(8,128)(2,1)S(1)} copy(bf16[64,16,768]{0,1,2:T(8,128)(2,1)} %all-gather.6.cloned.1.call-done) | data formatting | bytes 3145728 | tf_op jit(solution)/shard_map/all_gather | solution.py:147
  279.0 2.1 convolution_convert_fusion
  281.1 1.2 reshape.199
  282.4 12.2 %all-to-all-start.2 = ((bf16[64,8,2,512]{3,2,1,0:T(2,128)(2,1)}), bf16[64,8,2,512]{3,2,1,0:T(2,128)(2,1)S(1)}, u32[]{:S(2)}, u32[]{:S(2)}) async-start(bf16[64,8,2,512]{3,2,1,0:T(2,128)(2,1)} %reshape.199), calls=%async_computation.2 | async-start | bytes 2097152 | tf_op jit(solution)/shard_map/all_to_all | solution.py:153
  294.7 0.6 fusion.40
  296.0 2.1 fusion.17
  298.1 2.1 fusion.10
  300.2 46.3 %all-to-all-done.2 = bf16[64,8,2,512]{3,2,1,0:T(2,128)(2,1)S(1)} async-done(((bf16[64,8,2,512]{3,2,1,0:T(2,128)(2,1)}), bf16[64,8,2,512]{3,2,1,0:T(2,128)(2,1)S(1)}, u32[]{:S(2)}, u32[]{:S(2)}) %all-to-all-start.2) | async-done | bytes 1048608 | tf_op jit(solution)/shard_map/all_to_all | solution.py:153
  346.5 1.8 copy.82
  348.3 3.8 %all-to-all-start.3 = ((bf16[64,8,2,512]{3,2,0,1:T(2,128)(2,1)}), bf16[64,8,2,512]{3,2,0,1:T(2,128)(2,1)S(1)}, u32[]{:S(2)}, u32[]{:S(2)}) async-start(bf16[64,8,2,512]{3,2,0,1:T(2,128)(2,1)} %copy.82), calls=%async_computation.3 | async-start | bytes 2097152 | tf_op jit(solution)/shard_map/all_to_all | solution.py:152
  352.1 2.1 fusion.11
  354.2 12.6 %all-to-all-done.3 = bf16[64,8,2,512]{3,2,0,1:T(2,128)(2,1)S(1)} async-done(((bf16[64,8,2,512]{3,2,0,1:T(2,128)(2,1)}), bf16[64,8,2,512]{3,2,0,1:T(2,128)(2,1)S(1)}, u32[]{:S(2)}, u32[]{:S(2)}) %all-to-all-start.3) | async-done | bytes 1048608 | tf_op jit(solution)/shard_map/all_to_all | solution.py:152
  366.8 1.1 copy.83
  367.9 0.4 copy.89
  368.3 0.9 gather_fusion.1
  369.2 0.4 fusion.4
  369.7 0.7 add_convert_fusion
  (53 shorter events, 1.2 us)
Async XLA Ops:
  7.2 6.7 %copy-start = (bf16[8,16,512]{2,1,0:T(8,128)(2,1)S(1)}, bf16[8,16,512]{2,1,0:T(8,128)(2,1)}, u32[]{:S(2)}) copy-start(bf16[8,16,512]{2,1,0:T(8,128)(2,1)} %param.18) | copy-start | bytes 393220
  7.2 204.2 %all-gather.4.cloned.1.call-start = ((), (), s32[]{:S(2)}) async-start(), calls=%async_computation.4 | async-start | bytes 9437184 | tf_op jit(solution)/shard_map/all_gather | solution.py:130
  16.2 74.9 %copy-start.2 = (bf16[1,96,4096]{2,1,0:T(8,128)(2,1)S(1)}, bf16[1,96,4096]{2,1,0:T(8,128)(2,1)}, u32[]{:S(2)}) copy-start(bf16[1,96,4096]{2,1,0:T(8,128)(2,1)} %param.27) | copy-start | bytes 2359300
  16.2 95.3 %copy-start.8 = (s32[64]{0:T(128)S(1)}, s32[64]{0:T(128)}, u32[]{:S(2)}) copy-start(s32[64]{0:T(128)} %param.26) | copy-start | bytes 772
  16.2 96.6 %copy-start.9 = (s32[64]{0:T(128)S(1)}, s32[64]{0:T(128)}, u32[]{:S(2)}) copy-start(s32[64]{0:T(128)} %param.25) | copy-start | bytes 772
  91.1 126.2 %copy-start.3 = (bf16[1,96,4096]{2,1,0:T(8,128)(2,1)S(1)}, bf16[1,96,4096]{2,1,0:T(8,128)(2,1)}, u32[]{:S(2)}) copy-start(bf16[1,96,4096]{2,1,0:T(8,128)(2,1)} %param.28) | copy-start | bytes 2359300
  91.1 69.0 %collective-permute-start = (bf16[96,4096]{1,0:T(8,128)(2,1)S(1)}, bf16[96,4096]{1,0:T(8,128)(2,1)S(1)}, u32[]{:S(2)}, u32[]{:S(2)}) collective-permute-start(bf16[96,4096]{1,0:T(8,128)(2,1)S(1)} %bitcast.112), channel_id=1, source_target_pairs={{0,256},{8,264},{16,272},{24,280},{32,288},{40,296},{48,304},{56,3... | collective-permute-start | bytes 2359304 | tf_op jit(solution)/shard_map/ppermute | solution.py:14
  94.9 29.9 %all-to-all-start.1 = ((bf16[64,1,2]{2,1,0:T(2,128)(2,1)}), bf16[64,1,2]{2,1,0:T(2,128)(2,1)S(1)}, u32[]{:S(2)}, u32[]{:S(2)}) async-start(bf16[64,1,2]{2,1,0:T(2,128)(2,1)} %reshape.231), calls=%async_computation.1 | async-start | bytes 65536 | tf_op jit(solution)/shard_map/all_to_all | solution.py:127
  106.6 166.9 %all-gather.6.cloned.1.call-start = ((), (), s32[]{:S(2)}) async-start(), calls=%async_computation.5 | async-start | bytes 3538944 | tf_op jit(solution)/shard_map/all_gather | solution.py:147
  106.6 110.7 %collective-permute-start.1 = (bf16[96,4096]{1,0:T(8,128)(2,1)}, bf16[96,4096]{1,0:T(8,128)(2,1)}, u32[]{:S(2)}, u32[]{:S(2)}) collective-permute-start(bf16[96,4096]{1,0:T(8,128)(2,1)} %bitcast.113), channel_id=1, source_target_pairs={{0,256},{8,264},{16,272},{24,280},{32,288},{40,296},{48,304},{56,3... | collective-permute-start | bytes 2359304 | tf_op jit(solution)/shard_map/ppermute | solution.py:14
  160.1 59.6 %copy-start.4 = (bf16[96,4096]{1,0:T(8,128)(2,1)}, bf16[96,4096]{1,0:T(8,128)(2,1)S(1)}, u32[]{:S(2)}) copy-start(bf16[96,4096]{1,0:T(8,128)(2,1)S(1)} %collective-permute-done) | copy-start | bytes 2359300
  211.4 5.9 %copy-start.7 = (bf16[64,16,4096]{2,0,1:T(8,128)(2,1)S(1)}, bf16[64,16,4096]{2,0,1:T(8,128)(2,1)}, u32[]{:S(2)}) copy-start(bf16[64,16,4096]{2,0,1:T(8,128)(2,1)} %all-gather.4.cloned.1.call-done) | copy-start | bytes 25165828
  217.3 3.5 copy-start.1
  220.8 58.2 %collective-permute-start.2 = (bf16[768,512]{1,0:T(8,128)(2,1)S(1)}, bf16[768,512]{1,0:T(8,128)(2,1)}, u32[]{:S(2)}, u32[]{:S(2)}) collective-permute-start(bf16[768,512]{1,0:T(8,128)(2,1)S(1)} %bitcast.111), channel_id=1, source_target_pairs={{0,256},{8,264},{16,272},{24,280},{32,288},{40,296},{48,304},{56,3... | collective-permute-start | bytes 2359304 | tf_op jit(solution)/shard_map/ppermute | solution.py:14
  282.4 64.1 %all-to-all-start.2 = ((bf16[64,8,2,512]{3,2,1,0:T(2,128)(2,1)}), bf16[64,8,2,512]{3,2,1,0:T(2,128)(2,1)S(1)}, u32[]{:S(2)}, u32[]{:S(2)}) async-start(bf16[64,8,2,512]{3,2,1,0:T(2,128)(2,1)} %reshape.199), calls=%async_computation.2 | async-start | bytes 2097152 | tf_op jit(solution)/shard_map/all_to_all | solution.py:153
  298.1 71.2 %copy-start.6 = (f32[8,8]{1,0:T(8,128)S(1)}, f32[8,8]{1,0:T(8,128)}, u32[]{:S(2)}) copy-start(f32[8,8]{1,0:T(8,128)} %param.24) | copy-start | bytes 772
  300.2 69.5 %copy-start.5 = (bf16[8,4096]{1,0:T(8,128)(2,1)S(1)}, bf16[8,4096]{1,0:T(8,128)(2,1)}, u32[]{:S(2)}) copy-start(bf16[8,4096]{1,0:T(8,128)(2,1)} %param.15) | copy-start | bytes 196612
  348.3 18.5 %all-to-all-start.3 = ((bf16[64,8,2,512]{3,2,0,1:T(2,128)(2,1)}), bf16[64,8,2,512]{3,2,0,1:T(2,128)(2,1)S(1)}, u32[]{:S(2)}, u32[]{:S(2)}) async-start(bf16[64,8,2,512]{3,2,0,1:T(2,128)(2,1)} %copy.82), calls=%async_computation.3 | async-start | bytes 2097152 | tf_op jit(solution)/shard_map/all_to_all | solution.py:152
Sparse Core Ops, SparseCore 0:
  91.2 120.1 all-gather.3
  220.9 52.5 all-gather.5
where the time goes:
time: 381 us; the launch traced here: 378 us
  waiting for transfers between devices  169 us (44%)
  blocking collectives  106 us (28%)
  starting transfers between devices  40.5 us (11%)
  local copies, waits for them, and re-layouts  18.4 us (5%)
  between operations  17.5 us (5%)
  other arithmetic  14.8 us (4%)
  matrix products  12.8 us (3%)
    all_to_all x1, blocking collectives, per_device(): lax.all_to_all(outgoing, 'expert', split_axis=0, concat_axis=0, tiled=True)  71.3 us
    all_gather x1, waiting for transfers between devices, per_device(): lax.all_gather(arrived_rows, 'dp', axis=1, tiled=True)  51.3 us
    all_gather x1, waiting for transfers between devices, per_device(): lax.all_gather(hidden_kept, 'dp', axis=2, tiled=True)  47.9 us
    all_to_all x1, waiting for transfers between devices, per_device(): lax.all_to_all(results, 'expert', split_axis=0, concat_axis=0, tiled=True)  46.3 us
    all_gather x1, blocking collectives, per_device(): lax.all_gather(arrived_marks, 'dp', axis=1, tiled=True)  34.3 us
    ppermute x3, starting transfers between devices, swapped(): return lax.ppermute(value, axis, pairs)  12.6 us
    all_to_all x1, waiting for transfers between devices, per_device(): lax.all_to_all(lax.all_to_all(results, 'expert', split_axis=0, concat_axi...  12.6 us
    all_to_all x1, starting transfers between devices, per_device(): lax.all_to_all(results, 'expert', split_axis=0, concat_axis=0, tiled=True)  12.2 us
  transfers between devices with their start and end apart: 8, of which 5 were waited for; matrix products, arithmetic and copies ran while one was open for 6% of the time, Pallas kernels for 0%

commit v1 on v0

--- a/solution.py
+++ b/solution.py
@@ -72,17 +72,47 @@
     half_axis = experts // 2
     far_bit = experts.bit_length() - 2
     my_index = lax.axis_index("expert")
+    my_device = my_index * groups + lax.axis_index("dp")
     own_weights = (
         gating_projection_matrix[0],
         widening_projection_matrix[0],
         output_projection_matrix[0],
     )
-    partner = swapped((own_weights[0], own_weights[1], own_weights[2]), "expert", far_bit)
+    partner = swapped(own_weights, "expert", far_bit)
     take_other = swap_indicator[my_index] == 1
     gate_held = jnp.where(take_other, partner[0], own_weights[0])
     up_held = jnp.where(take_other, partner[1], own_weights[1])
     down_held = jnp.where(take_other, partner[2], own_weights[2])
     retained_specialist = jnp.where(take_other, (my_index + half_axis) % experts, my_index)
+
+    seq_rows = skip_stream.shape[0]
+    top_count = routed_specialist_indices.shape[1]
+    width = skip_stream.shape[1]
+    slot_cap = 2
+    expert_range = lax.broadcasted_iota(jnp.int32, (experts,), 0)
+
+    all_routes = lax.all_gather(routed_specialist_indices, ("expert", "dp"), axis=0, tiled=True)
+    all_hot = jnp.sum(
+        (all_routes[:, :, None] == expert_range[None, None, :]).astype(jnp.int32), axis=1
+    )
+    all_rows = lax.broadcasted_iota(jnp.int32, (all_routes.shape[0], 1), 0)
+    before_mine = jnp.sum(jnp.where(all_rows < my_device * seq_rows, all_hot, 0), axis=0)
+    tallies = jnp.sum(all_hot, axis=0)
+
+    route_hot = (routed_specialist_indices[:, :, None] == expert_range[None, None, :]).astype(
+        jnp.int32
+    )
+    row_hot = jnp.sum(route_hot, axis=1)
+    earlier = jnp.cumsum(row_hot, axis=0) - row_hot
+    local_rank = jnp.sum(route_hot * earlier[:, None, :], axis=-1)
+    global_rank = local_rank + jnp.sum(route_hot * before_mine[None, None, :], axis=-1)
+    pair_limit = jnp.sum(route_hot * admission_limits[None, None, :], axis=-1)
+    kept = global_rank < pair_limit
+    held_tally = jnp.sum(jnp.where(expert_range == retained_specialist, tallies, 0))
+    device_share = jnp.minimum(held_tally, admission_limits[retained_specialist]).astype(
+        jnp.float32
+    ) / (seq_rows * top_count * groups)
+
     attn = attention(
         attention_probes,
         stored_attention_lookups,
@@ -97,21 +127,8 @@
         * lax.rsqrt(jnp.mean(stream * stream, axis=-1, keepdims=True) + 1e-06)
         * layernorm_gain
     ).astype(jnp.bfloat16)
-    seq_rows = skip_stream.shape[0]
-    top_count = routed_specialist_indices.shape[1]
-    width = skip_stream.shape[1]
-    slot_cap = max(2, (seq_rows * top_count + experts - 1) // experts)
-    expert_range = lax.broadcasted_iota(jnp.int32, (experts,), 0)
-    owner_table = jnp.where(swap_indicator == 1, (expert_range + half_axis) % experts, expert_range)
-    gate_used, up_used, down_used = (gate_held, up_held, down_held)
-    route_hot = (routed_specialist_indices[:, :, None] == expert_range[None, None, :]).astype(
-        jnp.int32
-    )
-    row_hot = jnp.sum(route_hot, axis=1)
-    earlier = jnp.cumsum(row_hot, axis=0) - row_hot
-    local_rank = jnp.sum(route_hot * earlier[:, None, :], axis=-1)
-    dest_device = jnp.sum(route_hot * owner_table[None, None, :], axis=-1)
-    slot_code = dest_device * slot_cap + local_rank
+
+    slot_code = routed_specialist_indices * slot_cap + local_rank
     targets = lax.broadcasted_iota(jnp.int32, (experts * slot_cap,), 0)
     slot_hits = jnp.any(slot_code[:, :, None] == targets[None, None, :], axis=1)
     occupied = jnp.any(slot_hits, axis=0)
@@ -121,31 +138,20 @@
     )
     padded_rows = jnp.concatenate([normed, jnp.zeros((1, width), jnp.bfloat16)], axis=0)
     outgoing = padded_rows[source_row].reshape(experts, slot_cap, width)
-    marks_out = occupied.astype(jnp.bfloat16).reshape(experts, slot_cap)
-    arrived_rows, arrived_marks = (
-        lax.all_to_all(outgoing, "expert", split_axis=0, concat_axis=0, tiled=True),
-        lax.all_to_all(marks_out, "expert", split_axis=0, concat_axis=0, tiled=True),
-    )
-    column_rows, column_marks = (
-        lax.all_gather(arrived_rows, "dp", axis=1, tiled=True),
-        lax.all_gather(arrived_marks, "dp", axis=1, tiled=True),
-    )
-    gate_val = jnp.einsum("esf,hf->esh", column_rows, gate_used, preferred_element_type=jnp.float32)
-    up_val = jnp.einsum("esf,hf->esh", column_rows, up_used, preferred_element_type=jnp.float32)
+    arrived_rows = lax.all_to_all(outgoing, "expert", split_axis=0, concat_axis=0, tiled=True)
+    column_rows = lax.all_gather(arrived_rows, "dp", axis=1, tiled=True)
+    gate_val = jnp.einsum(
+        "esf,hf->esh", column_rows, own_weights[0], preferred_element_type=jnp.float32
+    )
+    up_val = jnp.einsum(
+        "esf,hf->esh", column_rows, own_weights[1], preferred_element_type=jnp.float32
+    )
     hidden = (jax.nn.silu(gate_val) * up_val).astype(jnp.bfloat16)
-    occupied_flat = column_marks.astype(jnp.float32).reshape(-1)
-    before_count = jnp.cumsum(occupied_flat) - occupied_flat
-    limit_offered = admission_limits[retained_specialist].astype(jnp.float32)
-    kept_mask = occupied_flat * (before_count < limit_offered).astype(jnp.float32)
-    hidden_kept = hidden * kept_mask.reshape(experts, groups * slot_cap, 1).astype(jnp.bfloat16)
-    arrived_total = jnp.sum(occupied_flat)
-    limit_retained = admission_limits[retained_specialist].astype(jnp.float32)
-    device_share = jnp.minimum(arrived_total, limit_retained) / (seq_rows * top_count * groups)
-    feature_cols = down_used.shape[1]
+    feature_cols = own_weights[2].shape[1]
     summed = jnp.einsum(
         "esn,nf->esf",
-        lax.all_gather(hidden_kept, "dp", axis=2, tiled=True),
-        down_used,
+        lax.all_gather(hidden, "dp", axis=2, tiled=True),
+        own_weights[2],
         preferred_element_type=jnp.float32,
     )
     results = summed.astype(jnp.bfloat16).reshape(experts, groups, slot_cap, feature_cols)
@@ -158,7 +164,8 @@
     )
     returned_flat = returned.reshape(experts * slot_cap, width)
     picked = returned_flat[slot_code]
-    expert_mix = jnp.sum(routing_probabilities[:, :, None] * picked.astype(jnp.float32), axis=1)
+    factor = jnp.where(kept, routing_probabilities, 0.0)
+    expert_mix = jnp.sum(factor[:, :, None] * picked.astype(jnp.float32), axis=1)
     layer_out = (stream + expert_mix).astype(jnp.bfloat16)
     return (layer_out, device_share.reshape(1), gate_held[None], up_held[None], down_held[None])
 

time: 381 us -> 1610 us (4.23)
  blocking collectives: 106 us -> 1320 us
  waiting for transfers between devices: 169 us -> 191 us
    all_gather x1, blocking collectives: 34.3 us -> 1250 us  [per_device(): lax.all_gather(routed_specialist_indices, ('expert', 'dp'), axis=0, tiled...]
    all_to_all x1, waiting for transfers between devices: 46.3 us -> 0.4 us  [per_device(): lax.all_to_all(results, 'expert', split_axis=0, concat_axis=0, tiled=True)]
    all_gather x2, waiting for transfers between devices: 99.2 us -> 141 us  [the longest x1 92.2 us: per_device(): column_rows = lax.all_gather(arrived_rows, 'dp', axis=1, tiled=True)]
    ppermute x3, waiting for transfers between devices: 0.01 us -> 40.8 us  [swapped(): return lax.ppermute(value, axis, pairs)]
  transfers between devices with their start and end apart: 8 -> 7, of which waited for: 5 -> 7; matrix products, arithmetic and copies ran while one was open for 6% -> 1% of each run, Pallas kernels for 0% -> 0%
where the time goes in v1:
time: 1610 us
  blocking collectives  1320 us (82%)
  waiting for transfers between devices  191 us (12%)
  starting transfers between devices  33.8 us (2%)
  between operations  17.5 us (1%)
  local copies, waits for them, and re-layouts  17.4 us (1%)
    all_gather x1, blocking collectives, per_device(): lax.all_gather(routed_specialist_indices, ('expert', 'dp'), axis=0, tiled...  1250 us
    all_gather x1, waiting for transfers between devices, per_device(): column_rows = lax.all_gather(arrived_rows, 'dp', axis=1, tiled=True)  92.2 us
    all_to_all x1, blocking collectives, per_device(): lax.all_to_all(outgoing, 'expert', split_axis=0, concat_axis=0, tiled=True)  72 us
    all_gather x1, waiting for transfers between devices, per_device(): lax.all_gather(hidden, 'dp', axis=2, tiled=True)  48.3 us
    ppermute x3, waiting for transfers between devices, swapped(): return lax.ppermute(value, axis, pairs)  40.8 us
  transfers between devices with their start and end apart: 7, of which 7 were waited for; matrix products, arithmetic and copies ran while one was open for 1% of the time, Pallas kernels for 0%

profile of v1, /device:TPU:1, one launch (start us, length us, event | category | flops | bytes accessed | tf_op | source)
XLA Modules:
  0.0 1606.2 jit_solution(4724986277860716594)
XLA Ops:
  7.3 1247.2 %all_gather.9 = s32[4096,8]{1,0:T(8,128)S(1)} all-gather(s32[8,8]{1,0:T(8,128)} %param.23), channel_id=1, replica_groups=mesh['expert'=64,'dp'=8] {'expert','dp'}, dimensions={0}, use_global_device_ids=true | all-gather | bytes 131328 | tf_op jit(solution)/shard_map/all_gather | solution.py:94
  1254.5 0.8 convert_reduce_fusion.2
  1255.3 0.7 iota_compare_fusion.4
  1256.0 1.0 fusion.17
  1257.0 1.2 fusion.28
  1258.2 0.2 fusion.14
  1258.5 0.7 bitcast_convert_fusion
  1259.2 0.3 fusion.4
  1259.5 1.0 multiply_reduce_fusion
  1260.5 0.6 copy.48
  1261.1 1.9 convert_reduce_fusion
  1263.0 0.2 select_reduce_fusion
  1263.2 0.5 select_reduce_fusion.2
  1264.0 1.2 gather_fusion
  1265.2 0.7 reshape.129
  1266.0 72.0 %all_to_all.25 = bf16[64,2,4096]{2,1,0:T(2,128)(2,1)S(1)} all-to-all(bf16[64,2,4096]{2,1,0:T(2,128)(2,1)S(1)} %reshape.129), channel_id=1, replica_groups=mesh['expert'=64,'dp'=8] {'expert'}, dimensions={0} | all-to-all | bytes 2097152 | tf_op jit(solution)/shard_map/all_to_all | solution.py:141
  1338.0 1.7 copy.49
  1339.7 0.2 all-gather.5.cloned.1.call-start
  1339.9 92.2 %all-gather.3.cloned.1.call-done = bf16[64,16,4096]{2,0,1:T(8,128)(2,1)} async-done(((bf16[64,2,4096]{2,0,1:T(8,128)(2,1)}), bf16[64,16,4096]{2,0,1:T(8,128)(2,1)}) %all-gather.3.cloned.1.call-update) | async-done | bytes 8388624 | tf_op jit(solution)/shard_map/all_gather | solution.py:142
  1432.1 5.8 fusion.8
  1438.0 2.4 fusion
  1440.4 1.1 copy.50
  1441.5 48.3 %all-gather.5.cloned.1.call-done = bf16[64,16,768]{0,1,2:T(8,128)(2,1)} async-done(((bf16[64,16,96]{0,1,2:T(8,128)(2,1)}), bf16[64,16,768]{0,1,2:T(8,128)(2,1)}) %all-gather.5.cloned.1.call-update) | async-done | bytes 1572880 | tf_op jit(solution)/shard_map/all_gather | solution.py:153
  1489.8 5.5 copy.51
  1495.3 2.1 convolution_convert_fusion
  1497.4 1.2 reshape.130
  1498.7 18.1 %all-to-all-start.1 = ((bf16[64,8,2,512]{3,2,1,0:T(2,128)(2,1)}), bf16[64,8,2,512]{3,2,1,0:T(2,128)(2,1)S(1)}, u32[]{:S(2)}, u32[]{:S(2)}) async-start(bf16[64,8,2,512]{3,2,1,0:T(2,128)(2,1)} %reshape.130), calls=%async_computation.1 | async-start | bytes 2097152 | tf_op jit(solution)/shard_map/all_to_all | solution.py:159
  1516.7 4.9 collective-permute-start.2
  1521.7 1.9 collective-permute-start.1
  1523.6 4.9 collective-permute-start
  1528.5 0.6 dynamic_slice.6
  1529.8 0.6 dynamic_slice.7
  1530.4 0.6 fusion.26
  1532.4 10.7 collective-permute-done.2
  1543.1 2.1 select_bitcast_fusion
  1545.2 20.9 %collective-permute-done.1 = bf16[96,4096]{1,0:T(8,128)(2,1)S(1)} collective-permute-done((bf16[96,4096]{1,0:T(8,128)(2,1)}, bf16[96,4096]{1,0:T(8,128)(2,1)S(1)}, u32[]{:S(2)}, u32[]{:S(2)}) %collective-permute-start.1) | collective-permute-done | bytes 786464 | tf_op jit(solution)/shard_map/ppermute | solution.py:14
  1566.1 2.1 select_bitcast_fusion.1
  1568.2 0.4 all-to-all-done.1
  1568.6 1.8 copy.52
  1570.4 3.8 all-to-all-start.2
  1574.2 9.1 collective-permute-done
  1583.3 2.1 select_bitcast_fusion.2
  1585.4 9.3 all-to-all-done.2
  1594.7 1.1 copy.53
  1595.8 0.4 copy.59
  1596.2 0.9 gather_fusion.1
  1597.1 0.4 fusion.5
  1597.5 0.7 add_convert_fusion
  (40 shorter events, 0.6 us)
Async XLA Ops:
  7.2 1252.0 %copy-start = (bf16[8,16,512]{2,1,0:T(8,128)(2,1)S(1)}, bf16[8,16,512]{2,1,0:T(8,128)(2,1)}, u32[]{:S(2)}) copy-start(bf16[8,16,512]{2,1,0:T(8,128)(2,1)} %param.18) | copy-start | bytes 393220
  7.2 1256.0 %copy-start.4 = (s32[8,8]{1,0:T(8,128)S(1)}, s32[8,8]{1,0:T(8,128)}, u32[]{:S(2)}) copy-start(s32[8,8]{1,0:T(8,128)} %param.23) | copy-start | bytes 772
  7.2 1256.7 %copy-start.3 = (bf16[8,4096]{1,0:T(8,128)(2,1)S(1)}, bf16[8,4096]{1,0:T(8,128)(2,1)}, u32[]{:S(2)}) copy-start(bf16[8,4096]{1,0:T(8,128)(2,1)} %param.15) | copy-start | bytes 196612
  7.2 1256.0 %copy-start.7 = (s32[64]{0:T(128)S(1)}, s32[64]{0:T(128)}, u32[]{:S(2)}) copy-start(s32[64]{0:T(128)} %param.25) | copy-start | bytes 772
  7.2 1256.7 %copy-start.5 = (f32[4096]{0:T(1024)S(1)}, f32[4096]{0:T(1024)}, u32[]{:S(2)}) copy-start(f32[4096]{0:T(1024)} %param.22) | copy-start | bytes 49156
  7.2 1424.9 %all-gather.3.cloned.1.call-start = ((), (), s32[]{:S(2)}) async-start(), calls=%async_computation.3 | async-start | bytes 9437184 | tf_op jit(solution)/shard_map/all_gather | solution.py:142
  1264.0 168.1 %copy-start.2 = (bf16[1,96,4096]{2,1,0:T(8,128)(2,1)S(1)}, bf16[1,96,4096]{2,1,0:T(8,128)(2,1)}, u32[]{:S(2)}) copy-start(bf16[1,96,4096]{2,1,0:T(8,128)(2,1)} %param.27) | copy-start | bytes 2359300
  1339.7 98.3 %copy-start.1 = (bf16[1,96,4096]{2,1,0:T(8,128)(2,1)S(1)}, bf16[1,96,4096]{2,1,0:T(8,128)(2,1)}, u32[]{:S(2)}) copy-start(bf16[1,96,4096]{2,1,0:T(8,128)(2,1)} %param.28) | copy-start | bytes 2359300
  1339.7 150.1 %all-gather.5.cloned.1.call-start = ((), (), s32[]{:S(2)}) async-start(), calls=%async_computation.4 | async-start | bytes 3538944 | tf_op jit(solution)/shard_map/all_gather | solution.py:153
  1432.1 5.9 copy-start.8
  1440.4 88.1 %copy-start.9 = (s32[64]{0:T(128)S(1)}, s32[64]{0:T(128)}, u32[]{:S(2)}) copy-start(s32[64]{0:T(128)} %param.26) | copy-start | bytes 772
  1440.4 91.9 %copy-start.6 = (f32[8,8]{1,0:T(8,128)S(1)}, f32[8,8]{1,0:T(8,128)}, u32[]{:S(2)}) copy-start(f32[8,8]{1,0:T(8,128)} %param.24) | copy-start | bytes 772
  1498.7 69.9 %all-to-all-start.1 = ((bf16[64,8,2,512]{3,2,1,0:T(2,128)(2,1)}), bf16[64,8,2,512]{3,2,1,0:T(2,128)(2,1)S(1)}, u32[]{:S(2)}, u32[]{:S(2)}) async-start(bf16[64,8,2,512]{3,2,1,0:T(2,128)(2,1)} %reshape.130), calls=%async_computation.1 | async-start | bytes 2097152 | tf_op jit(solution)/shard_map/all_to_all | solution.py:159
  1516.7 26.4 %collective-permute-start.2 = (bf16[768,512]{1,0:T(8,128)(2,1)}, bf16[768,512]{1,0:T(8,128)(2,1)}, u32[]{:S(2)}, u32[]{:S(2)}) collective-permute-start(bf16[768,512]{1,0:T(8,128)(2,1)} %bitcast.80), channel_id=1, source_target_pairs={{0,256},{8,264},{16,272},{24,280},{32,288},{40,296},{48,304},{56,3... | collective-permute-start | bytes 2359304 | tf_op jit(solution)/shard_map/ppermute | solution.py:14
  1521.7 44.5 %collective-permute-start.1 = (bf16[96,4096]{1,0:T(8,128)(2,1)}, bf16[96,4096]{1,0:T(8,128)(2,1)S(1)}, u32[]{:S(2)}, u32[]{:S(2)}) collective-permute-start(bf16[96,4096]{1,0:T(8,128)(2,1)} %bitcast.81), channel_id=1, source_target_pairs={{0,256},{8,264},{16,272},{24,280},{32,288},{40,296},{48,304},{56,3... | collective-permute-start | bytes 2359304 | tf_op jit(solution)/shard_map/ppermute | solution.py:14
  1523.6 59.7 %collective-permute-start = (bf16[96,4096]{1,0:T(8,128)(2,1)}, bf16[96,4096]{1,0:T(8,128)(2,1)S(1)}, u32[]{:S(2)}, u32[]{:S(2)}) collective-permute-start(bf16[96,4096]{1,0:T(8,128)(2,1)} %bitcast.82), channel_id=1, source_target_pairs={{0,256},{8,264},{16,272},{24,280},{32,288},{40,296},{48,304},{56,3... | collective-permute-start | bytes 2359304 | tf_op jit(solution)/shard_map/ppermute | solution.py:14
  1570.4 24.3 %all-to-all-start.2 = ((bf16[64,8,2,512]{3,2,0,1:T(2,128)(2,1)}), bf16[64,8,2,512]{3,2,0,1:T(2,128)(2,1)S(1)}, u32[]{:S(2)}, u32[]{:S(2)}) async-start(bf16[64,8,2,512]{3,2,0,1:T(2,128)(2,1)} %copy.52), calls=%async_computation.2 | async-start | bytes 2097152 | tf_op jit(solution)/shard_map/all_to_all | solution.py:158
Sparse Core Ops, SparseCore 0:
  1339.8 92.2 all-gather.2
  1441.6 48.1 all-gather.4

commit v2 on v1

--- a/solution.py
+++ b/solution.py
@@ -91,18 +91,16 @@
     slot_cap = 2
     expert_range = lax.broadcasted_iota(jnp.int32, (experts,), 0)
 
-    all_routes = lax.all_gather(routed_specialist_indices, ("expert", "dp"), axis=0, tiled=True)
-    all_hot = jnp.sum(
-        (all_routes[:, :, None] == expert_range[None, None, :]).astype(jnp.int32), axis=1
-    )
-    all_rows = lax.broadcasted_iota(jnp.int32, (all_routes.shape[0], 1), 0)
-    before_mine = jnp.sum(jnp.where(all_rows < my_device * seq_rows, all_hot, 0), axis=0)
-    tallies = jnp.sum(all_hot, axis=0)
-
     route_hot = (routed_specialist_indices[:, :, None] == expert_range[None, None, :]).astype(
         jnp.int32
     )
     row_hot = jnp.sum(route_hot, axis=1)
+    local_hist = jnp.sum(row_hot, axis=0).astype(jnp.bfloat16)
+    all_hist = lax.all_gather(local_hist[None], ("expert", "dp"), axis=0, tiled=True)
+    all_hist = all_hist.astype(jnp.int32)
+    device_range = lax.broadcasted_iota(jnp.int32, (all_hist.shape[0], 1), 0)
+    before_mine = jnp.sum(jnp.where(device_range < my_device, all_hist, 0), axis=0)
+    tallies = jnp.sum(all_hist, axis=0)
     earlier = jnp.cumsum(row_hot, axis=0) - row_hot
     local_rank = jnp.sum(route_hot * earlier[:, None, :], axis=-1)
     global_rank = local_rank + jnp.sum(route_hot * before_mine[None, None, :], axis=-1)

time: 1610 us -> 793 us (0.49)
  blocking collectives: 1320 us -> 58.2 us
  waiting for transfers between devices: 191 us -> 637 us
    all_gather x1 -> x0, blocking collectives: 1250 us -> none  [per_device(): lax.all_gather(routed_specialist_indices, ('expert', 'dp'), axis=0, tiled...]
    unnamed x2 -> x4, waiting for transfers between devices: 0.03 us -> 444 us
  transfers between devices with their start and end apart: 7 -> 8, of which waited for: 7 -> 8; matrix products, arithmetic and copies ran while one was open for 1% -> 2% of each run, Pallas kernels for 0% -> 0%
where the time goes in v2:
time: 793 us; the launch traced here: 792 us
  waiting for transfers between devices  637 us (80%)
  blocking collectives  58.2 us (7%)
  starting transfers between devices  33.6 us (4%)
  local copies, waits for them, and re-layouts  17.8 us (2%)
  between operations  17.2 us (2%)
  other arithmetic  15.7 us (2%)
  matrix products  12.8 us (2%)
    unnamed x4, waiting for transfers between devices  444 us
    all_gather x1, waiting for transfers between devices, per_device(): column_rows = lax.all_gather(arrived_rows, 'dp', axis=1, tiled=True)  94.2 us
    all_to_all x1, blocking collectives, per_device(): lax.all_to_all(outgoing, 'expert', split_axis=0, concat_axis=0, tiled=True)  58.2 us
    all_gather x1, waiting for transfers between devices, per_device(): lax.all_gather(hidden, 'dp', axis=2, tiled=True)  48.3 us
    ppermute x3, waiting for transfers between devices, swapped(): return lax.ppermute(value, axis, pairs)  41 us
    all_to_all x1, starting transfers between devices, per_device(): lax.all_to_all(results, 'expert', split_axis=0, concat_axis=0, tiled=True)  18.2 us
  transfers between devices with their start and end apart: 8, of which 8 were waited for; matrix products, arithmetic and copies ran while one was open for 2% of the time, Pallas kernels for 0%

profile of v2, /device:TPU:1, one launch (start us, length us, event | category | flops | bytes accessed | tf_op | source)
XLA Modules:
  0.0 792.2 jit_solution(8014849283501392009)
XLA Ops:
  7.2 0.8 convert_reduce_fusion
  8.1 0.2 dynamic-update-slice
  8.3 0.6 copy-done.4
  9.0 0.7 iota_compare_fusion.2
  9.7 1.0 fusion.17
  10.7 1.2 fusion.29
  12.2 0.7 bitcast_convert_fusion
  12.9 0.3 fusion.4
  13.2 1.0 multiply_reduce_fusion
  14.2 1.0 multiply_convert_fusion
  15.3 443.7 %all-reduce.4.cloned.1.call-done = bf16[32768]{0:T(1024)(128)(2,1)} async-done(((bf16[32768]{0:T(1024)(128)(2,1)}), bf16[32768]{0:T(1024)(128)(2,1)}) %all-reduce.4.cloned.1.call-update) | async-done | bytes 65552
  459.0 0.9 convert_element_type.91
  460.1 1.2 select_reduce_fusion.2
  461.4 0.7 compare_select_fusion
  462.2 1.2 gather_fusion
  463.4 0.7 reshape.136
  464.1 58.2 %all_to_all.25 = bf16[64,2,4096]{2,1,0:T(2,128)(2,1)S(1)} all-to-all(bf16[64,2,4096]{2,1,0:T(2,128)(2,1)S(1)} %reshape.136), channel_id=1, replica_groups=mesh['expert'=64,'dp'=8] {'expert'}, dimensions={0} | all-to-all | bytes 2097152 | tf_op jit(solution)/shard_map/all_to_all | solution.py:139
  522.4 1.7 copy.54
  524.1 94.2 %all-gather.4.cloned.1.call-done = bf16[64,16,4096]{2,0,1:T(8,128)(2,1)} async-done(((bf16[64,2,4096]{2,0,1:T(8,128)(2,1)}), bf16[64,16,4096]{2,0,1:T(8,128)(2,1)}) %all-gather.4.cloned.1.call-update) | async-done | bytes 8388624 | tf_op jit(solution)/shard_map/all_gather | solution.py:140
  618.3 5.9 fusion.8
  624.1 2.4 fusion
  626.6 1.1 copy.55
  627.7 48.3 %all-gather.6.cloned.1.call-done = bf16[64,16,768]{0,1,2:T(8,128)(2,1)} async-done(((bf16[64,16,96]{0,1,2:T(8,128)(2,1)}), bf16[64,16,768]{0,1,2:T(8,128)(2,1)}) %all-gather.6.cloned.1.call-update) | async-done | bytes 1572880 | tf_op jit(solution)/shard_map/all_gather | solution.py:151
  676.0 5.5 copy.56
  681.4 2.1 convolution_convert_fusion
  683.6 1.2 reshape.137
  684.8 18.2 %all-to-all-start.1 = ((bf16[64,8,2,512]{3,2,1,0:T(2,128)(2,1)}), bf16[64,8,2,512]{3,2,1,0:T(2,128)(2,1)S(1)}, u32[]{:S(2)}, u32[]{:S(2)}) async-start(bf16[64,8,2,512]{3,2,1,0:T(2,128)(2,1)} %reshape.137), calls=%async_computation.1 | async-start | bytes 2097152 | tf_op jit(solution)/shard_map/all_to_all | solution.py:157
  703.1 4.9 collective-permute-start.2
  708.0 1.9 collective-permute-start.1
  709.9 4.9 collective-permute-start
  714.8 0.6 dynamic_slice.6
  716.1 0.6 dynamic_slice.7
  716.7 0.6 fusion.26
  718.7 10.7 %collective-permute-done.2 = bf16[768,512]{1,0:T(8,128)(2,1)} collective-permute-done((bf16[768,512]{1,0:T(8,128)(2,1)}, bf16[768,512]{1,0:T(8,128)(2,1)}, u32[]{:S(2)}, u32[]{:S(2)}) %collective-permute-start.2) | collective-permute-done | bytes 786464 | tf_op jit(solution)/shard_map/ppermute | solution.py:14
  729.4 2.1 select_bitcast_fusion
  731.5 20.9 %collective-permute-done.1 = bf16[96,4096]{1,0:T(8,128)(2,1)S(1)} collective-permute-done((bf16[96,4096]{1,0:T(8,128)(2,1)}, bf16[96,4096]{1,0:T(8,128)(2,1)S(1)}, u32[]{:S(2)}, u32[]{:S(2)}) %collective-permute-start.1) | collective-permute-done | bytes 786464 | tf_op jit(solution)/shard_map/ppermute | solution.py:14
  752.4 2.1 select_bitcast_fusion.1
  754.5 0.4 all-to-all-done.1
  754.9 1.8 copy.57
  756.7 3.6 all-to-all-start.2
  760.3 9.3 %collective-permute-done = bf16[96,4096]{1,0:T(8,128)(2,1)S(1)} collective-permute-done((bf16[96,4096]{1,0:T(8,128)(2,1)}, bf16[96,4096]{1,0:T(8,128)(2,1)S(1)}, u32[]{:S(2)}, u32[]{:S(2)}) %collective-permute-start) | collective-permute-done | bytes 786464 | tf_op jit(solution)/shard_map/ppermute | solution.py:14
  769.6 2.1 select_bitcast_fusion.2
  771.7 9.3 %all-to-all-done.2 = bf16[64,8,2,512]{3,2,0,1:T(2,128)(2,1)S(1)} async-done(((bf16[64,8,2,512]{3,2,0,1:T(2,128)(2,1)}), bf16[64,8,2,512]{3,2,0,1:T(2,128)(2,1)S(1)}, u32[]{:S(2)}, u32[]{:S(2)}) %all-to-all-start.2) | async-done | bytes 1048608 | tf_op jit(solution)/shard_map/all_to_all | solution.py:156
  781.0 1.1 copy.58
  782.1 0.4 copy.64
  782.5 0.9 gather_fusion.1
  783.4 0.4 fusion.5
  783.9 0.7 add_convert_fusion
  (43 shorter events, 1.0 us)
Async XLA Ops:
  7.2 5.8 copy-start
  7.2 451.8 %all-reduce.4.cloned.1.call-start = ((), (), s32[]{:S(2)}) async-start(), calls=%async_computation.5 | async-start | bytes 131072
  8.3 0.6 copy-start.4
  9.0 609.3 %all-gather.4.cloned.1.call-start = ((), (), s32[]{:S(2)}) async-start(), calls=%async_computation.3 | async-start | bytes 9437184 | tf_op jit(solution)/shard_map/all_gather | solution.py:140
  462.2 156.1 %copy-start.2 = (bf16[1,96,4096]{2,1,0:T(8,128)(2,1)S(1)}, bf16[1,96,4096]{2,1,0:T(8,128)(2,1)}, u32[]{:S(2)}) copy-start(bf16[1,96,4096]{2,1,0:T(8,128)(2,1)} %param.27) | copy-start | bytes 2359300
  524.0 100.1 %copy-start.1 = (bf16[1,96,4096]{2,1,0:T(8,128)(2,1)S(1)}, bf16[1,96,4096]{2,1,0:T(8,128)(2,1)}, u32[]{:S(2)}) copy-start(bf16[1,96,4096]{2,1,0:T(8,128)(2,1)} %param.28) | copy-start | bytes 2359300
  524.0 151.9 %all-gather.6.cloned.1.call-start = ((), (), s32[]{:S(2)}) async-start(), calls=%async_computation.4 | async-start | bytes 3538944 | tf_op jit(solution)/shard_map/all_gather | solution.py:151
  618.3 5.9 copy-start.7
  626.5 88.3 %copy-start.8 = (s32[64]{0:T(128)S(1)}, s32[64]{0:T(128)}, u32[]{:S(2)}) copy-start(s32[64]{0:T(128)} %param.26) | copy-start | bytes 772
  626.5 89.5 %copy-start.6 = (s32[64]{0:T(128)S(1)}, s32[64]{0:T(128)}, u32[]{:S(2)}) copy-start(s32[64]{0:T(128)} %param.25) | copy-start | bytes 772
  626.6 92.1 %copy-start.5 = (f32[8,8]{1,0:T(8,128)S(1)}, f32[8,8]{1,0:T(8,128)}, u32[]{:S(2)}) copy-start(f32[8,8]{1,0:T(8,128)} %param.24) | copy-start | bytes 772
  684.8 70.1 %all-to-all-start.1 = ((bf16[64,8,2,512]{3,2,1,0:T(2,128)(2,1)}), bf16[64,8,2,512]{3,2,1,0:T(2,128)(2,1)S(1)}, u32[]{:S(2)}, u32[]{:S(2)}) async-start(bf16[64,8,2,512]{3,2,1,0:T(2,128)(2,1)} %reshape.137), calls=%async_computation.1 | async-start | bytes 2097152 | tf_op jit(solution)/shard_map/all_to_all | solution.py:157
  703.1 26.4 %collective-permute-start.2 = (bf16[768,512]{1,0:T(8,128)(2,1)}, bf16[768,512]{1,0:T(8,128)(2,1)}, u32[]{:S(2)}, u32[]{:S(2)}) collective-permute-start(bf16[768,512]{1,0:T(8,128)(2,1)} %bitcast.80), channel_id=1, source_target_pairs={{0,256},{8,264},{16,272},{24,280},{32,288},{40,296},{48,304},{56,3... | collective-permute-start | bytes 2359304 | tf_op jit(solution)/shard_map/ppermute | solution.py:14
  708.0 44.5 %collective-permute-start.1 = (bf16[96,4096]{1,0:T(8,128)(2,1)}, bf16[96,4096]{1,0:T(8,128)(2,1)S(1)}, u32[]{:S(2)}, u32[]{:S(2)}) collective-permute-start(bf16[96,4096]{1,0:T(8,128)(2,1)} %bitcast.81), channel_id=1, source_target_pairs={{0,256},{8,264},{16,272},{24,280},{32,288},{40,296},{48,304},{56,3... | collective-permute-start | bytes 2359304 | tf_op jit(solution)/shard_map/ppermute | solution.py:14
  709.9 59.7 %collective-permute-start = (bf16[96,4096]{1,0:T(8,128)(2,1)}, bf16[96,4096]{1,0:T(8,128)(2,1)S(1)}, u32[]{:S(2)}, u32[]{:S(2)}) collective-permute-start(bf16[96,4096]{1,0:T(8,128)(2,1)} %bitcast.82), channel_id=1, source_target_pairs={{0,256},{8,264},{16,272},{24,280},{32,288},{40,296},{48,304},{56,3... | collective-permute-start | bytes 2359304 | tf_op jit(solution)/shard_map/ppermute | solution.py:14
  754.5 29.3 %copy-start.3 = (bf16[8,4096]{1,0:T(8,128)(2,1)S(1)}, bf16[8,4096]{1,0:T(8,128)(2,1)}, u32[]{:S(2)}) copy-start(bf16[8,4096]{1,0:T(8,128)(2,1)} %param.15) | copy-start | bytes 196612
  756.7 24.3 %all-to-all-start.2 = ((bf16[64,8,2,512]{3,2,0,1:T(2,128)(2,1)}), bf16[64,8,2,512]{3,2,0,1:T(2,128)(2,1)S(1)}, u32[]{:S(2)}, u32[]{:S(2)}) async-start(bf16[64,8,2,512]{3,2,0,1:T(2,128)(2,1)} %copy.57), calls=%async_computation.2 | async-start | bytes 2097152 | tf_op jit(solution)/shard_map/all_to_all | solution.py:156
Sparse Core Ops, SparseCore 0:
  14.0 444.9 all-reduce.3
  524.2 94.0 all-gather.3
  627.8 48.1 all-gather.5

commit v3 on v2

--- a/solution.py
+++ b/solution.py
@@ -80,36 +80,13 @@
     )
     partner = swapped(own_weights, "expert", far_bit)
     take_other = swap_indicator[my_index] == 1
-    gate_held = jnp.where(take_other, partner[0], own_weights[0])
-    up_held = jnp.where(take_other, partner[1], own_weights[1])
-    down_held = jnp.where(take_other, partner[2], own_weights[2])
     retained_specialist = jnp.where(take_other, (my_index + half_axis) % experts, my_index)
 
     seq_rows = skip_stream.shape[0]
-    top_count = routed_specialist_indices.shape[1]
     width = skip_stream.shape[1]
     slot_cap = 2
+    side_cols = 128
     expert_range = lax.broadcasted_iota(jnp.int32, (experts,), 0)
-
-    route_hot = (routed_specialist_indices[:, :, None] == expert_range[None, None, :]).astype(
-        jnp.int32
-    )
-    row_hot = jnp.sum(route_hot, axis=1)
-    local_hist = jnp.sum(row_hot, axis=0).astype(jnp.bfloat16)
-    all_hist = lax.all_gather(local_hist[None], ("expert", "dp"), axis=0, tiled=True)
-    all_hist = all_hist.astype(jnp.int32)
-    device_range = lax.broadcasted_iota(jnp.int32, (all_hist.shape[0], 1), 0)
-    before_mine = jnp.sum(jnp.where(device_range < my_device, all_hist, 0), axis=0)
-    tallies = jnp.sum(all_hist, axis=0)
-    earlier = jnp.cumsum(row_hot, axis=0) - row_hot
-    local_rank = jnp.sum(route_hot * earlier[:, None, :], axis=-1)
-    global_rank = local_rank + jnp.sum(route_hot * before_mine[None, None, :], axis=-1)
-    pair_limit = jnp.sum(route_hot * admission_limits[None, None, :], axis=-1)
-    kept = global_rank < pair_limit
-    held_tally = jnp.sum(jnp.where(expert_range == retained_specialist, tallies, 0))
-    device_share = jnp.minimum(held_tally, admission_limits[retained_specialist]).astype(
-        jnp.float32
-    ) / (seq_rows * top_count * groups)
 
     attn = attention(
         attention_probes,
@@ -126,6 +103,12 @@
         * layernorm_gain
     ).astype(jnp.bfloat16)
 
+    route_hot = (routed_specialist_indices[:, :, None] == expert_range[None, None, :]).astype(
+        jnp.int32
+    )
+    row_hot = jnp.sum(route_hot, axis=1)
+    earlier = jnp.cumsum(row_hot, axis=0) - row_hot
+    local_rank = jnp.sum(route_hot * earlier[:, None, :], axis=-1)
     slot_code = routed_specialist_indices * slot_cap + local_rank
     targets = lax.broadcasted_iota(jnp.int32, (experts * slot_cap,), 0)
     slot_hits = jnp.any(slot_code[:, :, None] == targets[None, None, :], axis=1)
@@ -136,8 +119,32 @@
     )
     padded_rows = jnp.concatenate([normed, jnp.zeros((1, width), jnp.bfloat16)], axis=0)
     outgoing = padded_rows[source_row].reshape(experts, slot_cap, width)
-    arrived_rows = lax.all_to_all(outgoing, "expert", split_axis=0, concat_axis=0, tiled=True)
-    column_rows = lax.all_gather(arrived_rows, "dp", axis=1, tiled=True)
+    partner_hist = jnp.roll(jnp.sum(row_hot, axis=0), -half_axis)
+    col = lax.broadcasted_iota(jnp.int32, (experts, slot_cap, side_cols), 2)
+    slot_of = lax.broadcasted_iota(jnp.int32, (experts, slot_cap, side_cols), 1)
+    side = jnp.where(
+        col == 0,
+        occupied.reshape(experts, slot_cap, 1).astype(jnp.float32),
+        jnp.where(
+            (col == 1) & (slot_of == 0), partner_hist[:, None, None].astype(jnp.float32), 0.0
+        ),
+    ).astype(jnp.bfloat16)
+    payload = jnp.concatenate([outgoing, side], axis=-1)
+    arrived = lax.all_to_all(payload, "expert", split_axis=0, concat_axis=0, tiled=True)
+    column = lax.all_gather(arrived, "dp", axis=1, tiled=True)
+    column_rows = column[:, :, :width]
+    occupied_flat = column[:, :, width].astype(jnp.float32).reshape(-1)
+    partner_total = jnp.sum(column[:, :, width + 1].astype(jnp.float32))
+    before_count = jnp.cumsum(occupied_flat) - occupied_flat
+    kept_mask = occupied_flat * (
+        before_count < admission_limits[my_index].astype(jnp.float32)
+    ).astype(jnp.float32)
+    own_total = jnp.sum(occupied_flat)
+    held_tally = jnp.where(take_other, partner_total, own_total)
+    device_share = jnp.minimum(
+        held_tally, admission_limits[retained_specialist].astype(jnp.float32)
+    ) / (seq_rows * routed_specialist_indices.shape[1] * groups)
+
     gate_val = jnp.einsum(
         "esf,hf->esh", column_rows, own_weights[0], preferred_element_type=jnp.float32
     )
@@ -145,13 +152,15 @@
         "esf,hf->esh", column_rows, own_weights[1], preferred_element_type=jnp.float32
     )
     hidden = (jax.nn.silu(gate_val) * up_val).astype(jnp.bfloat16)
+    hidden_kept = hidden * kept_mask.reshape(experts, groups * slot_cap, 1).astype(jnp.bfloat16)
     feature_cols = own_weights[2].shape[1]
     summed = jnp.einsum(
         "esn,nf->esf",
-        lax.all_gather(hidden, "dp", axis=2, tiled=True),
+        lax.all_gather(hidden_kept, "dp", axis=2, tiled=True),
         own_weights[2],
         preferred_element_type=jnp.float32,
     )
+    summed, partner = lax.optimization_barrier((summed, partner))
     results = summed.astype(jnp.bfloat16).reshape(experts, groups, slot_cap, feature_cols)
     returned = lax.all_to_all(
         lax.all_to_all(results, "expert", split_axis=0, concat_axis=0, tiled=True),
@@ -162,9 +171,11 @@
     )
     returned_flat = returned.reshape(experts * slot_cap, width)
     picked = returned_flat[slot_code]
-    factor = jnp.where(kept, routing_probabilities, 0.0)
-    expert_mix = jnp.sum(factor[:, :, None] * picked.astype(jnp.float32), axis=1)
+    expert_mix = jnp.sum(routing_probabilities[:, :, None] * picked.astype(jnp.float32), axis=1)
     layer_out = (stream + expert_mix).astype(jnp.bfloat16)
+    gate_held = jnp.where(take_other, partner[0], own_weights[0])
+    up_held = jnp.where(take_other, partner[1], own_weights[1])
+    down_held = jnp.where(take_other, partner[2], own_weights[2])
     return (layer_out, device_share.reshape(1), gate_held[None], up_held[None], down_held[None])
 
 

time: 793 us -> 402 us (0.51)
  waiting for transfers between devices: 637 us -> 220 us
  blocking collectives: 58.2 us -> 72.5 us
  local copies, waits for them, and re-layouts: 17.8 us -> 26.4 us
    unnamed x4 -> x2, waiting for transfers between devices: 444 us -> 0.03 us
    all_to_all x1, waiting for transfers between devices: 0.4 us -> 43.8 us  [per_device(): lax.all_to_all(results, 'expert', split_axis=0, concat_axis=0, tiled=True)]
    ppermute x3, waiting for transfers between devices: 41 us -> 0.01 us  [swapped(): return lax.ppermute(value, axis, pairs)]
    all_gather x2, waiting for transfers between devices: 142 us -> 163 us  [the longest x1 95 us: per_device(): column = lax.all_gather(arrived, 'dp', axis=1, tiled=True)]
    all_to_all x1, blocking collectives: 58.2 us -> 72.5 us  [per_device(): lax.all_to_all(payload, 'expert', split_axis=0, concat_axis=0, tiled=True)]
    slice x0 -> x3, local copies, waits for them, and re-layouts: none -> 8.77 us  [the longest x1 7.73 us: per_device(): column_rows = column[:, :, :width]]
  transfers between devices with their start and end apart: 8 -> 7, of which waited for: 8 -> 4; matrix products, arithmetic and copies ran while one was open for 2% -> 4% of each run, Pallas kernels for 0% -> 0%
where the time goes in v3:
time: 402 us; the launch traced here: 400 us
  waiting for transfers between devices  220 us (55%)
  blocking collectives  72.5 us (18%)
  starting transfers between devices  30.5 us (8%)
  local copies, waits for them, and re-layouts  26.4 us (7%)
  between operations  18.8 us (5%)
  matrix products  18.6 us (5%)
  other arithmetic  14.1 us (4%)
    all_gather x1, waiting for transfers between devices, per_device(): column = lax.all_gather(arrived, 'dp', axis=1, tiled=True)  95 us
    all_to_all x1, blocking collectives, per_device(): lax.all_to_all(payload, 'expert', split_axis=0, concat_axis=0, tiled=True)  72.5 us
    all_gather x1, waiting for transfers between devices, per_device(): lax.all_gather(hidden_kept, 'dp', axis=2, tiled=True)  67.9 us
    all_to_all x1, waiting for transfers between devices, per_device(): lax.all_to_all(results, 'expert', split_axis=0, concat_axis=0, tiled=True)  43.8 us
    all_to_all x1, starting transfers between devices, per_device(): lax.all_to_all(results, 'expert', split_axis=0, concat_axis=0, tiled=True)  15.3 us
    all_to_all x1, waiting for transfers between devices, per_device(): lax.all_to_all(lax.all_to_all(results, 'expert', split_axis=0, concat_axi...  12.7 us
    ppermute x3, starting transfers between devices, swapped(): return lax.ppermute(value, axis, pairs)  11.4 us
    dot_general x1, matrix products, per_device(): jnp.einsum('esf,hf->esh', column_rows, own_weights[0], preferred_element_...  8.25 us
  transfers between devices with their start and end apart: 7, of which 4 were waited for; matrix products, arithmetic and copies ran while one was open for 4% of the time, Pallas kernels for 0%

profile of v3, /device:TPU:1, one launch (start us, length us, event | category | flops | bytes accessed | tf_op | source)
XLA Modules:
  0.0 400.3 jit_solution(3914790186504233417)
XLA Ops:
  7.3 0.7 iota_compare_fusion.2
  8.0 1.0 fusion.31
  9.0 1.2 fusion.43
  10.3 0.2 fusion.26
  10.5 0.7 bitcast_convert_fusion
  11.2 0.3 fusion.16
  11.5 0.2 multiply_reduce_fusion
  11.8 0.3 select_reduce_fusion
  12.4 1.2 gather_fusion
  13.6 0.7 reshape.207
  14.4 0.1 reshape.216
  14.6 0.2 fusion.28
  14.8 1.1 pad_maximum_fusion
  15.9 72.5 %all_to_all.25 = bf16[64,2,4224]{2,1,0:T(2,128)(2,1)S(1)} all-to-all(bf16[64,2,4224]{2,1,0:T(2,128)(2,1)S(1)} %pad_maximum_fusion), channel_id=1, replica_groups=mesh['expert'=64,'dp'=8] {'expert'}, dimensions={0} | all-to-all | bytes 2162688 | tf_op jit(solution)/shard_map/all_to_all | solution.py:133
  88.4 1.2 copy.77
  89.6 0.2 all-gather.5.cloned.1.call-start
  89.9 0.6 dynamic_slice.10
  91.1 0.6 fusion.41
  92.4 95.0 %all-gather.3.cloned.1.call-done = bf16[64,16,4224]{2,0,1:T(8,128)(2,1)} async-done(((bf16[64,2,4224]{2,0,1:T(8,128)(2,1)}), bf16[64,16,4224]{2,0,1:T(8,128)(2,1)}) %all-gather.3.cloned.1.call-update) | async-done | bytes 8650768 | tf_op jit(solution)/shard_map/all_gather | solution.py:134
  187.4 1.0 slice.36
  188.3 0.2 copy.90
  188.7 0.3 reduce-window.9
  189.5 0.6 convert_reduce_fusion.3
  190.2 7.7 %slice.35 = bf16[64,16,4096]{2,0,1:T(8,128)(2,1)} slice(bf16[64,16,4224]{2,0,1:T(8,128)(2,1)} %all-gather.3.cloned.1.call-done), slice={[0:64], [0:16], [0:4096]} | slice | bytes 16777216 | tf_op jit(solution)/shard_map/slice | solution.py:135
  197.9 8.2 %fusion.2 = f32[64,16,96]{2,1,0:T(8,128)S(1)} fusion(bf16[64,16,4096]{2,0,1:T(8,128)(2,1)} %slice.35, bf16[1,96,4096]{2,1,0:T(8,128)(2,1)} %param.27), kind=kOutput, calls=%fused_computation.4 | convolution fusion | flops 805306368 | bytes 9568256 | tf_op jit(solution)/shard_map/esf,hf->esh/dot_general | solution.py:148
  206.2 5.8 %fusion.10 = bf16[64,16,96]{2,1,0:T(8,128)(2,1)S(1)} fusion(bf16[64,16,4096]{2,0,1:T(8,128)(2,1)S(1)} %copy-done.1, bf16[1,96,4096]{2,1,0:T(8,128)(2,1)} %param.28, f32[64,16,96]{2,1,0:T(8,128)S(1)} %fusion.2, bf16[64,16]{1,0:T(8,128)(2,1)S(1)} %copy.82), kind=kOutput, calls=%fused_computation.8 | convolution fusion | flops 805994496 | bytes 9766912 | tf_op jit(solution)/shard_map/esf,hf->esh/dot_general | solution.py:151
  212.0 1.2 copy.83
  213.2 4.3 %collective-permute-start = (bf16[96,4096]{1,0:T(8,128)(2,1)}, bf16[96,4096]{1,0:T(8,128)(2,1)}, u32[]{:S(2)}, u32[]{:S(2)}) collective-permute-start(bf16[96,4096]{1,0:T(8,128)(2,1)} %bitcast.8), channel_id=1, source_target_pairs={{0,256},{8,264},{16,272},{24,280},{32,288},{40,296},{48,304},{56,3... | collective-permute-start | bytes 2359304 | tf_op jit(solution)/shard_map/ppermute | solution.py:14
  217.5 2.5 collective-permute-start.1
  220.0 4.6 %collective-permute-start.2 = (bf16[768,512]{1,0:T(8,128)(2,1)}, bf16[768,512]{1,0:T(8,128)(2,1)}, u32[]{:S(2)}, u32[]{:S(2)}) collective-permute-start(bf16[768,512]{1,0:T(8,128)(2,1)} %bitcast.14), channel_id=1, source_target_pairs={{0,256},{8,264},{16,272},{24,280},{32,288},{40,296},{48,304},{56,3... | collective-permute-start | bytes 2359304 | tf_op jit(solution)/shard_map/ppermute | solution.py:14
  224.6 67.9 %all-gather.5.cloned.1.call-done = bf16[64,16,768]{0,1,2:T(8,128)(2,1)} async-done(((bf16[64,16,96]{0,1,2:T(8,128)(2,1)}), bf16[64,16,768]{0,1,2:T(8,128)(2,1)}) %all-gather.5.cloned.1.call-update) | async-done | bytes 1572880 | tf_op jit(solution)/shard_map/all_gather | solution.py:159
  292.5 5.5 %copy.84 = bf16[64,16,768]{2,1,0:T(8,128)(2,1)S(1)} copy(bf16[64,16,768]{0,1,2:T(8,128)(2,1)} %all-gather.5.cloned.1.call-done) | data formatting | bytes 3145728 | tf_op jit(solution)/shard_map/all_gather | solution.py:159
  298.0 2.1 fusion.18
  300.1 1.3 reshape.211
  301.4 15.3 %all-to-all-start.1 = ((bf16[64,8,2,512]{3,2,1,0:T(2,128)(2,1)}), bf16[64,8,2,512]{3,2,1,0:T(2,128)(2,1)S(1)}, u32[]{:S(2)}, u32[]{:S(2)}) async-start(bf16[64,8,2,512]{3,2,1,0:T(2,128)(2,1)} %reshape.211), calls=%async_computation.1 | async-start | bytes 2097152 | tf_op jit(solution)/shard_map/all_to_all | solution.py:166
  317.5 1.8 convert_reduce_fusion
  320.5 2.1 select_bitcast_fusion
  322.6 2.1 select_bitcast_fusion.1
  324.7 43.8 %all-to-all-done.1 = bf16[64,8,2,512]{3,2,1,0:T(2,128)(2,1)S(1)} async-done(((bf16[64,8,2,512]{3,2,1,0:T(2,128)(2,1)}), bf16[64,8,2,512]{3,2,1,0:T(2,128)(2,1)S(1)}, u32[]{:S(2)}, u32[]{:S(2)}) %all-to-all-start.1) | async-done | bytes 1048608 | tf_op jit(solution)/shard_map/all_to_all | solution.py:166
  368.6 1.8 copy.85
  370.4 3.6 all-to-all-start.2
  374.0 2.1 select_bitcast_fusion.2
  376.1 12.7 %all-to-all-done.2 = bf16[64,8,2,512]{3,2,0,1:T(2,128)(2,1)S(1)} async-done(((bf16[64,8,2,512]{3,2,0,1:T(2,128)(2,1)}), bf16[64,8,2,512]{3,2,0,1:T(2,128)(2,1)S(1)}, u32[]{:S(2)}, u32[]{:S(2)}) %all-to-all-start.2) | async-done | bytes 1048608 | tf_op jit(solution)/shard_map/all_to_all | solution.py:165
  388.8 1.1 copy.86
  389.9 0.4 copy.94
  390.3 0.9 gather_fusion.1
  391.2 0.4 fusion.17
  391.7 0.7 add_convert_fusion
  (53 shorter events, 1.6 us)
Async XLA Ops:
  7.2 4.1 %copy-start = (bf16[8,16,512]{2,1,0:T(8,128)(2,1)S(1)}, bf16[8,16,512]{2,1,0:T(8,128)(2,1)}, u32[]{:S(2)}) copy-start(bf16[8,16,512]{2,1,0:T(8,128)(2,1)} %param.18) | copy-start | bytes 393220
  7.2 4.3 %copy-start.2 = (bf16[8,4096]{1,0:T(8,128)(2,1)S(1)}, bf16[8,4096]{1,0:T(8,128)(2,1)}, u32[]{:S(2)}) copy-start(bf16[8,4096]{1,0:T(8,128)(2,1)} %param.15) | copy-start | bytes 196612
  7.2 4.5 %copy-start.3 = (s32[8,8]{1,0:T(8,128)S(1)}, s32[8,8]{1,0:T(8,128)}, u32[]{:S(2)}) copy-start(s32[8,8]{1,0:T(8,128)} %param.23) | copy-start | bytes 772
  7.2 5.1 %copy-start.4 = (f32[4096]{0:T(1024)S(1)}, f32[4096]{0:T(1024)}, u32[]{:S(2)}) copy-start(f32[4096]{0:T(1024)} %param.22) | copy-start | bytes 49156
  7.2 180.1 %all-gather.3.cloned.1.call-start = ((), (), s32[]{:S(2)}) async-start(), calls=%async_computation.3 | async-start | bytes 9732096 | tf_op jit(solution)/shard_map/all_gather | solution.py:134
  88.4 1.4 copy-start.7
  88.4 2.7 copy-start.6
  89.6 202.9 %all-gather.5.cloned.1.call-start = ((), (), s32[]{:S(2)}) async-start(), calls=%async_computation.4 | async-start | bytes 3538944 | tf_op jit(solution)/shard_map/all_gather | solution.py:159
  197.9 8.3 %copy-start.1 = (bf16[64,16,4096]{2,0,1:T(8,128)(2,1)S(1)}, bf16[64,16,4096]{2,0,1:T(8,128)(2,1)}, u32[]{:S(2)}) copy-start(bf16[64,16,4096]{2,0,1:T(8,128)(2,1)} %slice.35) | copy-start | bytes 25165828
  213.2 86.9 %collective-permute-start = (bf16[96,4096]{1,0:T(8,128)(2,1)}, bf16[96,4096]{1,0:T(8,128)(2,1)}, u32[]{:S(2)}, u32[]{:S(2)}) collective-permute-start(bf16[96,4096]{1,0:T(8,128)(2,1)} %bitcast.8), channel_id=1, source_target_pairs={{0,256},{8,264},{16,272},{24,280},{32,288},{40,296},{48,304},{56,3... | collective-permute-start | bytes 2359304 | tf_op jit(solution)/shard_map/ppermute | solution.py:14
  217.5 82.6 %collective-permute-start.1 = (bf16[96,4096]{1,0:T(8,128)(2,1)}, bf16[96,4096]{1,0:T(8,128)(2,1)}, u32[]{:S(2)}, u32[]{:S(2)}) collective-permute-start(bf16[96,4096]{1,0:T(8,128)(2,1)} %bitcast.10), channel_id=1, source_target_pairs={{0,256},{8,264},{16,272},{24,280},{32,288},{40,296},{48,304},{56,3... | collective-permute-start | bytes 2359304 | tf_op jit(solution)/shard_map/ppermute | solution.py:14
  220.0 80.1 %collective-permute-start.2 = (bf16[768,512]{1,0:T(8,128)(2,1)}, bf16[768,512]{1,0:T(8,128)(2,1)}, u32[]{:S(2)}, u32[]{:S(2)}) collective-permute-start(bf16[768,512]{1,0:T(8,128)(2,1)} %bitcast.14), channel_id=1, source_target_pairs={{0,256},{8,264},{16,272},{24,280},{32,288},{40,296},{48,304},{56,3... | collective-permute-start | bytes 2359304 | tf_op jit(solution)/shard_map/ppermute | solution.py:14
  301.4 67.2 %all-to-all-start.1 = ((bf16[64,8,2,512]{3,2,1,0:T(2,128)(2,1)}), bf16[64,8,2,512]{3,2,1,0:T(2,128)(2,1)S(1)}, u32[]{:S(2)}, u32[]{:S(2)}) async-start(bf16[64,8,2,512]{3,2,1,0:T(2,128)(2,1)} %reshape.211), calls=%async_computation.1 | async-start | bytes 2097152 | tf_op jit(solution)/shard_map/all_to_all | solution.py:166
  370.4 18.4 %all-to-all-start.2 = ((bf16[64,8,2,512]{3,2,0,1:T(2,128)(2,1)}), bf16[64,8,2,512]{3,2,0,1:T(2,128)(2,1)S(1)}, u32[]{:S(2)}, u32[]{:S(2)}) async-start(bf16[64,8,2,512]{3,2,0,1:T(2,128)(2,1)} %copy.85), calls=%async_computation.2 | async-start | bytes 2097152 | tf_op jit(solution)/shard_map/all_to_all | solution.py:165
  390.3 0.9 copy-start.5
Sparse Core Ops, SparseCore 0:
  89.7 97.5 all-gather.2
  213.3 79.1 all-gather.4

commit v4 on v3

--- a/solution.py
+++ b/solution.py
@@ -131,41 +131,45 @@
     ).astype(jnp.bfloat16)
     payload = jnp.concatenate([outgoing, side], axis=-1)
     arrived = lax.all_to_all(payload, "expert", split_axis=0, concat_axis=0, tiled=True)
-    column = lax.all_gather(arrived, "dp", axis=1, tiled=True)
-    column_rows = column[:, :, :width]
-    occupied_flat = column[:, :, width].astype(jnp.float32).reshape(-1)
-    partner_total = jnp.sum(column[:, :, width + 1].astype(jnp.float32))
+    column = lax.all_gather(arrived[None], "dp", axis=0, tiled=True)
+    marks = column[:, :, :, width].astype(jnp.float32)
+    partner_total = jnp.sum(column[:, :, :, width + 1].astype(jnp.float32))
+    occupied_flat = jnp.transpose(marks, (1, 0, 2)).reshape(-1)
     before_count = jnp.cumsum(occupied_flat) - occupied_flat
-    kept_mask = occupied_flat * (
+    kept_flat = occupied_flat * (
         before_count < admission_limits[my_index].astype(jnp.float32)
     ).astype(jnp.float32)
+    kept_mask = jnp.transpose(kept_flat.reshape(experts, groups, slot_cap), (1, 0, 2))
     own_total = jnp.sum(occupied_flat)
     held_tally = jnp.where(take_other, partner_total, own_total)
     device_share = jnp.minimum(
         held_tally, admission_limits[retained_specialist].astype(jnp.float32)
     ) / (seq_rows * routed_specialist_indices.shape[1] * groups)
 
+    side_pad = ((0, 0), (0, side_cols))
+    gate_wide = jnp.pad(own_weights[0], side_pad)
+    up_wide = jnp.pad(own_weights[1], side_pad)
     gate_val = jnp.einsum(
-        "esf,hf->esh", column_rows, own_weights[0], preferred_element_type=jnp.float32
-    )
-    up_val = jnp.einsum(
-        "esf,hf->esh", column_rows, own_weights[1], preferred_element_type=jnp.float32
-    )
+        "desf,hf->desh", column, gate_wide, preferred_element_type=jnp.float32
+    )
+    up_val = jnp.einsum("desf,hf->desh", column, up_wide, preferred_element_type=jnp.float32)
     hidden = (jax.nn.silu(gate_val) * up_val).astype(jnp.bfloat16)
-    hidden_kept = hidden * kept_mask.reshape(experts, groups * slot_cap, 1).astype(jnp.bfloat16)
+    hidden_kept = hidden * kept_mask[..., None].astype(jnp.bfloat16)
+    unit_count = hidden_kept.shape[-1]
+    hidden_all = lax.all_gather(
+        hidden_kept.reshape(1, groups * experts * slot_cap, unit_count), "dp", axis=0, tiled=True
+    )
     feature_cols = own_weights[2].shape[1]
+    down_split = own_weights[2].reshape(groups, unit_count, feature_cols)
     summed = jnp.einsum(
-        "esn,nf->esf",
-        lax.all_gather(hidden_kept, "dp", axis=2, tiled=True),
-        own_weights[2],
-        preferred_element_type=jnp.float32,
+        "gsn,gnf->sf", hidden_all, down_split, preferred_element_type=jnp.float32
     )
     summed, partner = lax.optimization_barrier((summed, partner))
-    results = summed.astype(jnp.bfloat16).reshape(experts, groups, slot_cap, feature_cols)
+    results = summed.astype(jnp.bfloat16).reshape(groups, experts, slot_cap, feature_cols)
     returned = lax.all_to_all(
-        lax.all_to_all(results, "expert", split_axis=0, concat_axis=0, tiled=True),
+        lax.all_to_all(results, "expert", split_axis=1, concat_axis=1, tiled=True),
         "dp",
-        split_axis=1,
+        split_axis=0,
         concat_axis=3,
         tiled=True,
     )

time: 402 us -> 381 us (0.948)
  local copies, waits for them, and re-layouts: 26.4 us -> 13.5 us
  waiting for transfers between devices: 220 us -> 212 us
    all_gather x2, waiting for transfers between devices: 163 us -> 133 us  [the longest x1 95.1 us: per_device(): column = lax.all_gather(arrived[None], 'dp', axis=0, tiled=True)]
    ppermute x3, waiting for transfers between devices: 0.01 us -> 18.4 us  [swapped(): return lax.ppermute(value, axis, pairs)]
    slice x2 -> x0, local copies, waits for them, and re-layouts: 8.7 us -> none  [the longest x1 7.73 us: per_device(): column_rows = column[:, :, :width]]
    all_gather x1 -> x0, local copies, waits for them, and re-layouts: 5.48 us -> none  [per_device(): lax.all_gather(hidden_kept, 'dp', axis=2, tiled=True)]
    all_to_all x2, waiting for transfers between devices: 56.6 us -> 60.6 us  [the longest x1 47.9 us: per_device(): lax.all_to_all(results, 'expert', split_axis=1, concat_axis=1, tiled=True)]
  transfers between devices with their start and end apart: 7 -> 7, of which waited for: 4 -> 6; matrix products, arithmetic and copies ran while one was open for 4% -> 2% of each run, Pallas kernels for 0% -> 0%
where the time goes in v4:
time: 381 us; the launch traced here: 379 us
  waiting for transfers between devices  212 us (56%)
  blocking collectives  72.5 us (19%)
  starting transfers between devices  31.3 us (8%)
  between operations  18.8 us (5%)
  matrix products  16.8 us (4%)
  local copies, waits for them, and re-layouts  13.5 us (4%)
  other arithmetic  13.4 us (4%)
    all_gather x1, waiting for transfers between devices, per_device(): column = lax.all_gather(arrived[None], 'dp', axis=0, tiled=True)  95.1 us
    all_to_all x1, blocking collectives, per_device(): lax.all_to_all(payload, 'expert', split_axis=0, concat_axis=0, tiled=True)  72.5 us
    all_to_all x1, waiting for transfers between devices, per_device(): lax.all_to_all(results, 'expert', split_axis=1, concat_axis=1, tiled=True)  47.9 us
    all_gather x1, waiting for transfers between devices, per_device(): lax.all_gather(hidden_kept.reshape(1, groups * experts * slot_cap, unit_c...  38.3 us
    ppermute x3, waiting for transfers between devices, swapped(): return lax.ppermute(value, axis, pairs)  18.4 us
    all_to_all x1, starting transfers between devices, per_device(): lax.all_to_all(results, 'expert', split_axis=1, concat_axis=1, tiled=True)  16.6 us
    all_to_all x1, waiting for transfers between devices, per_device(): lax.all_to_all(lax.all_to_all(results, 'expert', split_axis=1, concat_axi...  12.7 us
    ppermute x3, starting transfers between devices, swapped(): return lax.ppermute(value, axis, pairs)  11.1 us
  transfers between devices with their start and end apart: 7, of which 6 were waited for; matrix products, arithmetic and copies ran while one was open for 2% of the time, Pallas kernels for 0%

profile of v4, /device:TPU:1, one launch (start us, length us, event | category | flops | bytes accessed | tf_op | source)
XLA Modules:
  0.0 378.9 jit_solution(7614219110413773662)
XLA Ops:
  7.3 0.8 convert_reduce_fusion.4
  8.1 1.0 select_reduce_fusion
  9.1 0.7 compare_select_fusion
  10.1 0.7 iota_compare_fusion.2
  10.8 0.7 bitcast_convert_fusion
  11.5 1.0 fusion.31
  12.5 1.2 fusion.45
  13.8 0.2 fusion.26
  14.0 0.3 fusion.16
  14.3 0.2 multiply_reduce_fusion
  14.7 1.2 gather_fusion
  15.9 0.7 reshape.179
  16.7 0.2 fusion.28
  16.9 1.1 pad_maximum_fusion
  17.9 72.5 %all_to_all.25 = bf16[64,2,4224]{2,1,0:T(2,128)(2,1)S(1)} all-to-all(bf16[64,2,4224]{2,1,0:T(2,128)(2,1)S(1)} %pad_maximum_fusion), channel_id=1, replica_groups=mesh['expert'=64,'dp'=8] {'expert'}, dimensions={0} | all-to-all | bytes 2162688 | tf_op jit(solution)/shard_map/all_to_all | solution.py:133
  90.5 1.2 copy.72
  91.7 0.6 dynamic_slice.10
  93.0 0.6 fusion.43
  94.2 95.1 %all-gather.6.cloned.1.call-done = bf16[512,2,4224]{2,0,1:T(8,128)(2,1)} async-done(((bf16[64,2,4224]{2,0,1:T(8,128)(2,1)}), bf16[512,2,4224]{2,0,1:T(8,128)(2,1)}) %all-gather.6.cloned.1.call-update) | async-done | bytes 8650768 | tf_op jit(solution)/shard_map/all_gather | solution.py:134
  189.4 1.9 convert_reduce_fusion
  191.6 0.3 reduce-window.9
  191.9 0.2 reshape.181
  192.2 5.8 %fusion.2 = f32[8,64,2,96]{3,1,2,0:T(8,128)S(1)} fusion(bf16[8,64,2,4224]{3,1,0,2:T(8,128)(2,1)} %bitcast.100, bf16[96,4096]{1,0:T(8,128)(2,1)S(1)} %bitcast.92), kind=kOutput, calls=%fused_computation.4 | convolution fusion | flops 830472192 | bytes 9830400 | tf_op jit(solution)/shard_map/desf,hf->desh/dot_general | solution.py:152
  198.5 6.1 %fusion.10 = bf16[8,64,2,96]{3,1,2,0:T(8,128)(2,1)S(1)} fusion(bf16[8,64,2,4224]{3,1,0,2:T(8,128)(2,1)} %bitcast.101, bf16[96,4096]{1,0:T(8,128)(2,1)} %bitcast.12, f32[8,64,2,96]{3,1,2,0:T(8,128)S(1)} %fusion.2, bf16[8,64,2]{1,2,0:T(2,128)(2,1)S(1)} %copy.77), kind=kOutput, calls=%fused_computation.9 | convolution fusion | flops 831160320 | bytes 10029056 | tf_op jit(solution)/shard_map/desf,hf->desh/dot_general | solution.py:155
  204.6 0.3 copy.78
  204.9 0.8 copy.79
  205.7 4.3 %collective-permute-start = (bf16[96,4096]{1,0:T(8,128)(2,1)S(1)}, bf16[96,4096]{1,0:T(8,128)(2,1)}, u32[]{:S(2)}, u32[]{:S(2)}) collective-permute-start(bf16[96,4096]{1,0:T(8,128)(2,1)S(1)} %bitcast.93), channel_id=1, source_target_pairs={{0,256},{8,264},{16,272},{24,280},{32,288},{40,296},{48,304},{56,3... | collective-permute-start | bytes 2359304 | tf_op jit(solution)/shard_map/ppermute | solution.py:14
  210.1 2.5 collective-permute-start.1
  212.6 4.3 %collective-permute-start.2 = (bf16[768,512]{1,0:T(8,128)(2,1)S(1)}, bf16[768,512]{1,0:T(8,128)(2,1)}, u32[]{:S(2)}, u32[]{:S(2)}) collective-permute-start(bf16[768,512]{1,0:T(8,128)(2,1)S(1)} %bitcast.90), channel_id=1, source_target_pairs={{0,256},{8,264},{16,272},{24,280},{32,288},{40,296},{48,304},{56,3... | collective-permute-start | bytes 2359304 | tf_op jit(solution)/shard_map/ppermute | solution.py:14
  216.9 38.3 %all-gather.4.cloned.1.call-done = bf16[8,1024,96]{1,2,0:T(8,128)(2,1)} async-done(((bf16[1,1024,96]{1,2,0:T(8,128)(2,1)}), bf16[8,1024,96]{1,2,0:T(8,128)(2,1)}) %all-gather.4.cloned.1.call-update) | async-done | bytes 1572880 | tf_op jit(solution)/shard_map/all_gather | solution.py:159
  255.2 2.4 convolution_bitcast_fusion
  257.6 1.6 collective-permute-done.1
  259.2 16.9 %collective-permute-done.2 = bf16[768,512]{1,0:T(8,128)(2,1)} collective-permute-done((bf16[768,512]{1,0:T(8,128)(2,1)S(1)}, bf16[768,512]{1,0:T(8,128)(2,1)}, u32[]{:S(2)}, u32[]{:S(2)}) %collective-permute-start.2) | collective-permute-done | bytes 786464 | tf_op jit(solution)/shard_map/ppermute | solution.py:14
  276.1 0.4 reshape.185
  276.5 2.2 copy.80
  278.6 16.6 %all-to-all-start.1 = ((bf16[8,64,2,512]{3,2,0,1:T(2,128)(2,1)}), bf16[8,64,2,512]{3,2,0,1:T(2,128)(2,1)S(1)}, u32[]{:S(2)}, u32[]{:S(2)}) async-start(bf16[8,64,2,512]{3,2,0,1:T(2,128)(2,1)} %copy.80), calls=%async_computation.1 | async-start | bytes 2097152 | tf_op jit(solution)/shard_map/all_to_all | solution.py:170
  297.3 1.0 select_bitcast_fusion
  298.3 1.0 select_bitcast_fusion.2
  299.2 47.9 %all-to-all-done.1 = bf16[8,64,2,512]{3,2,0,1:T(2,128)(2,1)S(1)} async-done(((bf16[8,64,2,512]{3,2,0,1:T(2,128)(2,1)}), bf16[8,64,2,512]{3,2,0,1:T(2,128)(2,1)S(1)}, u32[]{:S(2)}, u32[]{:S(2)}) %all-to-all-start.1) | async-done | bytes 1048608 | tf_op jit(solution)/shard_map/all_to_all | solution.py:170
  347.1 1.8 copy.81
  348.9 3.6 all-to-all-start.2
  352.5 2.1 select_bitcast_fusion.1
  354.6 12.7 %all-to-all-done.2 = bf16[8,64,2,512]{3,2,1,0:T(2,128)(2,1)S(1)} async-done(((bf16[8,64,2,512]{3,2,1,0:T(2,128)(2,1)}), bf16[8,64,2,512]{3,2,1,0:T(2,128)(2,1)S(1)}, u32[]{:S(2)}, u32[]{:S(2)}) %all-to-all-start.2) | async-done | bytes 1048608 | tf_op jit(solution)/shard_map/all_to_all | solution.py:169
  367.3 1.1 copy.82
  368.4 0.4 copy.90
  368.8 0.9 gather_fusion.1
  369.7 0.4 fusion.17
  370.2 0.7 add_convert_fusion
  (53 shorter events, 1.7 us)
Async XLA Ops:
  7.2 6.9 %copy-start = (bf16[8,16,512]{2,1,0:T(8,128)(2,1)S(1)}, bf16[8,16,512]{2,1,0:T(8,128)(2,1)}, u32[]{:S(2)}) copy-start(bf16[8,16,512]{2,1,0:T(8,128)(2,1)} %param.18) | copy-start | bytes 393220
  7.2 7.1 %copy-start.4 = (bf16[8,4096]{1,0:T(8,128)(2,1)S(1)}, bf16[8,4096]{1,0:T(8,128)(2,1)}, u32[]{:S(2)}) copy-start(bf16[8,4096]{1,0:T(8,128)(2,1)} %param.15) | copy-start | bytes 196612
  7.2 7.4 %copy-start.5 = (f32[4096]{0:T(1024)S(1)}, f32[4096]{0:T(1024)}, u32[]{:S(2)}) copy-start(f32[4096]{0:T(1024)} %param.22) | copy-start | bytes 49156
  7.2 182.2 %all-gather.6.cloned.1.call-start = ((), (), s32[]{:S(2)}) async-start(), calls=%async_computation.4 | async-start | bytes 9732096 | tf_op jit(solution)/shard_map/all_gather | solution.py:134
  90.5 1.3 copy-start.8
  90.5 2.5 copy-start.7
  90.5 101.8 %copy-start.2 = (bf16[1,96,4096]{2,1,0:T(8,128)(2,1)S(1)}, bf16[1,96,4096]{2,1,0:T(8,128)(2,1)}, u32[]{:S(2)}) copy-start(bf16[1,96,4096]{2,1,0:T(8,128)(2,1)} %param.27) | copy-start | bytes 2359300
  91.7 163.6 %all-gather.4.cloned.1.call-start = ((), (), s32[]{:S(2)}) async-start(), calls=%async_computation.3 | async-start | bytes 1769472 | tf_op jit(solution)/shard_map/all_gather | solution.py:159
  198.5 14.0 %copy-start.1 = (bf16[1,768,512]{2,1,0:T(8,128)(2,1)S(1)}, bf16[1,768,512]{2,1,0:T(8,128)(2,1)}, u32[]{:S(2)}) copy-start(bf16[1,768,512]{2,1,0:T(8,128)(2,1)} %param.29) | copy-start | bytes 2359300
  205.7 51.9 %collective-permute-start = (bf16[96,4096]{1,0:T(8,128)(2,1)S(1)}, bf16[96,4096]{1,0:T(8,128)(2,1)}, u32[]{:S(2)}, u32[]{:S(2)}) collective-permute-start(bf16[96,4096]{1,0:T(8,128)(2,1)S(1)} %bitcast.93), channel_id=1, source_target_pairs={{0,256},{8,264},{16,272},{24,280},{32,288},{40,296},{48,304},{56,3... | collective-permute-start | bytes 2359304 | tf_op jit(solution)/shard_map/ppermute | solution.py:14
  210.1 49.1 %collective-permute-start.1 = (bf16[96,4096]{1,0:T(8,128)(2,1)}, bf16[96,4096]{1,0:T(8,128)(2,1)}, u32[]{:S(2)}, u32[]{:S(2)}) collective-permute-start(bf16[96,4096]{1,0:T(8,128)(2,1)} %bitcast.12), channel_id=1, source_target_pairs={{0,256},{8,264},{16,272},{24,280},{32,288},{40,296},{48,304},{56,3... | collective-permute-start | bytes 2359304 | tf_op jit(solution)/shard_map/ppermute | solution.py:14
  212.6 63.5 %collective-permute-start.2 = (bf16[768,512]{1,0:T(8,128)(2,1)S(1)}, bf16[768,512]{1,0:T(8,128)(2,1)}, u32[]{:S(2)}, u32[]{:S(2)}) collective-permute-start(bf16[768,512]{1,0:T(8,128)(2,1)S(1)} %bitcast.90), channel_id=1, source_target_pairs={{0,256},{8,264},{16,272},{24,280},{32,288},{40,296},{48,304},{56,3... | collective-permute-start | bytes 2359304 | tf_op jit(solution)/shard_map/ppermute | solution.py:14
  278.6 19.6 %copy-start.3 = (bf16[1,96,4096]{2,1,0:T(8,128)(2,1)S(1)}, bf16[1,96,4096]{2,1,0:T(8,128)(2,1)}, u32[]{:S(2)}) copy-start(bf16[1,96,4096]{2,1,0:T(8,128)(2,1)} %param.27) | copy-start | bytes 2359300
  278.6 68.5 %all-to-all-start.1 = ((bf16[8,64,2,512]{3,2,0,1:T(2,128)(2,1)}), bf16[8,64,2,512]{3,2,0,1:T(2,128)(2,1)S(1)}, u32[]{:S(2)}, u32[]{:S(2)}) async-start(bf16[8,64,2,512]{3,2,0,1:T(2,128)(2,1)} %copy.80), calls=%async_computation.1 | async-start | bytes 2097152 | tf_op jit(solution)/shard_map/all_to_all | solution.py:170
  348.9 18.4 %all-to-all-start.2 = ((bf16[8,64,2,512]{3,2,1,0:T(2,128)(2,1)}), bf16[8,64,2,512]{3,2,1,0:T(2,128)(2,1)S(1)}, u32[]{:S(2)}, u32[]{:S(2)}) async-start(bf16[8,64,2,512]{3,2,1,0:T(2,128)(2,1)} %copy.81), calls=%async_computation.2 | async-start | bytes 2097152 | tf_op jit(solution)/shard_map/all_to_all | solution.py:169
  368.8 0.9 copy-start.6
Sparse Core Ops, SparseCore 0:
  91.8 97.5 all-gather.5
  205.9 49.2 all-gather.3

commit v5 on v4

--- a/solution.py
+++ b/solution.py
@@ -130,10 +130,20 @@
         ),
     ).astype(jnp.bfloat16)
     payload = jnp.concatenate([outgoing, side], axis=-1)
-    arrived = lax.all_to_all(payload, "expert", split_axis=0, concat_axis=0, tiled=True)
-    column = lax.all_gather(arrived[None], "dp", axis=0, tiled=True)
-    marks = column[:, :, :, width].astype(jnp.float32)
-    partner_total = jnp.sum(column[:, :, :, width + 1].astype(jnp.float32))
+    side_pad = ((0, 0), (0, side_cols))
+    gate_wide = jnp.pad(own_weights[0], side_pad)
+    up_wide = jnp.pad(own_weights[1], side_pad)
+    feature_cols = own_weights[2].shape[1]
+    unit_count = own_weights[0].shape[0]
+    down_split = own_weights[2].reshape(groups, unit_count, feature_cols)
+    columns = []
+    for chunk in range(slot_cap):
+        arrived = lax.all_to_all(
+            payload[:, chunk], "expert", split_axis=0, concat_axis=0, tiled=True
+        )
+        columns.append(lax.all_gather(arrived[None], "dp", axis=0, tiled=True))
+    marks = jnp.stack([c[:, :, width] for c in columns], axis=-1).astype(jnp.float32)
+    partner_total = sum(jnp.sum(c[:, :, width + 1].astype(jnp.float32)) for c in columns)
     occupied_flat = jnp.transpose(marks, (1, 0, 2)).reshape(-1)
     before_count = jnp.cumsum(occupied_flat) - occupied_flat
     kept_flat = occupied_flat * (
@@ -146,33 +156,34 @@
         held_tally, admission_limits[retained_specialist].astype(jnp.float32)
     ) / (seq_rows * routed_specialist_indices.shape[1] * groups)
 
-    side_pad = ((0, 0), (0, side_cols))
-    gate_wide = jnp.pad(own_weights[0], side_pad)
-    up_wide = jnp.pad(own_weights[1], side_pad)
-    gate_val = jnp.einsum(
-        "desf,hf->desh", column, gate_wide, preferred_element_type=jnp.float32
-    )
-    up_val = jnp.einsum("desf,hf->desh", column, up_wide, preferred_element_type=jnp.float32)
-    hidden = (jax.nn.silu(gate_val) * up_val).astype(jnp.bfloat16)
-    hidden_kept = hidden * kept_mask[..., None].astype(jnp.bfloat16)
-    unit_count = hidden_kept.shape[-1]
-    hidden_all = lax.all_gather(
-        hidden_kept.reshape(1, groups * experts * slot_cap, unit_count), "dp", axis=0, tiled=True
-    )
-    feature_cols = own_weights[2].shape[1]
-    down_split = own_weights[2].reshape(groups, unit_count, feature_cols)
-    summed = jnp.einsum(
-        "gsn,gnf->sf", hidden_all, down_split, preferred_element_type=jnp.float32
-    )
-    summed, partner = lax.optimization_barrier((summed, partner))
-    results = summed.astype(jnp.bfloat16).reshape(groups, experts, slot_cap, feature_cols)
-    returned = lax.all_to_all(
-        lax.all_to_all(results, "expert", split_axis=1, concat_axis=1, tiled=True),
-        "dp",
-        split_axis=0,
-        concat_axis=3,
-        tiled=True,
-    )
+    returned_parts = []
+    for chunk in range(slot_cap):
+        column = columns[chunk]
+        gate_val = jnp.einsum(
+            "def,hf->deh", column, gate_wide, preferred_element_type=jnp.float32
+        )
+        up_val = jnp.einsum("def,hf->deh", column, up_wide, preferred_element_type=jnp.float32)
+        hidden = (jax.nn.silu(gate_val) * up_val).astype(jnp.bfloat16)
+        hidden_all = lax.all_gather(
+            hidden.reshape(1, groups * experts, unit_count), "dp", axis=0, tiled=True
+        )
+        summed = jnp.einsum(
+            "gsn,gnf->sf", hidden_all, down_split, preferred_element_type=jnp.float32
+        )
+        if chunk == slot_cap - 1:
+            summed, partner = lax.optimization_barrier((summed, partner))
+        results = summed.astype(jnp.bfloat16).reshape(groups, experts, feature_cols)
+        results = results * kept_mask[:, :, chunk, None].astype(jnp.bfloat16)
+        returned_parts.append(
+            lax.all_to_all(
+                lax.all_to_all(results, "expert", split_axis=1, concat_axis=1, tiled=True),
+                "dp",
+                split_axis=0,
+                concat_axis=2,
+                tiled=True,
+            )
+        )
+    returned = jnp.stack([r[0] for r in returned_parts], axis=1)
     returned_flat = returned.reshape(experts * slot_cap, width)
     picked = returned_flat[slot_code]
     expert_mix = jnp.sum(routing_probabilities[:, :, None] * picked.astype(jnp.float32), axis=1)

time: 381 us -> 416 us (1.092)
  waiting for transfers between devices: 212 us -> 130 us
  blocking collectives: 72.5 us -> 144 us
  starting transfers between devices: 31.3 us -> 56.6 us
  other arithmetic: 13.4 us -> 27.4 us
    all_gather x0 -> x2, blocking collectives: none -> 49.7 us  [per_device(): lax.all_gather(hidden.reshape(1, groups * experts, unit_count), 'dp', axi...]
    all_gather x2, waiting for transfers between devices: 133 us -> 92.3 us  [per_device(): columns.append(lax.all_gather(arrived[None], 'dp', axis=0, tiled=True))]
    all_to_all x1 -> x2, starting transfers between devices: 16.6 us -> 40.7 us  [per_device(): lax.all_to_all(results, 'expert', split_axis=1, concat_axis=1, tiled=True)]
    all_to_all x1 -> x2, blocking collectives: 72.5 us -> 94 us  [per_device(): lax.all_to_all(payload[:, chunk], 'expert', split_axis=0, concat_axis=0,...]
    ppermute x3, waiting for transfers between devices: 18.4 us -> 0.01 us  [swapped(): return lax.ppermute(value, axis, pairs)]
    all_to_all x1 -> x2, waiting for transfers between devices: 47.9 us -> 30.5 us  [per_device(): lax.all_to_all(results, 'expert', split_axis=1, concat_axis=1, tiled=True)]
    concatenate x1 -> x3, other arithmetic: 1.06 us -> 11.5 us  [per_device(): payload = jnp.concatenate([outgoing, side], axis=-1)]
    all_to_all x1 -> x2, waiting for transfers between devices: 12.7 us -> 7.56 us  [per_device(): lax.all_to_all(lax.all_to_all(results, 'expert', split_axis=1, concat_axi...]
  transfers between devices with their start and end apart: 7 -> 9, of which waited for: 6 -> 5; matrix products, arithmetic and copies ran while one was open for 2% -> 9% of each run, Pallas kernels for 0% -> 0%
where the time goes in v5:
time: 416 us; the launch traced here: 414 us
  blocking collectives  144 us (35%)
  waiting for transfers between devices  130 us (31%)
  starting transfers between devices  56.6 us (14%)
  other arithmetic  27.4 us (7%)
  between operations  19.6 us (5%)
  matrix products  18.8 us (5%)
  local copies, waits for them, and re-layouts  17 us (4%)
    all_to_all x2, blocking collectives, per_device(): lax.all_to_all(payload[:, chunk], 'expert', split_axis=0, concat_axis=0,...  94 us
    all_gather x2, waiting for transfers between devices, per_device(): columns.append(lax.all_gather(arrived[None], 'dp', axis=0, tiled=True))  92.3 us
    all_gather x2, blocking collectives, per_device(): lax.all_gather(hidden.reshape(1, groups * experts, unit_count), 'dp', axi...  49.7 us
    all_to_all x2, starting transfers between devices, per_device(): lax.all_to_all(results, 'expert', split_axis=1, concat_axis=1, tiled=True)  40.7 us
    all_to_all x2, waiting for transfers between devices, per_device(): lax.all_to_all(results, 'expert', split_axis=1, concat_axis=1, tiled=True)  30.5 us
    concatenate x3, other arithmetic, per_device(): payload = jnp.concatenate([outgoing, side], axis=-1)  11.5 us
    ppermute x3, starting transfers between devices, swapped(): return lax.ppermute(value, axis, pairs)  8.71 us
  transfers between devices with their start and end apart: 9, of which 5 were waited for; matrix products, arithmetic and copies ran while one was open for 9% of the time, Pallas kernels for 0%

profile of v5, /device:TPU:1, one launch (start us, length us, event | category | flops | bytes accessed | tf_op | source)
XLA Modules:
  0.0 413.6 jit_solution(17000905522647212603)
XLA Ops:
  7.2 0.7 iota_compare_fusion.2
  8.0 0.8 convert_reduce_fusion.4
  8.8 1.0 select_reduce_fusion
  11.6 1.0 fusion.32
  12.6 1.2 fusion.48
  14.7 1.2 gather_fusion
  15.9 0.7 reshape.192
  16.9 3.7 slice_maximum_fusion
  21.1 3.9 reduce.9
  25.4 53.7 %all_to_all.52 = bf16[64,2,2112]{2,1,0:T(2,128)(2,1)S(1)} all-to-all(bf16[64,2,2112]{2,1,0:T(2,128)(2,1)S(1)} %reshape.236), channel_id=1, replica_groups=mesh['expert'=64,'dp'=8] {'expert'}, dimensions={0} | all-to-all | bytes 1081344 | tf_op jit(solution)/shard_map/all_to_all | solution.py:141
  79.8 0.9 copy.99
  80.9 3.9 reduce.8
  85.2 40.2 %all_to_all.53 = bf16[64,2,2112]{2,1,0:T(2,128)(2,1)S(1)} all-to-all(bf16[64,2,2112]{2,1,0:T(2,128)(2,1)S(1)} %reshape.234), channel_id=1, replica_groups=mesh['expert'=64,'dp'=8] {'expert'}, dimensions={0} | all-to-all | bytes 1081344 | tf_op jit(solution)/shard_map/all_to_all | solution.py:141
  126.1 0.9 copy.101
  127.0 1.9 collective-permute-start.2
  128.9 4.9 %collective-permute-start = (bf16[96,4096]{1,0:T(8,128)(2,1)S(1)}, bf16[96,4096]{1,0:T(8,128)(2,1)}, u32[]{:S(2)}, u32[]{:S(2)}) collective-permute-start(bf16[96,4096]{1,0:T(8,128)(2,1)S(1)} %bitcast.110), channel_id=1, source_target_pairs={{0,256},{8,264},{16,272},{24,280},{32,288},{40,296},{48,304},{56,3... | collective-permute-start | bytes 2359304 | tf_op jit(solution)/shard_map/ppermute | solution.py:14
  133.8 1.9 collective-permute-start.1
  138.2 8.2 %all-gather.5.cloned.1.call-done = bf16[512,1,4224]{2,0,1:T(8,128)(2,1)} async-done(((bf16[64,1,4224]{2,0,1:T(8,128)(2,1)}), bf16[512,1,4224]{2,0,1:T(8,128)(2,1)}) %all-gather.5.cloned.1.call-update) | async-done | bytes 4325392 | tf_op jit(solution)/shard_map/all_gather | solution.py:144
  146.4 0.9 slice.59
  147.3 84.1 %all-gather.7.cloned.1.call-done = bf16[512,1,4224]{2,0,1:T(8,128)(2,1)} async-done(((bf16[64,1,4224]{2,0,1:T(8,128)(2,1)}), bf16[512,1,4224]{2,0,1:T(8,128)(2,1)}) %all-gather.7.cloned.1.call-update) | async-done | bytes 4325392 | tf_op jit(solution)/shard_map/all_gather | solution.py:144
  231.4 0.9 slice.60
  233.4 3.5 fusion.10
  237.9 3.5 fusion.2
  241.6 24.5 %all_gather.15 = bf16[8,512,96]{1,2,0:T(8,128)(2,1)S(1)} all-gather(bf16[1,512,96]{1,2,0:T(8,128)(2,1)S(1)} %copy.108), channel_id=1, replica_groups=mesh['expert'=64,'dp'=8] {'dp'}, dimensions={0}, use_global_device_ids=true | all-gather | bytes 884736 | tf_op jit(solution)/shard_map/all_gather | solution.py:167
  266.7 1.1 copy_multiply_fusion
  267.8 20.6 %all-to-all-start.4 = ((bf16[8,64,512]{2,0,1:T(8,128)(2,1)}), bf16[8,64,512]{2,0,1:T(8,128)(2,1)S(1)}, u32[]{:S(2)}, u32[]{:S(2)}) async-start(bf16[8,64,512]{2,0,1:T(8,128)(2,1)} %copy_multiply_fusion), calls=%async_computation.4 | async-start | bytes 1048576 | tf_op jit(solution)/shard_map/all_to_all | solution.py:179
  288.4 3.5 fusion.12
  291.9 3.5 fusion.1
  296.0 25.2 %all_gather.13 = bf16[8,512,96]{1,2,0:T(8,128)(2,1)S(1)} all-gather(bf16[1,512,96]{1,2,0:T(8,128)(2,1)S(1)} %copy.100), channel_id=1, replica_groups=mesh['expert'=64,'dp'=8] {'dp'}, dimensions={0}, use_global_device_ids=true | all-gather | bytes 884736 | tf_op jit(solution)/shard_map/all_gather | solution.py:167
  321.2 1.7 fusion
  322.9 1.1 copy_multiply_fusion.1
  324.0 20.1 %all-to-all-start.2 = ((bf16[8,64,512]{2,0,1:T(8,128)(2,1)}), bf16[8,64,512]{2,0,1:T(8,128)(2,1)S(1)}, u32[]{:S(2)}, u32[]{:S(2)}) async-start(bf16[8,64,512]{2,0,1:T(8,128)(2,1)} %copy_multiply_fusion.1), calls=%async_computation.2 | async-start | bytes 1048576 | tf_op jit(solution)/shard_map/all_to_all | solution.py:179
  344.9 1.0 select_bitcast_fusion.2
  345.9 0.9 copy.111
  346.8 30.5 %all-to-all-done.2 = bf16[8,64,512]{2,0,1:T(8,128)(2,1)S(1)} async-done(((bf16[8,64,512]{2,0,1:T(8,128)(2,1)}), bf16[8,64,512]{2,0,1:T(8,128)(2,1)S(1)}, u32[]{:S(2)}, u32[]{:S(2)}) %all-to-all-start.2) | async-done | bytes 524320 | tf_op jit(solution)/shard_map/all_to_all | solution.py:179
  377.4 3.5 all-to-all-start.5
  380.9 1.0 select_bitcast_fusion.1
  381.8 0.9 copy.106
  382.8 6.8 %all-to-all-done.5 = bf16[8,64,512]{2,1,0:T(8,128)(2,1)S(1)} async-done(((bf16[8,64,512]{2,1,0:T(8,128)(2,1)}), bf16[8,64,512]{2,1,0:T(8,128)(2,1)S(1)}, u32[]{:S(2)}, u32[]{:S(2)}) %all-to-all-start.5) | async-done | bytes 524320 | tf_op jit(solution)/shard_map/all_to_all | solution.py:178
  389.6 3.5 all-to-all-start.3
  393.1 1.6 convert_reduce_fusion.2
  394.8 1.6 convert_reduce_fusion.1
  397.7 0.7 convert_reduce_fusion
  399.1 1.0 select_bitcast_fusion
  400.6 0.7 all-to-all-done.3
  402.0 1.1 copy.113
  403.6 0.9 gather_fusion.1
  404.9 0.7 add_convert_fusion
  (85 shorter events, 12.4 us)
Async XLA Ops:
  7.2 6.9 %copy-start = (bf16[8,16,512]{2,1,0:T(8,128)(2,1)S(1)}, bf16[8,16,512]{2,1,0:T(8,128)(2,1)}, u32[]{:S(2)}) copy-start(bf16[8,16,512]{2,1,0:T(8,128)(2,1)} %param.18) | copy-start | bytes 393220
  7.2 139.2 %all-gather.5.cloned.1.call-start = ((), (), s32[]{:S(2)}) async-start(), calls=%async_computation.6 | async-start | bytes 4866048 | tf_op jit(solution)/shard_map/all_gather | solution.py:144
  12.6 1.8 copy-start.5
  13.8 0.8 copy-start.6
  80.7 150.8 %all-gather.7.cloned.1.call-start = ((), (), s32[]{:S(2)}) async-start(), calls=%async_computation.7 | async-start | bytes 4866048 | tf_op jit(solution)/shard_map/all_gather | solution.py:144
  126.0 2.9 copy-start.1
  126.0 7.7 %copy-start.2 = (bf16[1,96,4096]{2,1,0:T(8,128)(2,1)S(1)}, bf16[1,96,4096]{2,1,0:T(8,128)(2,1)}, u32[]{:S(2)}) copy-start(bf16[1,96,4096]{2,1,0:T(8,128)(2,1)} %param.28) | copy-start | bytes 2359300
  126.0 9.7 %copy-start.9 = (s32[64]{0:T(128)S(1)}, s32[64]{0:T(128)}, u32[]{:S(2)}) copy-start(s32[64]{0:T(128)} %param.26) | copy-start | bytes 772
  126.1 10.9 %copy-start.8 = (s32[64]{0:T(128)S(1)}, s32[64]{0:T(128)}, u32[]{:S(2)}) copy-start(s32[64]{0:T(128)} %param.25) | copy-start | bytes 772
  127.0 139.7 %collective-permute-start.2 = (bf16[768,512]{1,0:T(8,128)(2,1)}, bf16[768,512]{1,0:T(8,128)(2,1)}, u32[]{:S(2)}, u32[]{:S(2)}) collective-permute-start(bf16[768,512]{1,0:T(8,128)(2,1)} %bitcast.116), channel_id=1, source_target_pairs={{0,256},{8,264},{16,272},{24,280},{32,288},{40,296},{48,304},{56,3... | collective-permute-start | bytes 2359304 | tf_op jit(solution)/shard_map/ppermute | solution.py:14
  128.9 137.8 %collective-permute-start = (bf16[96,4096]{1,0:T(8,128)(2,1)S(1)}, bf16[96,4096]{1,0:T(8,128)(2,1)}, u32[]{:S(2)}, u32[]{:S(2)}) collective-permute-start(bf16[96,4096]{1,0:T(8,128)(2,1)S(1)} %bitcast.110), channel_id=1, source_target_pairs={{0,256},{8,264},{16,272},{24,280},{32,288},{40,296},{48,304},{56,3... | collective-permute-start | bytes 2359304 | tf_op jit(solution)/shard_map/ppermute | solution.py:14
  133.8 132.9 %collective-permute-start.1 = (bf16[96,4096]{1,0:T(8,128)(2,1)S(1)}, bf16[96,4096]{1,0:T(8,128)(2,1)}, u32[]{:S(2)}, u32[]{:S(2)}) collective-permute-start(bf16[96,4096]{1,0:T(8,128)(2,1)S(1)} %bitcast.113), channel_id=1, source_target_pairs={{0,256},{8,264},{16,272},{24,280},{32,288},{40,296},{48,304},{56,3... | collective-permute-start | bytes 2359304 | tf_op jit(solution)/shard_map/ppermute | solution.py:14
  241.4 24.7 %copy-start.3 = (bf16[1,768,512]{2,1,0:T(8,128)(2,1)S(1)}, bf16[1,768,512]{2,1,0:T(8,128)(2,1)}, u32[]{:S(2)}) copy-start(bf16[1,768,512]{2,1,0:T(8,128)(2,1)} %param.29) | copy-start | bytes 2359300
  267.8 56.2 %all-to-all-start.4 = ((bf16[8,64,512]{2,0,1:T(8,128)(2,1)}), bf16[8,64,512]{2,0,1:T(8,128)(2,1)S(1)}, u32[]{:S(2)}, u32[]{:S(2)}) async-start(bf16[8,64,512]{2,0,1:T(8,128)(2,1)} %copy_multiply_fusion), calls=%async_computation.4 | async-start | bytes 1048576 | tf_op jit(solution)/shard_map/all_to_all | solution.py:179
  324.0 53.3 %all-to-all-start.2 = ((bf16[8,64,512]{2,0,1:T(8,128)(2,1)}), bf16[8,64,512]{2,0,1:T(8,128)(2,1)S(1)}, u32[]{:S(2)}, u32[]{:S(2)}) async-start(bf16[8,64,512]{2,0,1:T(8,128)(2,1)} %copy_multiply_fusion.1), calls=%async_computation.2 | async-start | bytes 1048576 | tf_op jit(solution)/shard_map/all_to_all | solution.py:179
  377.4 12.3 %all-to-all-start.5 = ((bf16[8,64,512]{2,1,0:T(8,128)(2,1)}), bf16[8,64,512]{2,1,0:T(8,128)(2,1)S(1)}, u32[]{:S(2)}, u32[]{:S(2)}) async-start(bf16[8,64,512]{2,1,0:T(8,128)(2,1)} %copy.111), calls=%async_computation.5 | async-start | bytes 1048576 | tf_op jit(solution)/shard_map/all_to_all | solution.py:178
  381.8 17.3 %copy-start.4 = (bf16[1,768,512]{2,1,0:T(8,128)(2,1)S(1)}, bf16[1,768,512]{2,1,0:T(8,128)(2,1)}, u32[]{:S(2)}) copy-start(bf16[1,768,512]{2,1,0:T(8,128)(2,1)} %param.29) | copy-start | bytes 2359300
  389.6 11.8 %all-to-all-start.3 = ((bf16[8,64,512]{2,1,0:T(8,128)(2,1)}), bf16[8,64,512]{2,1,0:T(8,128)(2,1)S(1)}, u32[]{:S(2)}, u32[]{:S(2)}) async-start(bf16[8,64,512]{2,1,0:T(8,128)(2,1)} %copy.106), calls=%async_computation.3 | async-start | bytes 1048576 | tf_op jit(solution)/shard_map/all_to_all | solution.py:178
  403.6 0.9 copy-start.7
Sparse Core Ops, SparseCore 0:
  80.8 65.5 all-gather.4
  149.1 82.3 all-gather.6

commit v6 on v4

--- a/solution.py
+++ b/solution.py
@@ -164,7 +164,6 @@
     summed = jnp.einsum(
         "gsn,gnf->sf", hidden_all, down_split, preferred_element_type=jnp.float32
     )
-    summed, partner = lax.optimization_barrier((summed, partner))
     results = summed.astype(jnp.bfloat16).reshape(groups, experts, slot_cap, feature_cols)
     returned = lax.all_to_all(
         lax.all_to_all(results, "expert", split_axis=1, concat_axis=1, tiled=True),

time: 381 us -> 365 us (0.958)
  waiting for transfers between devices: 212 us -> 193 us
  starting transfers between devices: 31.3 us -> 37.2 us
    all_to_all x1, waiting for transfers between devices: 47.9 us -> 1.46 us  [per_device(): lax.all_to_all(results, 'expert', split_axis=1, concat_axis=1, tiled=True)]
    ppermute x3, waiting for transfers between devices: 18.4 us -> 45.2 us  [swapped(): return lax.ppermute(value, axis, pairs)]
    all_to_all x1, starting transfers between devices: 16.6 us -> 21.7 us  [per_device(): lax.all_to_all(results, 'expert', split_axis=1, concat_axis=1, tiled=True)]
  transfers between devices with their start and end apart: 7 -> 7, of which waited for: 6 -> 7; matrix products, arithmetic and copies ran while one was open for 2% -> 2% of each run, Pallas kernels for 0% -> 0%
where the time goes in v6:
time: 365 us
  waiting for transfers between devices  193 us (53%)
  blocking collectives  72.5 us (20%)
  starting transfers between devices  37.2 us (10%)
  between operations  18.8 us (5%)
  matrix products  17.6 us (5%)
  local copies, waits for them, and re-layouts  13.5 us (4%)
  other arithmetic  12.3 us (3%)
    all_gather x1, waiting for transfers between devices, per_device(): column = lax.all_gather(arrived[None], 'dp', axis=0, tiled=True)  95.1 us
    all_to_all x1, blocking collectives, per_device(): lax.all_to_all(payload, 'expert', split_axis=0, concat_axis=0, tiled=True)  72.5 us
    ppermute x3, waiting for transfers between devices, swapped(): return lax.ppermute(value, axis, pairs)  45.2 us
    all_gather x1, waiting for transfers between devices, per_device(): lax.all_gather(hidden_kept.reshape(1, groups * experts * slot_cap, unit_c...  41.1 us
    all_to_all x1, starting transfers between devices, per_device(): lax.all_to_all(results, 'expert', split_axis=1, concat_axis=1, tiled=True)  21.7 us
    ppermute x3, starting transfers between devices, swapped(): return lax.ppermute(value, axis, pairs)  11.9 us
    all_to_all x1, waiting for transfers between devices, per_device(): lax.all_to_all(lax.all_to_all(results, 'expert', split_axis=1, concat_axi...  9.84 us
  transfers between devices with their start and end apart: 7, of which 7 were waited for; matrix products, arithmetic and copies ran while one was open for 2% of the time, Pallas kernels for 0%

profile of v6, /device:TPU:1, one launch (start us, length us, event | category | flops | bytes accessed | tf_op | source)
XLA Modules:
  0.0 364.7 jit_solution(13863365616823546631)
XLA Ops:
  7.3 0.8 convert_reduce_fusion.4
  8.1 1.0 select_reduce_fusion
  9.1 0.7 compare_select_fusion
  10.1 0.7 iota_compare_fusion.2
  10.8 0.7 bitcast_convert_fusion.1
  11.5 1.0 fusion.31
  12.5 1.2 fusion.45
  13.8 0.2 fusion.26
  14.0 0.3 fusion.16
  14.7 1.2 gather_fusion
  15.9 0.7 reshape.179
  16.7 0.2 fusion.28
  16.9 1.1 pad_maximum_fusion
  17.9 72.5 %all_to_all.25 = bf16[64,2,4224]{2,1,0:T(2,128)(2,1)S(1)} all-to-all(bf16[64,2,4224]{2,1,0:T(2,128)(2,1)S(1)} %pad_maximum_fusion), channel_id=1, replica_groups=mesh['expert'=64,'dp'=8] {'expert'}, dimensions={0} | all-to-all | bytes 2162688 | tf_op jit(solution)/shard_map/all_to_all | solution.py:133
  90.5 1.2 copy.72
  91.7 0.6 dynamic_slice.10
  93.0 0.6 fusion.43
  94.2 95.1 %all-gather.6.cloned.1.call-done = bf16[512,2,4224]{2,0,1:T(8,128)(2,1)} async-done(((bf16[64,2,4224]{2,0,1:T(8,128)(2,1)}), bf16[512,2,4224]{2,0,1:T(8,128)(2,1)}) %all-gather.6.cloned.1.call-update) | async-done | bytes 8650768 | tf_op jit(solution)/shard_map/all_gather | solution.py:134
  189.4 1.9 convert_reduce_fusion
  191.6 0.3 reduce-window.9
  191.9 0.2 reshape.181
  192.2 6.7 %fusion.2 = f32[8,64,2,96]{3,1,2,0:T(8,128)} fusion(bf16[8,64,2,4224]{3,1,0,2:T(8,128)(2,1)} %bitcast.102, bf16[96,4096]{1,0:T(8,128)(2,1)S(1)} %bitcast.92), kind=kOutput, calls=%fused_computation.4 | convolution fusion | flops 830472192 | bytes 9830400 | tf_op jit(solution)/shard_map/desf,hf->desh/dot_general | solution.py:152
  199.4 6.0 %fusion.10 = bf16[8,64,2,96]{3,1,2,0:T(8,128)(2,1)S(1)} fusion(bf16[8,64,2,4224]{3,1,0,2:T(8,128)(2,1)} %bitcast.103, bf16[96,4096]{1,0:T(8,128)(2,1)S(1)} %bitcast.95, f32[8,64,2,96]{3,1,2,0:T(8,128)} %fusion.2, bf16[8,64,2]{1,2,0:T(2,128)(2,1)S(1)} %copy.77), kind=kOutput, calls=%fused_computation.9 | convolution fusion | flops 831160320 | bytes 10029056 | tf_op jit(solution)/shard_map/desf,hf->desh/dot_general | solution.py:155
  205.4 0.3 copy.78
  205.7 0.8 copy.79
  206.5 41.1 %all-gather.4.cloned.1.call-done = bf16[8,1024,96]{1,2,0:T(8,128)(2,1)} async-done(((bf16[1,1024,96]{1,2,0:T(8,128)(2,1)}), bf16[8,1024,96]{1,2,0:T(8,128)(2,1)}) %all-gather.4.cloned.1.call-update) | async-done | bytes 1572880 | tf_op jit(solution)/shard_map/all_gather | solution.py:159
  247.6 2.4 bitcast_convert_fusion
  250.0 0.4 reshape.185
  250.5 2.2 copy.80
  252.7 21.7 %all-to-all-start.1 = ((bf16[8,64,2,512]{3,2,0,1:T(2,128)(2,1)}), bf16[8,64,2,512]{3,2,0,1:T(2,128)(2,1)S(1)}, u32[]{:S(2)}, u32[]{:S(2)}) async-start(bf16[8,64,2,512]{3,2,0,1:T(2,128)(2,1)} %copy.80), calls=%async_computation.1 | async-start | bytes 2097152 | tf_op jit(solution)/shard_map/all_to_all | solution.py:169
  274.4 5.1 %collective-permute-start.2 = (bf16[768,512]{1,0:T(8,128)(2,1)S(1)}, bf16[768,512]{1,0:T(8,128)(2,1)}, u32[]{:S(2)}, u32[]{:S(2)}) collective-permute-start(bf16[768,512]{1,0:T(8,128)(2,1)S(1)} %bitcast.91), channel_id=1, source_target_pairs={{0,256},{8,264},{16,272},{24,280},{32,288},{40,296},{48,304},{56,3... | collective-permute-start | bytes 2359304 | tf_op jit(solution)/shard_map/ppermute | solution.py:14
  279.5 1.9 collective-permute-start
  281.4 4.9 %collective-permute-start.1 = (bf16[96,4096]{1,0:T(8,128)(2,1)}, bf16[96,4096]{1,0:T(8,128)(2,1)}, u32[]{:S(2)}, u32[]{:S(2)}) collective-permute-start(bf16[96,4096]{1,0:T(8,128)(2,1)} %bitcast.94), channel_id=1, source_target_pairs={{0,256},{8,264},{16,272},{24,280},{32,288},{40,296},{48,304},{56,3... | collective-permute-start | bytes 2359304 | tf_op jit(solution)/shard_map/ppermute | solution.py:14
  287.0 13.7 %collective-permute-done.2 = bf16[768,512]{1,0:T(8,128)(2,1)} collective-permute-done((bf16[768,512]{1,0:T(8,128)(2,1)S(1)}, bf16[768,512]{1,0:T(8,128)(2,1)}, u32[]{:S(2)}, u32[]{:S(2)}) %collective-permute-start.2) | collective-permute-done | bytes 786464 | tf_op jit(solution)/shard_map/ppermute | solution.py:14
  300.7 1.0 select_bitcast_fusion
  301.6 22.2 %collective-permute-done = bf16[96,4096]{1,0:T(8,128)(2,1)} collective-permute-done((bf16[96,4096]{1,0:T(8,128)(2,1)S(1)}, bf16[96,4096]{1,0:T(8,128)(2,1)}, u32[]{:S(2)}, u32[]{:S(2)}) %collective-permute-start) | collective-permute-done | bytes 786464 | tf_op jit(solution)/shard_map/ppermute | solution.py:14
  323.8 1.0 select_bitcast_fusion.2
  324.8 1.5 all-to-all-done.1
  326.2 1.8 copy.81
  328.0 3.6 all-to-all-start.2
  331.6 9.4 %collective-permute-done.1 = bf16[96,4096]{1,0:T(8,128)(2,1)} collective-permute-done((bf16[96,4096]{1,0:T(8,128)(2,1)}, bf16[96,4096]{1,0:T(8,128)(2,1)}, u32[]{:S(2)}, u32[]{:S(2)}) %collective-permute-start.1) | collective-permute-done | bytes 786464 | tf_op jit(solution)/shard_map/ppermute | solution.py:14
  341.0 1.0 select_bitcast_fusion.1
  343.3 9.8 %all-to-all-done.2 = bf16[8,64,2,512]{3,2,1,0:T(2,128)(2,1)S(1)} async-done(((bf16[8,64,2,512]{3,2,1,0:T(2,128)(2,1)}), bf16[8,64,2,512]{3,2,1,0:T(2,128)(2,1)S(1)}, u32[]{:S(2)}, u32[]{:S(2)}) %all-to-all-start.2) | async-done | bytes 1048608 | tf_op jit(solution)/shard_map/all_to_all | solution.py:168
  353.1 1.1 copy.82
  354.2 0.4 copy.90
  354.7 0.9 gather_fusion.1
  355.5 0.4 fusion.17
  356.0 0.7 add_convert_fusion
  (57 shorter events, 1.9 us)
Async XLA Ops:
  7.2 6.9 %copy-start = (bf16[8,16,512]{2,1,0:T(8,128)(2,1)S(1)}, bf16[8,16,512]{2,1,0:T(8,128)(2,1)}, u32[]{:S(2)}) copy-start(bf16[8,16,512]{2,1,0:T(8,128)(2,1)} %param.18) | copy-start | bytes 393220
  7.2 7.1 %copy-start.6 = (bf16[8,4096]{1,0:T(8,128)(2,1)S(1)}, bf16[8,4096]{1,0:T(8,128)(2,1)}, u32[]{:S(2)}) copy-start(bf16[8,4096]{1,0:T(8,128)(2,1)} %param.15) | copy-start | bytes 196612
  7.2 7.4 %copy-start.7 = (f32[4096]{0:T(1024)S(1)}, f32[4096]{0:T(1024)}, u32[]{:S(2)}) copy-start(f32[4096]{0:T(1024)} %param.22) | copy-start | bytes 49156
  7.2 182.2 %all-gather.6.cloned.1.call-start = ((), (), s32[]{:S(2)}) async-start(), calls=%async_computation.4 | async-start | bytes 9732096 | tf_op jit(solution)/shard_map/all_gather | solution.py:134
  90.5 1.3 copy-start.10
  90.5 2.5 copy-start.9
  90.5 101.8 %copy-start.2 = (bf16[1,96,4096]{2,1,0:T(8,128)(2,1)S(1)}, bf16[1,96,4096]{2,1,0:T(8,128)(2,1)}, u32[]{:S(2)}) copy-start(bf16[1,96,4096]{2,1,0:T(8,128)(2,1)} %param.27) | copy-start | bytes 2359300
  91.7 156.0 %all-gather.4.cloned.1.call-start = ((), (), s32[]{:S(2)}) async-start(), calls=%async_computation.3 | async-start | bytes 1769472 | tf_op jit(solution)/shard_map/all_gather | solution.py:159
  192.2 7.2 %copy-start.4 = (bf16[1,96,4096]{2,1,0:T(8,128)(2,1)S(1)}, bf16[1,96,4096]{2,1,0:T(8,128)(2,1)}, u32[]{:S(2)}) copy-start(bf16[1,96,4096]{2,1,0:T(8,128)(2,1)} %param.28) | copy-start | bytes 2359300
  199.4 48.2 %copy-start.1 = (bf16[1,768,512]{2,1,0:T(8,128)(2,1)S(1)}, bf16[1,768,512]{2,1,0:T(8,128)(2,1)}, u32[]{:S(2)}) copy-start(bf16[1,768,512]{2,1,0:T(8,128)(2,1)} %param.29) | copy-start | bytes 2359300
  250.5 29.0 %copy-start.3 = (bf16[1,96,4096]{2,1,0:T(8,128)(2,1)S(1)}, bf16[1,96,4096]{2,1,0:T(8,128)(2,1)}, u32[]{:S(2)}) copy-start(bf16[1,96,4096]{2,1,0:T(8,128)(2,1)} %param.27) | copy-start | bytes 2359300
  252.7 73.6 %all-to-all-start.1 = ((bf16[8,64,2,512]{3,2,0,1:T(2,128)(2,1)}), bf16[8,64,2,512]{3,2,0,1:T(2,128)(2,1)S(1)}, u32[]{:S(2)}, u32[]{:S(2)}) async-start(bf16[8,64,2,512]{3,2,0,1:T(2,128)(2,1)} %copy.80), calls=%async_computation.1 | async-start | bytes 2097152 | tf_op jit(solution)/shard_map/all_to_all | solution.py:169
  274.4 26.3 %collective-permute-start.2 = (bf16[768,512]{1,0:T(8,128)(2,1)S(1)}, bf16[768,512]{1,0:T(8,128)(2,1)}, u32[]{:S(2)}, u32[]{:S(2)}) collective-permute-start(bf16[768,512]{1,0:T(8,128)(2,1)S(1)} %bitcast.91), channel_id=1, source_target_pairs={{0,256},{8,264},{16,272},{24,280},{32,288},{40,296},{48,304},{56,3... | collective-permute-start | bytes 2359304 | tf_op jit(solution)/shard_map/ppermute | solution.py:14
  279.5 44.3 %collective-permute-start = (bf16[96,4096]{1,0:T(8,128)(2,1)S(1)}, bf16[96,4096]{1,0:T(8,128)(2,1)}, u32[]{:S(2)}, u32[]{:S(2)}) collective-permute-start(bf16[96,4096]{1,0:T(8,128)(2,1)S(1)} %bitcast.93), channel_id=1, source_target_pairs={{0,256},{8,264},{16,272},{24,280},{32,288},{40,296},{48,304},{56,3... | collective-permute-start | bytes 2359304 | tf_op jit(solution)/shard_map/ppermute | solution.py:14
  281.4 59.6 %collective-permute-start.1 = (bf16[96,4096]{1,0:T(8,128)(2,1)}, bf16[96,4096]{1,0:T(8,128)(2,1)}, u32[]{:S(2)}, u32[]{:S(2)}) collective-permute-start(bf16[96,4096]{1,0:T(8,128)(2,1)} %bitcast.94), channel_id=1, source_target_pairs={{0,256},{8,264},{16,272},{24,280},{32,288},{40,296},{48,304},{56,3... | collective-permute-start | bytes 2359304 | tf_op jit(solution)/shard_map/ppermute | solution.py:14
  324.8 16.2 %copy-start.5 = (bf16[1,96,4096]{2,1,0:T(8,128)(2,1)S(1)}, bf16[1,96,4096]{2,1,0:T(8,128)(2,1)}, u32[]{:S(2)}) copy-start(bf16[1,96,4096]{2,1,0:T(8,128)(2,1)} %param.28) | copy-start | bytes 2359300
  328.0 25.1 %all-to-all-start.2 = ((bf16[8,64,2,512]{3,2,1,0:T(2,128)(2,1)}), bf16[8,64,2,512]{3,2,1,0:T(2,128)(2,1)S(1)}, u32[]{:S(2)}, u32[]{:S(2)}) async-start(bf16[8,64,2,512]{3,2,1,0:T(2,128)(2,1)} %copy.81), calls=%async_computation.2 | async-start | bytes 2097152 | tf_op jit(solution)/shard_map/all_to_all | solution.py:168
  354.6 0.9 copy-start.8
Sparse Core Ops, SparseCore 0:
  91.8 97.5 all-gather.5
  206.6 40.9 all-gather.3

commit v7 on v6

--- a/solution.py
+++ b/solution.py
@@ -130,48 +130,34 @@
         ),
     ).astype(jnp.bfloat16)
     payload = jnp.concatenate([outgoing, side], axis=-1)
+    side_pad = ((0, 0), (0, side_cols))
+    gate_full = lax.all_gather(jnp.pad(own_weights[0], side_pad), "dp", axis=0, tiled=True)
+    up_full = lax.all_gather(jnp.pad(own_weights[1], side_pad), "dp", axis=0, tiled=True)
+    down_full = lax.all_gather(own_weights[2][None], "dp", axis=0, tiled=True)
+
     arrived = lax.all_to_all(payload, "expert", split_axis=0, concat_axis=0, tiled=True)
-    column = lax.all_gather(arrived[None], "dp", axis=0, tiled=True)
-    marks = column[:, :, :, width].astype(jnp.float32)
-    partner_total = jnp.sum(column[:, :, :, width + 1].astype(jnp.float32))
+    side_all = lax.all_gather(arrived[None, :, :, width:width + 2], "dp", axis=0, tiled=True)
+    marks = side_all[..., 0].astype(jnp.float32)
+    partner_total = jnp.sum(side_all[..., 1].astype(jnp.float32))
     occupied_flat = jnp.transpose(marks, (1, 0, 2)).reshape(-1)
     before_count = jnp.cumsum(occupied_flat) - occupied_flat
     kept_flat = occupied_flat * (
         before_count < admission_limits[my_index].astype(jnp.float32)
     ).astype(jnp.float32)
-    kept_mask = jnp.transpose(kept_flat.reshape(experts, groups, slot_cap), (1, 0, 2))
+    kept_mine = kept_flat.reshape(experts, groups, slot_cap)[:, lax.axis_index("dp")]
     own_total = jnp.sum(occupied_flat)
     held_tally = jnp.where(take_other, partner_total, own_total)
     device_share = jnp.minimum(
         held_tally, admission_limits[retained_specialist].astype(jnp.float32)
     ) / (seq_rows * routed_specialist_indices.shape[1] * groups)
 
-    side_pad = ((0, 0), (0, side_cols))
-    gate_wide = jnp.pad(own_weights[0], side_pad)
-    up_wide = jnp.pad(own_weights[1], side_pad)
-    gate_val = jnp.einsum(
-        "desf,hf->desh", column, gate_wide, preferred_element_type=jnp.float32
-    )
-    up_val = jnp.einsum("desf,hf->desh", column, up_wide, preferred_element_type=jnp.float32)
+    gate_val = jnp.einsum("esf,hf->esh", arrived, gate_full, preferred_element_type=jnp.float32)
+    up_val = jnp.einsum("esf,hf->esh", arrived, up_full, preferred_element_type=jnp.float32)
     hidden = (jax.nn.silu(gate_val) * up_val).astype(jnp.bfloat16)
-    hidden_kept = hidden * kept_mask[..., None].astype(jnp.bfloat16)
-    unit_count = hidden_kept.shape[-1]
-    hidden_all = lax.all_gather(
-        hidden_kept.reshape(1, groups * experts * slot_cap, unit_count), "dp", axis=0, tiled=True
-    )
-    feature_cols = own_weights[2].shape[1]
-    down_split = own_weights[2].reshape(groups, unit_count, feature_cols)
-    summed = jnp.einsum(
-        "gsn,gnf->sf", hidden_all, down_split, preferred_element_type=jnp.float32
-    )
-    results = summed.astype(jnp.bfloat16).reshape(groups, experts, slot_cap, feature_cols)
-    returned = lax.all_to_all(
-        lax.all_to_all(results, "expert", split_axis=1, concat_axis=1, tiled=True),
-        "dp",
-        split_axis=0,
-        concat_axis=3,
-        tiled=True,
-    )
+    summed = jnp.einsum("esn,gnf->esgf", hidden, down_full, preferred_element_type=jnp.float32)
+    results = summed.reshape(experts, slot_cap, width).astype(jnp.bfloat16)
+    results = results * kept_mine[..., None].astype(jnp.bfloat16)
+    returned = lax.all_to_all(results, "expert", split_axis=0, concat_axis=0, tiled=True)
     returned_flat = returned.reshape(experts * slot_cap, width)
     picked = returned_flat[slot_code]
     expert_mix = jnp.sum(routing_probabilities[:, :, None] * picked.astype(jnp.float32), axis=1)

time: 365 us -> 378 us (1.036)
  waiting for transfers between devices: 193 us -> 250 us
  blocking collectives: 72.5 us -> 24.5 us
  starting transfers between devices: 37.2 us -> 47 us
    all_to_all x1 -> x0, blocking collectives: 72.5 us -> none  [per_device(): lax.all_to_all(payload, 'expert', split_axis=0, concat_axis=0, tiled=True)]
    all_to_all x2, waiting for transfers between devices: 11.3 us -> 50.6 us  [the longest x1 50.6 us: per_device(): lax.all_to_all(payload, 'expert', split_axis=0, concat_axis=0, tiled=True)]
    all_gather x0 -> x1, blocking collectives: none -> 24.5 us  [per_device(): lax.all_gather(arrived[None, :, :, width:width + 2], 'dp', axis=0, tiled=...]
    all_gather x2 -> x3, waiting for transfers between devices: 136 us -> 146 us  [the longest x1 76.1 us: per_device(): down_full = lax.all_gather(own_weights[2][None], 'dp', axis=0, tiled=True)]
    all_to_all x2, starting transfers between devices: 25.2 us -> 35.1 us  [the longest x1 19.6 us: per_device(): lax.all_to_all(payload, 'expert', split_axis=0, concat_axis=0, tiled=True)]
    ppermute x3, waiting for transfers between devices: 45.2 us -> 52.1 us  [swapped(): return lax.ppermute(value, axis, pairs)]
    all_to_all x3 -> x0, local copies, waits for them, and re-layouts: 4.09 us -> none  [the longest x1 1.8 us: per_device(): lax.all_to_all(results, 'expert', split_axis=1, concat_axis=1, tiled=True)]
  transfers between devices with their start and end apart: 7 -> 8, of which waited for: 7 -> 6; matrix products, arithmetic and copies ran while one was open for 2% -> 7% of each run, Pallas kernels for 0% -> 0%
where the time goes in v7:
time: 378 us; the launch traced here: 376 us
  waiting for transfers between devices  250 us (66%)
  starting transfers between devices  47 us (12%)
  blocking collectives  24.5 us (6%)
  between operations  18.7 us (5%)
  matrix products  14.1 us (4%)
  local copies, waits for them, and re-layouts  13.1 us (3%)
  other arithmetic  9.35 us (2%)
    all_gather x1, waiting for transfers between devices, per_device(): down_full = lax.all_gather(own_weights[2][None], 'dp', axis=0, tiled=True)  76.1 us
    all_gather x1, waiting for transfers between devices, per_device(): lax.all_gather(jnp.pad(own_weights[1], side_pad), 'dp', axis=0, tiled=True)  70.3 us
    ppermute x3, waiting for transfers between devices, swapped(): return lax.ppermute(value, axis, pairs)  52.1 us
    all_to_all x1, waiting for transfers between devices, per_device(): lax.all_to_all(payload, 'expert', split_axis=0, concat_axis=0, tiled=True)  50.6 us
    all_gather x1, blocking collectives, per_device(): lax.all_gather(arrived[None, :, :, width:width + 2], 'dp', axis=0, tiled=...  24.5 us
    all_to_all x1, starting transfers between devices, per_device(): lax.all_to_all(payload, 'expert', split_axis=0, concat_axis=0, tiled=True)  19.6 us
    all_to_all x1, starting transfers between devices, per_device(): lax.all_to_all(results, 'expert', split_axis=0, concat_axis=0, tiled=True)  15.5 us
    ppermute x3, starting transfers between devices, swapped(): return lax.ppermute(value, axis, pairs)  11.7 us
  transfers between devices with their start and end apart: 8, of which 6 were waited for; matrix products, arithmetic and copies ran while one was open for 7% of the time, Pallas kernels for 0%

profile of v7, /device:TPU:1, one launch (start us, length us, event | category | flops | bytes accessed | tf_op | source)
XLA Modules:
  0.0 376.5 jit_solution(6168136245290113707)
XLA Ops:
  7.2 2.2 pad.8
  9.5 1.0 pad.9
  10.5 0.7 all-gather.9.cloned.1.call-update
  11.3 0.2 fusion.37
  11.5 0.3 fusion.50
  11.8 0.2 fusion.32
  12.1 0.3 fusion.24
  12.4 0.2 multiply_reduce_fusion
  12.6 0.5 copy-done.4
  13.3 0.3 select_reduce_fusion
  13.7 1.2 gather_fusion
  14.9 0.7 reshape.180
  16.0 0.2 fusion.34
  16.2 2.1 pad_maximum_fusion
  18.3 19.6 %all-to-all-start = ((bf16[64,2,4224]{2,1,0:T(2,128)(2,1)}), bf16[64,2,4224]{2,1,0:T(2,128)(2,1)S(1)}, u32[]{:S(2)}, u32[]{:S(2)}) async-start(bf16[64,2,4224]{2,1,0:T(2,128)(2,1)} %pad_maximum_fusion), calls=%async_computation | async-start | bytes 2162688 | tf_op jit(solution)/shard_map/all_to_all | solution.py:138
  37.9 0.6 dynamic_slice.14
  39.2 0.6 fusion.48
  40.4 50.6 %all-to-all-done = bf16[64,2,4224]{2,1,0:T(2,128)(2,1)S(1)} async-done(((bf16[64,2,4224]{2,1,0:T(2,128)(2,1)}), bf16[64,2,4224]{2,1,0:T(2,128)(2,1)S(1)}, u32[]{:S(2)}, u32[]{:S(2)}) %all-to-all-start) | async-done | bytes 1081376 | tf_op jit(solution)/shard_map/all_to_all | solution.py:138
  91.0 24.5 %all-gather = bf16[512,2,2]{2,1,0:T(2,128)(2,1)S(1)} all-gather(bf16[64,2,2]{2,1,0:T(2,128)(2,1)S(1)} %slice.35), channel_id=2, replica_groups=mesh['expert'=64,'dp'=8] {'dp'}, dimensions={0}, use_global_device_ids=true | all-gather | bytes 4608 | tf_op jit(solution)/shard_map/all_gather | solution.py:139
  115.6 1.1 fusion.47
  116.7 0.2 copy.96
  116.9 0.2 copy.88
  117.1 0.2 reshape.181
  117.2 0.3 reduce-window.9
  117.5 0.2 reshape.182
  118.3 4.8 %fusion.2 = f32[64,2,768]{2,0,1:T(8,128)S(1)} fusion(bf16[768,4224]{1,0:T(8,128)(2,1)} %all-gather.5.cloned.1.call-done, bf16[64,2,4224]{2,1,0:T(2,128)(2,1)S(1)} %all-to-all-done), kind=kOutput, calls=%fused_computation.4 | convolution fusion | flops 830472192 | bytes 7962624 | tf_op jit(solution)/shard_map/esf,hf->esh/dot_general | solution.py:154
  123.1 70.3 %all-gather.7.cloned.1.call-done = bf16[768,4224]{1,0:T(8,128)(2,1)} async-done(((bf16[96,4224]{1,0:T(8,128)(2,1)}), bf16[768,4224]{1,0:T(8,128)(2,1)}) %all-gather.7.cloned.1.call-update) | async-done | bytes 6488080 | tf_op jit(solution)/shard_map/all_gather | solution.py:135
  193.4 4.8 %fusion.18 = bf16[64,2,768,1]{2,0,3,1:T(8,128)(2,1)S(1)} fusion(bf16[768,4224]{1,0:T(8,128)(2,1)} %all-gather.7.cloned.1.call-done, bf16[64,2,4224]{2,1,0:T(2,128)(2,1)S(1)} %all-to-all-done, f32[64,2,768]{2,0,1:T(8,128)S(1)} %fusion.2), kind=kOutput, calls=%fused_computation.12 | convolution fusion | flops 831062016 | bytes 8159232 | tf_op jit(solution)/shard_map/esf,hf->esh/dot_general | solution.py:155
  198.2 76.1 %all-gather.9.cloned.1.call-done = bf16[8,768,512]{2,1,0:T(8,128)(2,1)} async-done(((bf16[1,768,512]{2,1,0:T(8,128)(2,1)}), bf16[8,768,512]{2,1,0:T(8,128)(2,1)}) %all-gather.9.cloned.1.call-update) | async-done | bytes 6291472 | tf_op jit(solution)/shard_map/all_gather | solution.py:136
  274.3 3.8 %fusion.9 = bf16[2,8,8,8,512]{4,3,2,1,0:T(8,128)(2,1)S(1)} fusion(bf16[64,2,768,1]{2,0,3,1:T(8,128)(2,1)S(1)} %fusion.18, bf16[8,768,512]{2,1,0:T(8,128)(2,1)} %all-gather.9.cloned.1.call-done), kind=kOutput, calls=%fused_computation.9 | convolution fusion | flops 805830656 | bytes 7536640 | tf_op jit(solution)/shard_map/esn,gnf->esgf/dot_general | solution.py:157
  278.4 2.1 copy.90
  280.5 15.5 %all-to-all-start.1 = ((bf16[64,2,4096]{2,1,0:T(2,128)(2,1)}), bf16[64,2,4096]{2,1,0:T(2,128)(2,1)S(1)}, u32[]{:S(2)}, u32[]{:S(2)}) async-start(bf16[64,2,4096]{2,1,0:T(2,128)(2,1)} %copy.90), calls=%async_computation.1 | async-start | bytes 2097152 | tf_op jit(solution)/shard_map/all_to_all | solution.py:160
  296.0 4.9 %collective-permute-start.2 = (bf16[768,512]{1,0:T(8,128)(2,1)S(1)}, bf16[768,512]{1,0:T(8,128)(2,1)}, u32[]{:S(2)}, u32[]{:S(2)}) collective-permute-start(bf16[768,512]{1,0:T(8,128)(2,1)S(1)} %bitcast.95), channel_id=1, source_target_pairs={{0,256},{8,264},{16,272},{24,280},{32,288},{40,296},{48,304},{56,3... | collective-permute-start | bytes 2359304 | tf_op jit(solution)/shard_map/ppermute | solution.py:14
  300.9 1.9 collective-permute-start.1
  302.9 4.9 %collective-permute-start = (bf16[96,4096]{1,0:T(8,128)(2,1)S(1)}, bf16[96,4096]{1,0:T(8,128)(2,1)}, u32[]{:S(2)}, u32[]{:S(2)}) collective-permute-start(bf16[96,4096]{1,0:T(8,128)(2,1)S(1)} %bitcast.99), channel_id=1, source_target_pairs={{0,256},{8,264},{16,272},{24,280},{32,288},{40,296},{48,304},{56,3... | collective-permute-start | bytes 2359304 | tf_op jit(solution)/shard_map/ppermute | solution.py:14
  308.5 13.7 %collective-permute-done.2 = bf16[768,512]{1,0:T(8,128)(2,1)} collective-permute-done((bf16[768,512]{1,0:T(8,128)(2,1)S(1)}, bf16[768,512]{1,0:T(8,128)(2,1)}, u32[]{:S(2)}, u32[]{:S(2)}) %collective-permute-start.2) | collective-permute-done | bytes 786464 | tf_op jit(solution)/shard_map/ppermute | solution.py:14
  322.2 1.0 select_bitcast_fusion
  323.1 22.2 %collective-permute-done.1 = bf16[96,4096]{1,0:T(8,128)(2,1)} collective-permute-done((bf16[96,4096]{1,0:T(8,128)(2,1)S(1)}, bf16[96,4096]{1,0:T(8,128)(2,1)}, u32[]{:S(2)}, u32[]{:S(2)}) %collective-permute-start.1) | collective-permute-done | bytes 786464 | tf_op jit(solution)/shard_map/ppermute | solution.py:14
  345.3 1.0 select_bitcast_fusion.1
  346.2 16.2 %collective-permute-done = bf16[96,4096]{1,0:T(8,128)(2,1)} collective-permute-done((bf16[96,4096]{1,0:T(8,128)(2,1)S(1)}, bf16[96,4096]{1,0:T(8,128)(2,1)}, u32[]{:S(2)}, u32[]{:S(2)}) %collective-permute-start) | collective-permute-done | bytes 786464 | tf_op jit(solution)/shard_map/ppermute | solution.py:14
  362.5 1.0 select_bitcast_fusion.2
  363.4 0.2 copy.97
  363.6 0.7 convert_reduce_fusion.2
  364.3 0.6 convert_reduce_fusion.3
  366.2 0.4 reshape.185
  366.7 0.9 gather_fusion.1
  367.6 0.4 fusion.25
  368.1 0.7 add_convert_fusion
  (81 shorter events, 1.9 us)
Async XLA Ops:
  7.2 4.9 %copy-start = (bf16[8,16,512]{2,1,0:T(8,128)(2,1)S(1)}, bf16[8,16,512]{2,1,0:T(8,128)(2,1)}, u32[]{:S(2)}) copy-start(bf16[8,16,512]{2,1,0:T(8,128)(2,1)} %param.18) | copy-start | bytes 393220
  7.2 2.3 copy-start.2
  7.2 111.1 %all-gather.5.cloned.1.call-start = ((), (), s32[]{:S(2)}) async-start(), calls=%async_computation.2 | async-start | bytes 7299072 | tf_op jit(solution)/shard_map/all_gather | solution.py:134
  9.4 1.8 copy-start.13
  9.4 1.9 copy-start.10
  9.4 1.9 copy-start.16
  9.4 2.0 copy-start.17
  9.4 2.1 copy-start.9
  9.5 184.0 %all-gather.7.cloned.1.call-start = ((), (), s32[]{:S(2)}) async-start(), calls=%async_computation.3 | async-start | bytes 7299072 | tf_op jit(solution)/shard_map/all_gather | solution.py:135
  10.5 1.9 copy-start.7
  10.5 2.5 copy-start.12
  10.5 2.7 copy-start.11
  10.5 263.8 %all-gather.9.cloned.1.call-start = ((), (), s32[]{:S(2)}) async-start(), calls=%async_computation.4 | async-start | bytes 7077888 | tf_op jit(solution)/shard_map/all_gather | solution.py:136
  12.4 0.7 copy-start.4
  16.2 21.7 %copy-start.18 = (s32[64]{0:T(128)S(1)}, s32[64]{0:T(128)}, u32[]{:S(2)}) copy-start(s32[64]{0:T(128)} %param.26) | copy-start | bytes 772
  16.2 23.0 %copy-start.15 = (s32[64]{0:T(128)S(1)}, s32[64]{0:T(128)}, u32[]{:S(2)}) copy-start(s32[64]{0:T(128)} %param.25) | copy-start | bytes 772
  18.3 72.7 %all-to-all-start = ((bf16[64,2,4224]{2,1,0:T(2,128)(2,1)}), bf16[64,2,4224]{2,1,0:T(2,128)(2,1)S(1)}, u32[]{:S(2)}, u32[]{:S(2)}) async-start(bf16[64,2,4224]{2,1,0:T(2,128)(2,1)} %pad_maximum_fusion), calls=%async_computation | async-start | bytes 2162688 | tf_op jit(solution)/shard_map/all_to_all | solution.py:138
  278.4 17.7 %copy-start.1 = (bf16[1,768,512]{2,1,0:T(8,128)(2,1)S(1)}, bf16[1,768,512]{2,1,0:T(8,128)(2,1)}, u32[]{:S(2)}) copy-start(bf16[1,768,512]{2,1,0:T(8,128)(2,1)} %param.29) | copy-start | bytes 2359300
  278.4 24.5 %copy-start.3 = (bf16[1,96,4096]{2,1,0:T(8,128)(2,1)S(1)}, bf16[1,96,4096]{2,1,0:T(8,128)(2,1)}, u32[]{:S(2)}) copy-start(bf16[1,96,4096]{2,1,0:T(8,128)(2,1)} %param.27) | copy-start | bytes 2359300
  280.5 85.8 %all-to-all-start.1 = ((bf16[64,2,4096]{2,1,0:T(2,128)(2,1)}), bf16[64,2,4096]{2,1,0:T(2,128)(2,1)S(1)}, u32[]{:S(2)}, u32[]{:S(2)}) async-start(bf16[64,2,4096]{2,1,0:T(2,128)(2,1)} %copy.90), calls=%async_computation.1 | async-start | bytes 2097152 | tf_op jit(solution)/shard_map/all_to_all | solution.py:160
  296.0 26.1 %collective-permute-start.2 = (bf16[768,512]{1,0:T(8,128)(2,1)S(1)}, bf16[768,512]{1,0:T(8,128)(2,1)}, u32[]{:S(2)}, u32[]{:S(2)}) collective-permute-start(bf16[768,512]{1,0:T(8,128)(2,1)S(1)} %bitcast.95), channel_id=1, source_target_pairs={{0,256},{8,264},{16,272},{24,280},{32,288},{40,296},{48,304},{56,3... | collective-permute-start | bytes 2359304 | tf_op jit(solution)/shard_map/ppermute | solution.py:14
  300.9 44.4 %collective-permute-start.1 = (bf16[96,4096]{1,0:T(8,128)(2,1)S(1)}, bf16[96,4096]{1,0:T(8,128)(2,1)}, u32[]{:S(2)}, u32[]{:S(2)}) collective-permute-start(bf16[96,4096]{1,0:T(8,128)(2,1)S(1)} %bitcast.97), channel_id=1, source_target_pairs={{0,256},{8,264},{16,272},{24,280},{32,288},{40,296},{48,304},{56,3... | collective-permute-start | bytes 2359304 | tf_op jit(solution)/shard_map/ppermute | solution.py:14
  302.9 59.6 %collective-permute-start = (bf16[96,4096]{1,0:T(8,128)(2,1)S(1)}, bf16[96,4096]{1,0:T(8,128)(2,1)}, u32[]{:S(2)}, u32[]{:S(2)}) collective-permute-start(bf16[96,4096]{1,0:T(8,128)(2,1)S(1)} %bitcast.99), channel_id=1, source_target_pairs={{0,256},{8,264},{16,272},{24,280},{32,288},{40,296},{48,304},{56,3... | collective-permute-start | bytes 2359304 | tf_op jit(solution)/shard_map/ppermute | solution.py:14
  323.1 40.3 %copy-start.6 = (bf16[8,64,2,1]{3,2,1,0:T(2,128)(2,1)S(1)}, bf16[8,64,2,1]{3,2,1,0:T(2,128)(2,1)}, u32[]{:S(2)}) copy-start(bf16[8,64,2,1]{3,2,1,0:T(2,128)(2,1)} %get-tuple-element.11) | copy-start | bytes 6148
  366.7 0.9 copy-start.14
  366.7 1.4 copy-start.5
  366.7 1.4 copy-start.8
Sparse Core Ops, SparseCore 0:
  10.1 99.9 all-gather.4
  112.1 81.2 all-gather.6
  195.5 78.7 all-gather.8

commit v8 on v6

--- a/solution.py
+++ b/solution.py
@@ -156,22 +156,20 @@
     hidden = (jax.nn.silu(gate_val) * up_val).astype(jnp.bfloat16)
     hidden_kept = hidden * kept_mask[..., None].astype(jnp.bfloat16)
     unit_count = hidden_kept.shape[-1]
-    hidden_all = lax.all_gather(
-        hidden_kept.reshape(1, groups * experts * slot_cap, unit_count), "dp", axis=0, tiled=True
-    )
-    feature_cols = own_weights[2].shape[1]
-    down_split = own_weights[2].reshape(groups, unit_count, feature_cols)
+    hidden_col = lax.all_to_all(hidden_kept, "dp", split_axis=0, concat_axis=3, tiled=True)[0]
+    own_down = own_weights[2]
+    down_blocks = [own_down] + [
+        lax.ppermute(own_down, "dp", [(j, (j + k) % groups) for j in range(groups)])
+        for k in range(1, groups)
+    ]
+    down_shifted = jnp.stack(down_blocks, axis=0)
     summed = jnp.einsum(
-        "gsn,gnf->sf", hidden_all, down_split, preferred_element_type=jnp.float32
-    )
-    results = summed.astype(jnp.bfloat16).reshape(groups, experts, slot_cap, feature_cols)
-    returned = lax.all_to_all(
-        lax.all_to_all(results, "expert", split_axis=1, concat_axis=1, tiled=True),
-        "dp",
-        split_axis=0,
-        concat_axis=3,
-        tiled=True,
-    )
+        "esn,knf->eskf", hidden_col, down_shifted, preferred_element_type=jnp.float32
+    )
+    block_of = (lax.axis_index("dp") - lax.broadcasted_iota(jnp.int32, (groups,), 0)) % groups
+    summed = jnp.take(summed.astype(jnp.bfloat16), block_of, axis=2)
+    results = summed.reshape(experts, slot_cap, width)
+    returned = lax.all_to_all(results, "expert", split_axis=0, concat_axis=0, tiled=True)
     returned_flat = returned.reshape(experts * slot_cap, width)
     picked = returned_flat[slot_code]
     expert_mix = jnp.sum(routing_probabilities[:, :, None] * picked.astype(jnp.float32), axis=1)

time: 365 us -> 400 us (1.096)
  starting transfers between devices: 37.2 us -> 70.8 us
  waiting for transfers between devices: 193 us -> 182 us
  local copies, waits for them, and re-layouts: 13.5 us -> 23.6 us
    ppermute x0 -> x7, waiting for transfers between devices: none -> 73 us  [per_device(): lax.ppermute(own_down, 'dp', [(j, (j + k) % groups) for j in range(groups)])]
    all_gather x1, waiting for transfers between devices: 95.1 us -> 53.2 us  [per_device(): column = lax.all_gather(arrived[None], 'dp', axis=0, tiled=True)]
    all_gather x1 -> x0, waiting for transfers between devices: 41.1 us -> none  [per_device(): lax.all_gather(hidden_kept.reshape(1, groups * experts * slot_cap, unit_c...]
    ppermute x0 -> x7, starting transfers between devices: none -> 32.5 us  [per_device(): lax.ppermute(own_down, 'dp', [(j, (j + k) % groups) for j in range(groups)])]
    unnamed x23 -> x33, local copies, waits for them, and re-layouts: 0.45 us -> 11.5 us
    all_to_all x2, waiting for transfers between devices: 11.3 us -> 4.14 us  [the longest x1 4.14 us: per_device(): lax.all_to_all(hidden_kept, 'dp', split_axis=0, concat_axis=3, tiled=True)]
    ppermute x3, waiting for transfers between devices: 45.2 us -> 52.1 us  [swapped(): return lax.ppermute(value, axis, pairs)]
  transfers between devices with their start and end apart: 7 -> 13, of which waited for: 7 -> 9; matrix products, arithmetic and copies ran while one was open for 2% -> 8% of each run, Pallas kernels for 0% -> 0%
where the time goes in v8:
time: 400 us; the launch traced here: 399 us
  waiting for transfers between devices  182 us (46%)
  blocking collectives  72.5 us (18%)
  starting transfers between devices  70.8 us (18%)
  local copies, waits for them, and re-layouts  23.6 us (6%)
  between operations  19 us (5%)
  matrix products  15.4 us (4%)
  other arithmetic  15.2 us (4%)
    ppermute x7, waiting for transfers between devices, per_device(): lax.ppermute(own_down, 'dp', [(j, (j + k) % groups) for j in range(groups)])  73 us
    all_to_all x1, blocking collectives, per_device(): lax.all_to_all(payload, 'expert', split_axis=0, concat_axis=0, tiled=True)  72.5 us
    all_gather x1, waiting for transfers between devices, per_device(): column = lax.all_gather(arrived[None], 'dp', axis=0, tiled=True)  53.2 us
    ppermute x3, waiting for transfers between devices, swapped(): return lax.ppermute(value, axis, pairs)  52.1 us
    ppermute x7, starting transfers between devices, per_device(): lax.ppermute(own_down, 'dp', [(j, (j + k) % groups) for j in range(groups)])  32.5 us
    all_to_all x1, starting transfers between devices, per_device(): lax.all_to_all(results, 'expert', split_axis=0, concat_axis=0, tiled=True)  14 us
    all_to_all x1, starting transfers between devices, per_device(): lax.all_to_all(hidden_kept, 'dp', split_axis=0, concat_axis=3, tiled=True)  12.5 us
    ppermute x3, starting transfers between devices, swapped(): return lax.ppermute(value, axis, pairs)  11.7 us
  transfers between devices with their start and end apart: 13, of which 9 were waited for; matrix products, arithmetic and copies ran while one was open for 8% of the time, Pallas kernels for 0%

profile of v8, /device:TPU:1, one launch (start us, length us, event | category | flops | bytes accessed | tf_op | source)
XLA Modules:
  0.0 398.8 jit_solution(493544865219542502)
XLA Ops:
  8.0 1.0 fusion.37
  9.0 1.2 fusion.54
  11.4 1.0 multiply_reduce_fusion
  12.5 0.8 convert_reduce_fusion.4
  13.3 1.0 select_reduce_fusion
  15.1 0.9 multiply_convert_fusion
  16.1 1.2 gather_fusion
  18.6 1.1 pad_maximum_fusion
  19.6 72.5 %all_to_all.25 = bf16[64,2,4224]{2,1,0:T(2,128)(2,1)S(1)} all-to-all(bf16[64,2,4224]{2,1,0:T(2,128)(2,1)S(1)} %pad_maximum_fusion), channel_id=1, replica_groups=mesh['expert'=64,'dp'=8] {'expert'}, dimensions={0} | all-to-all | bytes 2162688 | tf_op jit(solution)/shard_map/all_to_all | solution.py:133
  92.1 1.1 copy.55
  93.3 3.2 collective-permute-start
  96.5 4.5 %collective-permute-start.1 = (bf16[768,512]{1,0:T(8,128)(2,1)S(1)}, bf16[768,512]{1,0:T(8,128)(2,1)}, u32[]{:S(2)}, u32[]{:S(2)}) collective-permute-start(bf16[768,512]{1,0:T(8,128)(2,1)S(1)} %bitcast.114), channel_id=1, source_target_pairs={{0,2},{1,3},{2,4},{3,5},{4,6},{5,7},{6,0},{7,1},{8,10},{9,11},{10,... | collective-permute-start | bytes 2359304 | tf_op jit(solution)/shard_map/ppermute | solution.py:162
  101.0 3.0 collective-permute-start.2
  104.0 3.1 collective-permute-start.3
  107.1 2.3 collective-permute-start.4
  112.1 1.0 constant_dynamic-update-slice_fusion
  113.2 27.5 %collective-permute-done = bf16[768,512]{1,0:T(8,128)(2,1)} collective-permute-done((bf16[768,512]{1,0:T(8,128)(2,1)S(1)}, bf16[768,512]{1,0:T(8,128)(2,1)}, u32[]{:S(2)}, u32[]{:S(2)}) %collective-permute-start) | collective-permute-done | bytes 786464 | tf_op jit(solution)/shard_map/ppermute | solution.py:162
  140.7 2.6 collective-permute-start.5
  143.3 2.1 bitcast_dynamic-update-slice_fusion.6
  145.4 16.3 %collective-permute-done.1 = bf16[768,512]{1,0:T(8,128)(2,1)} collective-permute-done((bf16[768,512]{1,0:T(8,128)(2,1)S(1)}, bf16[768,512]{1,0:T(8,128)(2,1)}, u32[]{:S(2)}, u32[]{:S(2)}) %collective-permute-start.1) | collective-permute-done | bytes 786464 | tf_op jit(solution)/shard_map/ppermute | solution.py:162
  161.7 13.7 %collective-permute-start.6 = (bf16[768,512]{1,0:T(8,128)(2,1)S(1)}, bf16[768,512]{1,0:T(8,128)(2,1)}, u32[]{:S(2)}, u32[]{:S(2)}) collective-permute-start(bf16[768,512]{1,0:T(8,128)(2,1)S(1)} %bitcast.119), channel_id=1, source_target_pairs={{0,7},{1,0},{2,1},{3,2},{4,3},{5,4},{6,5},{7,6},{8,15},{9,8},{10,9... | collective-permute-start | bytes 2359304 | tf_op jit(solution)/shard_map/ppermute | solution.py:162
  175.5 2.1 bitcast_dynamic-update-slice_fusion.5
  177.6 12.6 %collective-permute-done.2 = bf16[768,512]{1,0:T(8,128)(2,1)} collective-permute-done((bf16[768,512]{1,0:T(8,128)(2,1)S(1)}, bf16[768,512]{1,0:T(8,128)(2,1)}, u32[]{:S(2)}, u32[]{:S(2)}) %collective-permute-start.2) | collective-permute-done | bytes 786464 | tf_op jit(solution)/shard_map/ppermute | solution.py:162
  190.2 2.1 bitcast_dynamic-update-slice_fusion.4
  192.2 2.1 bitcast_dynamic-update-slice_fusion.3
  194.3 16.5 %collective-permute-done.4 = bf16[768,512]{1,0:T(8,128)(2,1)S(1)} collective-permute-done((bf16[768,512]{1,0:T(8,128)(2,1)S(1)}, bf16[768,512]{1,0:T(8,128)(2,1)S(1)}, u32[]{:S(2)}, u32[]{:S(2)}) %collective-permute-start.4) | collective-permute-done | bytes 786464 | tf_op jit(solution)/shard_map/ppermute | solution.py:162
  210.8 1.0 bitcast_dynamic-update-slice_fusion.2
  211.8 0.9 bitcast_dynamic-update-slice_fusion.1
  212.7 53.2 %all-gather.3.cloned.1.call-done = bf16[512,2,4224]{2,0,1:T(8,128)(2,1)} async-done(((bf16[64,2,4224]{2,0,1:T(8,128)(2,1)}), bf16[512,2,4224]{2,0,1:T(8,128)(2,1)}) %all-gather.3.cloned.1.call-update) | async-done | bytes 8650768 | tf_op jit(solution)/shard_map/all_gather | solution.py:134
  265.9 1.9 convert_reduce_fusion
  269.3 6.0 %fusion.2 = f32[8,64,2,96]{3,1,2,0:T(8,128)S(1)} fusion(bf16[8,64,2,4224]{3,1,0,2:T(8,128)(2,1)} %bitcast.132, bf16[96,4096]{1,0:T(8,128)(2,1)S(1)} %bitcast.125), kind=kOutput, calls=%fused_computation.5 | convolution fusion | flops 830472192 | bytes 9830400 | tf_op jit(solution)/shard_map/desf,hf->desh/dot_general | solution.py:152
  275.5 3.1 fusion.15
  278.6 12.5 %all-to-all-start.1 = ((bf16[8,64,2,96]{3,1,2,0:T(8,128)(2,1)}), bf16[8,64,2,96]{3,1,2,0:T(8,128)(2,1)S(1)}, u32[]{:S(2)}, u32[]{:S(2)}) async-start(bf16[8,64,2,96]{3,1,2,0:T(8,128)(2,1)} %fusion.15), calls=%async_computation.1 | async-start | bytes 524288 | tf_op jit(solution)/shard_map/all_to_all | solution.py:159
  291.1 2.1 bitcast_dynamic-update-slice_fusion
  293.2 4.1 %all-to-all-done.1 = bf16[8,64,2,96]{3,1,2,0:T(8,128)(2,1)S(1)} async-done(((bf16[8,64,2,96]{3,1,2,0:T(8,128)(2,1)}), bf16[8,64,2,96]{3,1,2,0:T(8,128)(2,1)S(1)}, u32[]{:S(2)}, u32[]{:S(2)}) %all-to-all-start.1) | async-done | bytes 196640 | tf_op jit(solution)/shard_map/all_to_all | solution.py:159
  297.7 3.8 fusion.6
  302.4 2.1 copy.63
  304.4 14.0 %all-to-all-start.2 = ((bf16[64,2,4096]{2,1,0:T(2,128)(2,1)}), bf16[64,2,4096]{2,1,0:T(2,128)(2,1)S(1)}, u32[]{:S(2)}, u32[]{:S(2)}) async-start(bf16[64,2,4096]{2,1,0:T(2,128)(2,1)} %copy.63), calls=%async_computation.2 | async-start | bytes 2097152 | tf_op jit(solution)/shard_map/all_to_all | solution.py:172
  318.5 4.9 %collective-permute-start.9 = (bf16[768,512]{1,0:T(8,128)(2,1)S(1)}, bf16[768,512]{1,0:T(8,128)(2,1)}, u32[]{:S(2)}, u32[]{:S(2)}) collective-permute-start(bf16[768,512]{1,0:T(8,128)(2,1)S(1)} %bitcast.120), channel_id=1, source_target_pairs={{0,256},{8,264},{16,272},{24,280},{32,288},{40,296},{48,304},{56,3... | collective-permute-start | bytes 2359304 | tf_op jit(solution)/shard_map/ppermute | solution.py:14
  323.4 1.9 collective-permute-start.8
  325.3 4.9 %collective-permute-start.7 = (bf16[96,4096]{1,0:T(8,128)(2,1)}, bf16[96,4096]{1,0:T(8,128)(2,1)}, u32[]{:S(2)}, u32[]{:S(2)}) collective-permute-start(bf16[96,4096]{1,0:T(8,128)(2,1)} %bitcast.124), channel_id=1, source_target_pairs={{0,256},{8,264},{16,272},{24,280},{32,288},{40,296},{48,304},{56,3... | collective-permute-start | bytes 2359304 | tf_op jit(solution)/shard_map/ppermute | solution.py:14
  330.9 13.7 %collective-permute-done.9 = bf16[768,512]{1,0:T(8,128)(2,1)} collective-permute-done((bf16[768,512]{1,0:T(8,128)(2,1)S(1)}, bf16[768,512]{1,0:T(8,128)(2,1)}, u32[]{:S(2)}, u32[]{:S(2)}) %collective-permute-start.9) | collective-permute-done | bytes 786464 | tf_op jit(solution)/shard_map/ppermute | solution.py:14
  344.6 1.0 select_bitcast_fusion
  345.6 22.2 %collective-permute-done.8 = bf16[96,4096]{1,0:T(8,128)(2,1)} collective-permute-done((bf16[96,4096]{1,0:T(8,128)(2,1)S(1)}, bf16[96,4096]{1,0:T(8,128)(2,1)}, u32[]{:S(2)}, u32[]{:S(2)}) %collective-permute-start.8) | collective-permute-done | bytes 786464 | tf_op jit(solution)/shard_map/ppermute | solution.py:14
  367.7 1.0 select_bitcast_fusion.1
  368.7 16.2 %collective-permute-done.7 = bf16[96,4096]{1,0:T(8,128)(2,1)} collective-permute-done((bf16[96,4096]{1,0:T(8,128)(2,1)}, bf16[96,4096]{1,0:T(8,128)(2,1)}, u32[]{:S(2)}, u32[]{:S(2)}) %collective-permute-start.7) | collective-permute-done | bytes 786464 | tf_op jit(solution)/shard_map/ppermute | solution.py:14
  384.9 2.1 select_bitcast_fusion.2
  388.8 0.9 gather_fusion.2
  (84 shorter events, 9.8 us)
Async XLA Ops:
  7.2 4.0 %copy-start = (bf16[8,16,512]{2,1,0:T(8,128)(2,1)S(1)}, bf16[8,16,512]{2,1,0:T(8,128)(2,1)}, u32[]{:S(2)}) copy-start(bf16[8,16,512]{2,1,0:T(8,128)(2,1)} %param.18) | copy-start | bytes 393220
  7.2 258.8 %all-gather.3.cloned.1.call-start = ((), (), s32[]{:S(2)}) async-start(), calls=%async_computation.3 | async-start | bytes 9732096 | tf_op jit(solution)/shard_map/all_gather | solution.py:134
  17.3 76.0 %copy-start.1 = (bf16[1,768,512]{2,1,0:T(8,128)(2,1)S(1)}, bf16[1,768,512]{2,1,0:T(8,128)(2,1)}, u32[]{:S(2)}) copy-start(bf16[1,768,512]{2,1,0:T(8,128)(2,1)} %param.29) | copy-start | bytes 2359300
  17.3 92.3 %copy-start.8 = (s32[64]{0:T(128)S(1)}, s32[64]{0:T(128)}, u32[]{:S(2)}) copy-start(s32[64]{0:T(128)} %param.26) | copy-start | bytes 772
  17.3 93.5 %copy-start.7 = (s32[64]{0:T(128)S(1)}, s32[64]{0:T(128)}, u32[]{:S(2)}) copy-start(s32[64]{0:T(128)} %param.25) | copy-start | bytes 772
  93.3 47.4 %collective-permute-start = (bf16[768,512]{1,0:T(8,128)(2,1)S(1)}, bf16[768,512]{1,0:T(8,128)(2,1)}, u32[]{:S(2)}, u32[]{:S(2)}) collective-permute-start(bf16[768,512]{1,0:T(8,128)(2,1)S(1)} %bitcast.113), channel_id=1, source_target_pairs={{0,1},{1,2},{2,3},{3,4},{4,5},{5,6},{6,7},{7,0},{8,9},{9,10},{10,1... | collective-permute-start | bytes 2359304 | tf_op jit(solution)/shard_map/ppermute | solution.py:162
  96.5 65.3 %collective-permute-start.1 = (bf16[768,512]{1,0:T(8,128)(2,1)S(1)}, bf16[768,512]{1,0:T(8,128)(2,1)}, u32[]{:S(2)}, u32[]{:S(2)}) collective-permute-start(bf16[768,512]{1,0:T(8,128)(2,1)S(1)} %bitcast.114), channel_id=1, source_target_pairs={{0,2},{1,3},{2,4},{3,5},{4,6},{5,7},{6,0},{7,1},{8,10},{9,11},{10,... | collective-permute-start | bytes 2359304 | tf_op jit(solution)/shard_map/ppermute | solution.py:162
  101.0 89.1 %collective-permute-start.2 = (bf16[768,512]{1,0:T(8,128)(2,1)S(1)}, bf16[768,512]{1,0:T(8,128)(2,1)}, u32[]{:S(2)}, u32[]{:S(2)}) collective-permute-start(bf16[768,512]{1,0:T(8,128)(2,1)S(1)} %bitcast.115), channel_id=1, source_target_pairs={{0,3},{1,4},{2,5},{3,6},{4,7},{5,0},{6,1},{7,2},{8,11},{9,12},{10,... | collective-permute-start | bytes 2359304 | tf_op jit(solution)/shard_map/ppermute | solution.py:162
  104.0 88.2 %collective-permute-start.3 = (bf16[768,512]{1,0:T(8,128)(2,1)S(1)}, bf16[768,512]{1,0:T(8,128)(2,1)}, u32[]{:S(2)}, u32[]{:S(2)}) collective-permute-start(bf16[768,512]{1,0:T(8,128)(2,1)S(1)} %bitcast.116), channel_id=1, source_target_pairs={{0,4},{1,5},{2,6},{3,7},{4,0},{5,1},{6,2},{7,3},{8,12},{9,13},{10,... | collective-permute-start | bytes 2359304 | tf_op jit(solution)/shard_map/ppermute | solution.py:162
  107.1 103.7 %collective-permute-start.4 = (bf16[768,512]{1,0:T(8,128)(2,1)S(1)}, bf16[768,512]{1,0:T(8,128)(2,1)S(1)}, u32[]{:S(2)}, u32[]{:S(2)}) collective-permute-start(bf16[768,512]{1,0:T(8,128)(2,1)S(1)} %bitcast.117), channel_id=1, source_target_pairs={{0,5},{1,6},{2,7},{3,0},{4,1},{5,2},{6,3},{7,4},{8,13},{9,14},{10,... | collective-permute-start | bytes 2359304 | tf_op jit(solution)/shard_map/ppermute | solution.py:162
  112.1 157.1 %copy-start.4 = (bf16[1,96,4096]{2,1,0:T(8,128)(2,1)S(1)}, bf16[1,96,4096]{2,1,0:T(8,128)(2,1)}, u32[]{:S(2)}) copy-start(bf16[1,96,4096]{2,1,0:T(8,128)(2,1)} %param.27) | copy-start | bytes 2359300
  140.7 71.1 %collective-permute-start.5 = (bf16[768,512]{1,0:T(8,128)(2,1)S(1)}, bf16[768,512]{1,0:T(8,128)(2,1)S(1)}, u32[]{:S(2)}, u32[]{:S(2)}) collective-permute-start(bf16[768,512]{1,0:T(8,128)(2,1)S(1)} %bitcast.118), channel_id=1, source_target_pairs={{0,6},{1,7},{2,0},{3,1},{4,2},{5,3},{6,4},{7,5},{8,14},{9,15},{10,... | collective-permute-start | bytes 2359304 | tf_op jit(solution)/shard_map/ppermute | solution.py:162
  161.7 129.4 %collective-permute-start.6 = (bf16[768,512]{1,0:T(8,128)(2,1)S(1)}, bf16[768,512]{1,0:T(8,128)(2,1)}, u32[]{:S(2)}, u32[]{:S(2)}) collective-permute-start(bf16[768,512]{1,0:T(8,128)(2,1)S(1)} %bitcast.119), channel_id=1, source_target_pairs={{0,7},{1,0},{2,1},{3,2},{4,3},{5,4},{6,5},{7,6},{8,15},{9,8},{10,9... | collective-permute-start | bytes 2359304 | tf_op jit(solution)/shard_map/ppermute | solution.py:162
  268.8 6.5 %slice-start = ((s8[8650752]{0:T(1024)(128)(4,1)}), s8[262144]{0:T(1024)(128)(4,1)S(1)}, s32[]{:S(2)}) async-start(s8[8650752]{0:T(1024)(128)(4,1)} %bitcast.133), calls=%async_computation.4 | async-start | bytes 524288
  269.3 6.0 %copy-start.2 = (bf16[1,96,4096]{2,1,0:T(8,128)(2,1)S(1)}, bf16[1,96,4096]{2,1,0:T(8,128)(2,1)}, u32[]{:S(2)}) copy-start(bf16[1,96,4096]{2,1,0:T(8,128)(2,1)} %param.28) | copy-start | bytes 2359300
  269.3 6.0 %slice-start.1 = ((s8[8650752]{0:T(1024)(128)(4,1)}), s8[4194304]{0:T(1024)(128)(4,1)S(1)}, s32[]{:S(2)}) async-start(s8[8650752]{0:T(1024)(128)(4,1)} %bitcast.133), calls=%async_computation.5 | async-start | bytes 8388608
  269.3 6.2 %slice-start.2 = ((s8[8650752]{0:T(1024)(128)(4,1)}), s8[4194304]{0:T(1024)(128)(4,1)S(1)}, s32[]{:S(2)}) async-start(s8[8650752]{0:T(1024)(128)(4,1)} %bitcast.133), calls=%async_computation.6 | async-start | bytes 8388608
  278.6 18.7 %all-to-all-start.1 = ((bf16[8,64,2,96]{3,1,2,0:T(8,128)(2,1)}), bf16[8,64,2,96]{3,1,2,0:T(8,128)(2,1)S(1)}, u32[]{:S(2)}, u32[]{:S(2)}) async-start(bf16[8,64,2,96]{3,1,2,0:T(8,128)(2,1)} %fusion.15), calls=%async_computation.1 | async-start | bytes 524288 | tf_op jit(solution)/shard_map/all_to_all | solution.py:159
  302.1 21.3 %copy-start.3 = (bf16[1,96,4096]{2,1,0:T(8,128)(2,1)S(1)}, bf16[1,96,4096]{2,1,0:T(8,128)(2,1)}, u32[]{:S(2)}) copy-start(bf16[1,96,4096]{2,1,0:T(8,128)(2,1)} %param.28) | copy-start | bytes 2359300
  304.4 83.9 %all-to-all-start.2 = ((bf16[64,2,4096]{2,1,0:T(2,128)(2,1)}), bf16[64,2,4096]{2,1,0:T(2,128)(2,1)S(1)}, u32[]{:S(2)}, u32[]{:S(2)}) async-start(bf16[64,2,4096]{2,1,0:T(2,128)(2,1)} %copy.63), calls=%async_computation.2 | async-start | bytes 2097152 | tf_op jit(solution)/shard_map/all_to_all | solution.py:172
  318.5 26.1 %collective-permute-start.9 = (bf16[768,512]{1,0:T(8,128)(2,1)S(1)}, bf16[768,512]{1,0:T(8,128)(2,1)}, u32[]{:S(2)}, u32[]{:S(2)}) collective-permute-start(bf16[768,512]{1,0:T(8,128)(2,1)S(1)} %bitcast.120), channel_id=1, source_target_pairs={{0,256},{8,264},{16,272},{24,280},{32,288},{40,296},{48,304},{56,3... | collective-permute-start | bytes 2359304 | tf_op jit(solution)/shard_map/ppermute | solution.py:14
  323.4 44.3 %collective-permute-start.8 = (bf16[96,4096]{1,0:T(8,128)(2,1)S(1)}, bf16[96,4096]{1,0:T(8,128)(2,1)}, u32[]{:S(2)}, u32[]{:S(2)}) collective-permute-start(bf16[96,4096]{1,0:T(8,128)(2,1)S(1)} %bitcast.123), channel_id=1, source_target_pairs={{0,256},{8,264},{16,272},{24,280},{32,288},{40,296},{48,304},{56,3... | collective-permute-start | bytes 2359304 | tf_op jit(solution)/shard_map/ppermute | solution.py:14
  325.3 59.6 %collective-permute-start.7 = (bf16[96,4096]{1,0:T(8,128)(2,1)}, bf16[96,4096]{1,0:T(8,128)(2,1)}, u32[]{:S(2)}, u32[]{:S(2)}) collective-permute-start(bf16[96,4096]{1,0:T(8,128)(2,1)} %bitcast.124), channel_id=1, source_target_pairs={{0,256},{8,264},{16,272},{24,280},{32,288},{40,296},{48,304},{56,3... | collective-permute-start | bytes 2359304 | tf_op jit(solution)/shard_map/ppermute | solution.py:14
  345.6 44.1 %copy-start.6 = (f32[8,8]{1,0:T(8,128)S(1)}, f32[8,8]{1,0:T(8,128)}, u32[]{:S(2)}) copy-start(f32[8,8]{1,0:T(8,128)} %param.24) | copy-start | bytes 772
  345.6 44.6 %copy-start.5 = (bf16[8,4096]{1,0:T(8,128)(2,1)S(1)}, bf16[8,4096]{1,0:T(8,128)(2,1)}, u32[]{:S(2)}) copy-start(bf16[8,4096]{1,0:T(8,128)(2,1)} %param.15) | copy-start | bytes 196612
Sparse Core Ops, SparseCore 0:
  93.4 172.5 all-gather.2

commit v9 on v8

--- a/solution.py
+++ b/solution.py
@@ -130,7 +130,14 @@
         ),
     ).astype(jnp.bfloat16)
     payload = jnp.concatenate([outgoing, side], axis=-1)
+    own_down = own_weights[2]
+    down_blocks = [own_down] + [
+        lax.ppermute(own_down, "dp", [(j, (j + k) % groups) for j in range(groups)])
+        for k in range(1, groups)
+    ]
     arrived = lax.all_to_all(payload, "expert", split_axis=0, concat_axis=0, tiled=True)
+    arrived, down_blocks = lax.optimization_barrier((arrived, down_blocks))
+    down_shifted = jnp.stack(down_blocks, axis=0)
     column = lax.all_gather(arrived[None], "dp", axis=0, tiled=True)
     marks = column[:, :, :, width].astype(jnp.float32)
     partner_total = jnp.sum(column[:, :, :, width + 1].astype(jnp.float32))
@@ -157,12 +164,6 @@
     hidden_kept = hidden * kept_mask[..., None].astype(jnp.bfloat16)
     unit_count = hidden_kept.shape[-1]
     hidden_col = lax.all_to_all(hidden_kept, "dp", split_axis=0, concat_axis=3, tiled=True)[0]
-    own_down = own_weights[2]
-    down_blocks = [own_down] + [
-        lax.ppermute(own_down, "dp", [(j, (j + k) % groups) for j in range(groups)])
-        for k in range(1, groups)
-    ]
-    down_shifted = jnp.stack(down_blocks, axis=0)
     summed = jnp.einsum(
         "esn,knf->eskf", hidden_col, down_shifted, preferred_element_type=jnp.float32
     )

time: 400 us -> 393 us (0.983)
  blocking collectives: 72.5 us -> 0 us
  waiting for transfers between devices: 182 us -> 220 us
  starting transfers between devices: 70.8 us -> 96.7 us
    all_to_all x1 -> x0, blocking collectives: 72.5 us -> none  [per_device(): lax.all_to_all(payload, 'expert', split_axis=0, concat_axis=0, tiled=True)]
    all_gather x1, waiting for transfers between devices: 53.2 us -> 97.2 us  [per_device(): column = lax.all_gather(arrived[None], 'dp', axis=0, tiled=True)]
    all_to_all x0 -> x1, starting transfers between devices: none -> 19.6 us  [per_device(): lax.all_to_all(payload, 'expert', split_axis=0, concat_axis=0, tiled=True)]
    ppermute x7, starting transfers between devices: 32.5 us -> 44.9 us  [per_device(): lax.ppermute(own_down, 'dp', [(j, (j + k) % groups) for j in range(groups)])]
    all_to_all x1, starting transfers between devices: 12.5 us -> 3.59 us  [per_device(): lax.all_to_all(hidden_kept, 'dp', split_axis=0, concat_axis=3, tiled=True)]
    ppermute x7, waiting for transfers between devices: 73 us -> 65.9 us  [per_device(): lax.ppermute(own_down, 'dp', [(j, (j + k) % groups) for j in range(groups)])]
    unnamed x33 -> x47, local copies, waits for them, and re-layouts: 11.5 us -> 10.1 us
  transfers between devices with their start and end apart: 13 -> 14, of which waited for: 9 -> 9; matrix products, arithmetic and copies ran while one was open for 8% -> 4% of each run, Pallas kernels for 0% -> 0%
where the time goes in v9:
time: 393 us; the launch traced here: 392 us
  waiting for transfers between devices  220 us (56%)
  starting transfers between devices  96.7 us (25%)
  local copies, waits for them, and re-layouts  21 us (5%)
  between operations  19.1 us (5%)
  matrix products  18.7 us (5%)
  other arithmetic  16.3 us (4%)
    all_gather x1, waiting for transfers between devices, per_device(): column = lax.all_gather(arrived[None], 'dp', axis=0, tiled=True)  97.2 us
    ppermute x7, waiting for transfers between devices, per_device(): lax.ppermute(own_down, 'dp', [(j, (j + k) % groups) for j in range(groups)])  65.9 us
    ppermute x3, waiting for transfers between devices, swapped(): return lax.ppermute(value, axis, pairs)  52.1 us
    ppermute x7, starting transfers between devices, per_device(): lax.ppermute(own_down, 'dp', [(j, (j + k) % groups) for j in range(groups)])  44.9 us
    all_to_all x1, starting transfers between devices, per_device(): lax.all_to_all(payload, 'expert', split_axis=0, concat_axis=0, tiled=True)  19.6 us
    all_to_all x1, starting transfers between devices, per_device(): lax.all_to_all(results, 'expert', split_axis=0, concat_axis=0, tiled=True)  16.8 us
    ppermute x3, starting transfers between devices, swapped(): return lax.ppermute(value, axis, pairs)  11.7 us
    unnamed x47, local copies, waits for them, and re-layouts  10.1 us
  transfers between devices with their start and end apart: 14, of which 9 were waited for; matrix products, arithmetic and copies ran while one was open for 4% of the time, Pallas kernels for 0%

profile of v9, /device:TPU:1, one launch (start us, length us, event | category | flops | bytes accessed | tf_op | source)
XLA Modules:
  0.0 392.0 jit_solution(10391541444058460341)
XLA Ops:
  8.0 1.0 fusion.37
  9.0 1.2 fusion.54
  11.4 1.0 multiply_reduce_fusion
  13.3 1.0 select_reduce_fusion
  15.1 0.9 multiply_convert_fusion
  16.1 1.2 gather_fusion
  18.6 2.1 pad_maximum_fusion
  20.6 19.6 %all-to-all-start = ((bf16[64,2,4224]{2,1,0:T(2,128)(2,1)}), bf16[64,2,4224]{2,1,0:T(2,128)(2,1)S(1)}, u32[]{:S(2)}, u32[]{:S(2)}) async-start(bf16[64,2,4224]{2,1,0:T(2,128)(2,1)} %pad_maximum_fusion), calls=%async_computation | async-start | bytes 2162688 | tf_op jit(solution)/shard_map/all_to_all | solution.py:138
  40.3 3.2 collective-permute-start
  43.5 4.5 %collective-permute-start.1 = (bf16[768,512]{1,0:T(8,128)(2,1)S(1)}, bf16[768,512]{1,0:T(8,128)(2,1)S(1)}, u32[]{:S(2)}, u32[]{:S(2)}) collective-permute-start(bf16[768,512]{1,0:T(8,128)(2,1)S(1)} %bitcast.116), channel_id=1, source_target_pairs={{0,2},{1,3},{2,4},{3,5},{4,6},{5,7},{6,0},{7,1},{8,10},{9,11},{10,... | collective-permute-start | bytes 2359304 | tf_op jit(solution)/shard_map/ppermute | solution.py:135
  48.1 3.0 collective-permute-start.2
  51.1 3.1 collective-permute-start.3
  54.1 2.3 collective-permute-start.4
  56.5 22.7 %collective-permute-done = bf16[768,512]{1,0:T(8,128)(2,1)S(1)} collective-permute-done((bf16[768,512]{1,0:T(8,128)(2,1)S(1)}, bf16[768,512]{1,0:T(8,128)(2,1)S(1)}, u32[]{:S(2)}, u32[]{:S(2)}) %collective-permute-start) | collective-permute-done | bytes 786464 | tf_op jit(solution)/shard_map/ppermute | solution.py:135
  79.2 1.9 collective-permute-start.5
  81.2 26.9 %collective-permute-start.6 = (bf16[768,512]{1,0:T(8,128)(2,1)S(1)}, bf16[768,512]{1,0:T(8,128)(2,1)S(1)}, u32[]{:S(2)}, u32[]{:S(2)}) collective-permute-start(bf16[768,512]{1,0:T(8,128)(2,1)S(1)} %bitcast.121), channel_id=1, source_target_pairs={{0,7},{1,0},{2,1},{3,2},{4,3},{5,4},{6,5},{7,6},{8,15},{9,8},{10,9... | collective-permute-start | bytes 2359304 | tf_op jit(solution)/shard_map/ppermute | solution.py:135
  108.1 7.0 %collective-permute-done.4 = bf16[768,512]{1,0:T(8,128)(2,1)S(1)} collective-permute-done((bf16[768,512]{1,0:T(8,128)(2,1)S(1)}, bf16[768,512]{1,0:T(8,128)(2,1)S(1)}, u32[]{:S(2)}, u32[]{:S(2)}) %collective-permute-start.4) | collective-permute-done | bytes 786464 | tf_op jit(solution)/shard_map/ppermute | solution.py:135
  115.1 6.9 %collective-permute-done.5 = bf16[768,512]{1,0:T(8,128)(2,1)S(1)} collective-permute-done((bf16[768,512]{1,0:T(8,128)(2,1)S(1)}, bf16[768,512]{1,0:T(8,128)(2,1)S(1)}, u32[]{:S(2)}, u32[]{:S(2)}) %collective-permute-start.5) | collective-permute-done | bytes 786464 | tf_op jit(solution)/shard_map/ppermute | solution.py:135
  122.0 0.9 copy-done.13
  122.9 29.3 %collective-permute-done.6 = bf16[768,512]{1,0:T(8,128)(2,1)S(1)} collective-permute-done((bf16[768,512]{1,0:T(8,128)(2,1)S(1)}, bf16[768,512]{1,0:T(8,128)(2,1)S(1)}, u32[]{:S(2)}, u32[]{:S(2)}) %collective-permute-start.6) | collective-permute-done | bytes 786464 | tf_op jit(solution)/shard_map/ppermute | solution.py:135
  152.2 1.1 copy.55
  156.1 1.0 bitcast_dynamic-update-slice_fusion.7
  157.1 2.1 bitcast_dynamic-update-slice_fusion.6
  159.1 2.1 bitcast_dynamic-update-slice_fusion.5
  161.3 1.0 bitcast_dynamic-update-slice_fusion.4
  162.2 0.9 bitcast_dynamic-update-slice_fusion.3
  163.2 1.0 bitcast_dynamic-update-slice_fusion.2
  164.1 0.9 bitcast_dynamic-update-slice_fusion.1
  165.1 97.2 %all-gather.3.cloned.1.call-done = bf16[512,2,4224]{2,0,1:T(8,128)(2,1)} async-done(((bf16[64,2,4224]{2,0,1:T(8,128)(2,1)}), bf16[512,2,4224]{2,0,1:T(8,128)(2,1)}) %all-gather.3.cloned.1.call-update) | async-done | bytes 8650768 | tf_op jit(solution)/shard_map/all_gather | solution.py:141
  262.3 1.9 convert_reduce_fusion
  265.6 5.9 %fusion.2 = f32[8,64,2,96]{3,1,2,0:T(8,128)S(1)} fusion(bf16[8,64,2,4224]{3,1,0,2:T(8,128)(2,1)} %bitcast.135, bf16[96,4096]{1,0:T(8,128)(2,1)S(1)} %bitcast.128), kind=kOutput, calls=%fused_computation.5 | convolution fusion | flops 830472192 | bytes 9830400 | tf_op jit(solution)/shard_map/desf,hf->desh/dot_general | solution.py:159
  271.5 6.6 %fusion.15 = bf16[8,64,2,96]{3,1,2,0:T(8,128)(2,1)} fusion(bf16[8,64,2,4224]{3,1,0,2:T(8,128)(2,1)} %bitcast.136, bf16[96,4096]{1,0:T(8,128)(2,1)S(1)} %bitcast.125, f32[8,64,2,96]{3,1,2,0:T(8,128)S(1)} %fusion.2, bf16[8,64,2]{1,2,0:T(2,128)(2,1)S(1)} %copy.60), kind=kOutput, calls=%fused_computation.12 | convolution fusion | flops 831160320 | bytes 10029056 | tf_op jit(solution)/shard_map/desf,hf->desh/dot_general | solution.py:162
  278.1 3.6 all-to-all-start.1
  281.7 0.9 bitcast_dynamic-update-slice_fusion
  282.6 5.0 %all-to-all-done.1 = bf16[8,64,2,96]{3,1,2,0:T(8,128)(2,1)S(1)} async-done(((bf16[8,64,2,96]{3,1,2,0:T(8,128)(2,1)}), bf16[8,64,2,96]{3,1,2,0:T(8,128)(2,1)S(1)}, u32[]{:S(2)}, u32[]{:S(2)}) %all-to-all-start.1) | async-done | bytes 196640 | tf_op jit(solution)/shard_map/all_to_all | solution.py:166
  288.1 3.8 fusion.6
  292.7 2.1 copy.63
  294.8 16.8 %all-to-all-start.2 = ((bf16[64,2,4096]{2,1,0:T(2,128)(2,1)}), bf16[64,2,4096]{2,1,0:T(2,128)(2,1)S(1)}, u32[]{:S(2)}, u32[]{:S(2)}) async-start(bf16[64,2,4096]{2,1,0:T(2,128)(2,1)} %copy.63), calls=%async_computation.2 | async-start | bytes 2097152 | tf_op jit(solution)/shard_map/all_to_all | solution.py:173
  311.6 4.9 %collective-permute-start.9 = (bf16[768,512]{1,0:T(8,128)(2,1)S(1)}, bf16[768,512]{1,0:T(8,128)(2,1)}, u32[]{:S(2)}, u32[]{:S(2)}) collective-permute-start(bf16[768,512]{1,0:T(8,128)(2,1)S(1)} %bitcast.123), channel_id=1, source_target_pairs={{0,256},{8,264},{16,272},{24,280},{32,288},{40,296},{48,304},{56,3... | collective-permute-start | bytes 2359304 | tf_op jit(solution)/shard_map/ppermute | solution.py:14
  316.5 1.9 collective-permute-start.8
  318.5 4.9 %collective-permute-start.7 = (bf16[96,4096]{1,0:T(8,128)(2,1)}, bf16[96,4096]{1,0:T(8,128)(2,1)}, u32[]{:S(2)}, u32[]{:S(2)}) collective-permute-start(bf16[96,4096]{1,0:T(8,128)(2,1)} %bitcast.127), channel_id=1, source_target_pairs={{0,256},{8,264},{16,272},{24,280},{32,288},{40,296},{48,304},{56,3... | collective-permute-start | bytes 2359304 | tf_op jit(solution)/shard_map/ppermute | solution.py:14
  324.1 13.7 %collective-permute-done.9 = bf16[768,512]{1,0:T(8,128)(2,1)} collective-permute-done((bf16[768,512]{1,0:T(8,128)(2,1)S(1)}, bf16[768,512]{1,0:T(8,128)(2,1)}, u32[]{:S(2)}, u32[]{:S(2)}) %collective-permute-start.9) | collective-permute-done | bytes 786464 | tf_op jit(solution)/shard_map/ppermute | solution.py:14
  337.8 1.0 select_bitcast_fusion
  338.7 22.2 %collective-permute-done.8 = bf16[96,4096]{1,0:T(8,128)(2,1)} collective-permute-done((bf16[96,4096]{1,0:T(8,128)(2,1)S(1)}, bf16[96,4096]{1,0:T(8,128)(2,1)}, u32[]{:S(2)}, u32[]{:S(2)}) %collective-permute-start.8) | collective-permute-done | bytes 786464 | tf_op jit(solution)/shard_map/ppermute | solution.py:14
  360.9 1.0 select_bitcast_fusion.1
  361.9 16.2 %collective-permute-done.7 = bf16[96,4096]{1,0:T(8,128)(2,1)} collective-permute-done((bf16[96,4096]{1,0:T(8,128)(2,1)}, bf16[96,4096]{1,0:T(8,128)(2,1)}, u32[]{:S(2)}, u32[]{:S(2)}) %collective-permute-start.7) | collective-permute-done | bytes 786464 | tf_op jit(solution)/shard_map/ppermute | solution.py:14
  378.1 2.1 select_bitcast_fusion.2
  382.0 0.9 gather_fusion.2
  (97 shorter events, 10.6 us)
Async XLA Ops:
  7.2 4.0 %copy-start = (bf16[8,16,512]{2,1,0:T(8,128)(2,1)S(1)}, bf16[8,16,512]{2,1,0:T(8,128)(2,1)}, u32[]{:S(2)}) copy-start(bf16[8,16,512]{2,1,0:T(8,128)(2,1)} %param.18) | copy-start | bytes 393220
  16.1 24.2 %copy-start.1 = (bf16[1,768,512]{2,1,0:T(8,128)(2,1)S(1)}, bf16[1,768,512]{2,1,0:T(8,128)(2,1)}, u32[]{:S(2)}) copy-start(bf16[1,768,512]{2,1,0:T(8,128)(2,1)} %param.29) | copy-start | bytes 2359300
  17.3 136.0 %copy-start.18 = (s32[64]{0:T(128)S(1)}, s32[64]{0:T(128)}, u32[]{:S(2)}) copy-start(s32[64]{0:T(128)} %param.26) | copy-start | bytes 772
  17.3 137.3 %copy-start.17 = (s32[64]{0:T(128)S(1)}, s32[64]{0:T(128)}, u32[]{:S(2)}) copy-start(s32[64]{0:T(128)} %param.25) | copy-start | bytes 772
  20.6 131.5 %all-to-all-start = ((bf16[64,2,4224]{2,1,0:T(2,128)(2,1)}), bf16[64,2,4224]{2,1,0:T(2,128)(2,1)S(1)}, u32[]{:S(2)}, u32[]{:S(2)}) async-start(bf16[64,2,4224]{2,1,0:T(2,128)(2,1)} %pad_maximum_fusion), calls=%async_computation | async-start | bytes 2162688 | tf_op jit(solution)/shard_map/all_to_all | solution.py:138
  40.3 222.0 %all-gather.3.cloned.1.call-start = ((), (), s32[]{:S(2)}) async-start(), calls=%async_computation.3 | async-start | bytes 9732096 | tf_op jit(solution)/shard_map/all_gather | solution.py:141
  40.3 38.9 %collective-permute-start = (bf16[768,512]{1,0:T(8,128)(2,1)S(1)}, bf16[768,512]{1,0:T(8,128)(2,1)S(1)}, u32[]{:S(2)}, u32[]{:S(2)}) collective-permute-start(bf16[768,512]{1,0:T(8,128)(2,1)S(1)} %bitcast.115), channel_id=1, source_target_pairs={{0,1},{1,2},{2,3},{3,4},{4,5},{5,6},{6,7},{7,0},{8,9},{9,10},{10,1... | collective-permute-start | bytes 2359304 | tf_op jit(solution)/shard_map/ppermute | solution.py:135
  43.5 37.6 %collective-permute-start.1 = (bf16[768,512]{1,0:T(8,128)(2,1)S(1)}, bf16[768,512]{1,0:T(8,128)(2,1)S(1)}, u32[]{:S(2)}, u32[]{:S(2)}) collective-permute-start(bf16[768,512]{1,0:T(8,128)(2,1)S(1)} %bitcast.116), channel_id=1, source_target_pairs={{0,2},{1,3},{2,4},{3,5},{4,6},{5,7},{6,0},{7,1},{8,10},{9,11},{10,... | collective-permute-start | bytes 2359304 | tf_op jit(solution)/shard_map/ppermute | solution.py:135
  48.1 60.0 %collective-permute-start.2 = (bf16[768,512]{1,0:T(8,128)(2,1)S(1)}, bf16[768,512]{1,0:T(8,128)(2,1)S(1)}, u32[]{:S(2)}, u32[]{:S(2)}) collective-permute-start(bf16[768,512]{1,0:T(8,128)(2,1)S(1)} %bitcast.117), channel_id=1, source_target_pairs={{0,3},{1,4},{2,5},{3,6},{4,7},{5,0},{6,1},{7,2},{8,11},{9,12},{10,... | collective-permute-start | bytes 2359304 | tf_op jit(solution)/shard_map/ppermute | solution.py:135
  51.1 57.0 %collective-permute-start.3 = (bf16[768,512]{1,0:T(8,128)(2,1)S(1)}, bf16[768,512]{1,0:T(8,128)(2,1)S(1)}, u32[]{:S(2)}, u32[]{:S(2)}) collective-permute-start(bf16[768,512]{1,0:T(8,128)(2,1)S(1)} %bitcast.118), channel_id=1, source_target_pairs={{0,4},{1,5},{2,6},{3,7},{4,0},{5,1},{6,2},{7,3},{8,12},{9,13},{10,... | collective-permute-start | bytes 2359304 | tf_op jit(solution)/shard_map/ppermute | solution.py:135
  54.1 60.9 %collective-permute-start.4 = (bf16[768,512]{1,0:T(8,128)(2,1)S(1)}, bf16[768,512]{1,0:T(8,128)(2,1)S(1)}, u32[]{:S(2)}, u32[]{:S(2)}) collective-permute-start(bf16[768,512]{1,0:T(8,128)(2,1)S(1)} %bitcast.119), channel_id=1, source_target_pairs={{0,5},{1,6},{2,7},{3,0},{4,1},{5,2},{6,3},{7,4},{8,13},{9,14},{10,... | collective-permute-start | bytes 2359304 | tf_op jit(solution)/shard_map/ppermute | solution.py:135
  79.2 42.7 %copy-start.5 = (bf16[768,512]{1,0:T(8,128)(2,1)}, bf16[768,512]{1,0:T(8,128)(2,1)S(1)}, u32[]{:S(2)}) copy-start(bf16[768,512]{1,0:T(8,128)(2,1)S(1)} %collective-permute-done) | copy-start | bytes 2359300
  79.2 42.7 %collective-permute-start.5 = (bf16[768,512]{1,0:T(8,128)(2,1)S(1)}, bf16[768,512]{1,0:T(8,128)(2,1)S(1)}, u32[]{:S(2)}, u32[]{:S(2)}) collective-permute-start(bf16[768,512]{1,0:T(8,128)(2,1)S(1)} %bitcast.120), channel_id=1, source_target_pairs={{0,6},{1,7},{2,0},{3,1},{4,2},{5,3},{6,4},{7,5},{8,14},{9,15},{10,... | collective-permute-start | bytes 2359304 | tf_op jit(solution)/shard_map/ppermute | solution.py:135
  81.2 40.8 %copy-start.6 = (bf16[768,512]{1,0:T(8,128)(2,1)}, bf16[768,512]{1,0:T(8,128)(2,1)S(1)}, u32[]{:S(2)}) copy-start(bf16[768,512]{1,0:T(8,128)(2,1)S(1)} %collective-permute-done.1) | copy-start | bytes 2359300
  81.2 71.0 %collective-permute-start.6 = (bf16[768,512]{1,0:T(8,128)(2,1)S(1)}, bf16[768,512]{1,0:T(8,128)(2,1)S(1)}, u32[]{:S(2)}, u32[]{:S(2)}) collective-permute-start(bf16[768,512]{1,0:T(8,128)(2,1)S(1)} %bitcast.121), channel_id=1, source_target_pairs={{0,7},{1,0},{2,1},{3,2},{4,3},{5,4},{6,5},{7,6},{8,15},{9,8},{10,9... | collective-permute-start | bytes 2359304 | tf_op jit(solution)/shard_map/ppermute | solution.py:135
  108.0 13.9 %copy-start.7 = (bf16[768,512]{1,0:T(8,128)(2,1)}, bf16[768,512]{1,0:T(8,128)(2,1)S(1)}, u32[]{:S(2)}) copy-start(bf16[768,512]{1,0:T(8,128)(2,1)S(1)} %collective-permute-done.2) | copy-start | bytes 2359300
  108.1 13.9 %copy-start.9 = (bf16[768,512]{1,0:T(8,128)(2,1)}, bf16[768,512]{1,0:T(8,128)(2,1)S(1)}, u32[]{:S(2)}) copy-start(bf16[768,512]{1,0:T(8,128)(2,1)S(1)} %collective-permute-done.3) | copy-start | bytes 2359300
  115.1 6.9 %copy-start.11 = (bf16[768,512]{1,0:T(8,128)(2,1)}, bf16[768,512]{1,0:T(8,128)(2,1)S(1)}, u32[]{:S(2)}) copy-start(bf16[768,512]{1,0:T(8,128)(2,1)S(1)} %collective-permute-done.4) | copy-start | bytes 2359300
  122.0 0.9 copy-start.13
  153.3 8.0 %copy-start.8 = (bf16[768,512]{1,0:T(8,128)(2,1)S(1)}, bf16[768,512]{1,0:T(8,128)(2,1)}, u32[]{:S(2)}) copy-start(bf16[768,512]{1,0:T(8,128)(2,1)} %copy-done.7) | copy-start | bytes 2359300
  154.6 7.6 %copy-start.10 = (bf16[768,512]{1,0:T(8,128)(2,1)S(1)}, bf16[768,512]{1,0:T(8,128)(2,1)}, u32[]{:S(2)}) copy-start(bf16[768,512]{1,0:T(8,128)(2,1)} %copy-done.9) | copy-start | bytes 2359300
  154.6 8.6 %copy-start.12 = (bf16[768,512]{1,0:T(8,128)(2,1)S(1)}, bf16[768,512]{1,0:T(8,128)(2,1)}, u32[]{:S(2)}) copy-start(bf16[768,512]{1,0:T(8,128)(2,1)} %copy-done.11) | copy-start | bytes 2359300
  154.6 9.5 %copy-start.14 = (bf16[768,512]{1,0:T(8,128)(2,1)S(1)}, bf16[768,512]{1,0:T(8,128)(2,1)}, u32[]{:S(2)}) copy-start(bf16[768,512]{1,0:T(8,128)(2,1)} %copy-done.13) | copy-start | bytes 2359300
  156.0 109.5 %copy-start.4 = (bf16[1,96,4096]{2,1,0:T(8,128)(2,1)S(1)}, bf16[1,96,4096]{2,1,0:T(8,128)(2,1)}, u32[]{:S(2)}) copy-start(bf16[1,96,4096]{2,1,0:T(8,128)(2,1)} %param.27) | copy-start | bytes 2359300
  265.6 5.9 %copy-start.2 = (bf16[1,96,4096]{2,1,0:T(8,128)(2,1)S(1)}, bf16[1,96,4096]{2,1,0:T(8,128)(2,1)}, u32[]{:S(2)}) copy-start(bf16[1,96,4096]{2,1,0:T(8,128)(2,1)} %param.28) | copy-start | bytes 2359300
  278.1 9.6 %all-to-all-start.1 = ((bf16[8,64,2,96]{3,1,2,0:T(8,128)(2,1)}), bf16[8,64,2,96]{3,1,2,0:T(8,128)(2,1)S(1)}, u32[]{:S(2)}, u32[]{:S(2)}) async-start(bf16[8,64,2,96]{3,1,2,0:T(8,128)(2,1)} %fusion.15), calls=%async_computation.1 | async-start | bytes 524288 | tf_op jit(solution)/shard_map/all_to_all | solution.py:166
  292.6 24.0 %copy-start.3 = (bf16[1,96,4096]{2,1,0:T(8,128)(2,1)S(1)}, bf16[1,96,4096]{2,1,0:T(8,128)(2,1)}, u32[]{:S(2)}) copy-start(bf16[1,96,4096]{2,1,0:T(8,128)(2,1)} %param.28) | copy-start | bytes 2359300
  294.8 86.7 %all-to-all-start.2 = ((bf16[64,2,4096]{2,1,0:T(2,128)(2,1)}), bf16[64,2,4096]{2,1,0:T(2,128)(2,1)S(1)}, u32[]{:S(2)}, u32[]{:S(2)}) async-start(bf16[64,2,4096]{2,1,0:T(2,128)(2,1)} %copy.63), calls=%async_computation.2 | async-start | bytes 2097152 | tf_op jit(solution)/shard_map/all_to_all | solution.py:173
  311.6 26.1 %collective-permute-start.9 = (bf16[768,512]{1,0:T(8,128)(2,1)S(1)}, bf16[768,512]{1,0:T(8,128)(2,1)}, u32[]{:S(2)}, u32[]{:S(2)}) collective-permute-start(bf16[768,512]{1,0:T(8,128)(2,1)S(1)} %bitcast.123), channel_id=1, source_target_pairs={{0,256},{8,264},{16,272},{24,280},{32,288},{40,296},{48,304},{56,3... | collective-permute-start | bytes 2359304 | tf_op jit(solution)/shard_map/ppermute | solution.py:14
  316.5 44.3 %collective-permute-start.8 = (bf16[96,4096]{1,0:T(8,128)(2,1)S(1)}, bf16[96,4096]{1,0:T(8,128)(2,1)}, u32[]{:S(2)}, u32[]{:S(2)}) collective-permute-start(bf16[96,4096]{1,0:T(8,128)(2,1)S(1)} %bitcast.126), channel_id=1, source_target_pairs={{0,256},{8,264},{16,272},{24,280},{32,288},{40,296},{48,304},{56,3... | collective-permute-start | bytes 2359304 | tf_op jit(solution)/shard_map/ppermute | solution.py:14
  318.5 59.6 %collective-permute-start.7 = (bf16[96,4096]{1,0:T(8,128)(2,1)}, bf16[96,4096]{1,0:T(8,128)(2,1)}, u32[]{:S(2)}, u32[]{:S(2)}) collective-permute-start(bf16[96,4096]{1,0:T(8,128)(2,1)} %bitcast.127), channel_id=1, source_target_pairs={{0,256},{8,264},{16,272},{24,280},{32,288},{40,296},{48,304},{56,3... | collective-permute-start | bytes 2359304 | tf_op jit(solution)/shard_map/ppermute | solution.py:14
  338.7 44.1 %copy-start.16 = (f32[8,8]{1,0:T(8,128)S(1)}, f32[8,8]{1,0:T(8,128)}, u32[]{:S(2)}) copy-start(f32[8,8]{1,0:T(8,128)} %param.24) | copy-start | bytes 772
  338.7 44.6 %copy-start.15 = (bf16[8,4096]{1,0:T(8,128)(2,1)S(1)}, bf16[8,4096]{1,0:T(8,128)(2,1)}, u32[]{:S(2)}) copy-start(bf16[8,4096]{1,0:T(8,128)(2,1)} %param.15) | copy-start | bytes 196612
Sparse Core Ops, SparseCore 0:
  153.4 108.7 all-gather.2

commit v10 on v6

--- a/solution.py
+++ b/solution.py
@@ -131,6 +131,7 @@
     ).astype(jnp.bfloat16)
     payload = jnp.concatenate([outgoing, side], axis=-1)
     arrived = lax.all_to_all(payload, "expert", split_axis=0, concat_axis=0, tiled=True)
+    arrived, partner = lax.optimization_barrier((arrived, partner))
     column = lax.all_gather(arrived[None], "dp", axis=0, tiled=True)
     marks = column[:, :, :, width].astype(jnp.float32)
     partner_total = jnp.sum(column[:, :, :, width + 1].astype(jnp.float32))

time: 365 us -> 379 us (1.038)
  blocking collectives: 72.5 us -> 0 us
  waiting for transfers between devices: 193 us -> 257 us
  starting transfers between devices: 37.2 us -> 56.9 us
    all_to_all x1 -> x0, blocking collectives: 72.5 us -> none  [per_device(): lax.all_to_all(payload, 'expert', split_axis=0, concat_axis=0, tiled=True)]
    all_to_all x1, waiting for transfers between devices: 1.46 us -> 49.1 us  [per_device(): lax.all_to_all(results, 'expert', split_axis=1, concat_axis=1, tiled=True)]
    all_to_all x0 -> x1, starting transfers between devices: none -> 19.7 us  [per_device(): lax.all_to_all(payload, 'expert', split_axis=0, concat_axis=0, tiled=True)]
    ppermute x3, waiting for transfers between devices: 45.2 us -> 54.2 us  [swapped(): return lax.ppermute(value, axis, pairs)]
    all_gather x1, waiting for transfers between devices: 95.1 us -> 99.9 us  [per_device(): column = lax.all_gather(arrived[None], 'dp', axis=0, tiled=True)]
  transfers between devices with their start and end apart: 7 -> 8, of which waited for: 7 -> 7; matrix products, arithmetic and copies ran while one was open for 2% -> 1% of each run, Pallas kernels for 0% -> 0%
where the time goes in v10:
time: 379 us; the launch traced here: 377 us
  waiting for transfers between devices  257 us (68%)
  starting transfers between devices  56.9 us (15%)
  between operations  19 us (5%)
  matrix products  16.7 us (4%)
  local copies, waits for them, and re-layouts  14.4 us (4%)
  other arithmetic  13.3 us (4%)
    all_gather x1, waiting for transfers between devices, per_device(): column = lax.all_gather(arrived[None], 'dp', axis=0, tiled=True)  99.9 us
    ppermute x3, waiting for transfers between devices, swapped(): return lax.ppermute(value, axis, pairs)  54.2 us
    all_to_all x1, waiting for transfers between devices, per_device(): lax.all_to_all(results, 'expert', split_axis=1, concat_axis=1, tiled=True)  49.1 us
    all_gather x1, waiting for transfers between devices, per_device(): lax.all_gather(hidden_kept.reshape(1, groups * experts * slot_cap, unit_c...  41.1 us
    all_to_all x1, starting transfers between devices, per_device(): lax.all_to_all(results, 'expert', split_axis=1, concat_axis=1, tiled=True)  21.8 us
    all_to_all x1, starting transfers between devices, per_device(): lax.all_to_all(payload, 'expert', split_axis=0, concat_axis=0, tiled=True)  19.7 us
    all_to_all x1, waiting for transfers between devices, per_device(): lax.all_to_all(lax.all_to_all(results, 'expert', split_axis=1, concat_axi...  12.6 us
    ppermute x3, starting transfers between devices, swapped(): return lax.ppermute(value, axis, pairs)  11.7 us
  transfers between devices with their start and end apart: 8, of which 7 were waited for; matrix products, arithmetic and copies ran while one was open for 1% of the time, Pallas kernels for 0%

profile of v10, /device:TPU:1, one launch (start us, length us, event | category | flops | bytes accessed | tf_op | source)
XLA Modules:
  0.0 377.1 jit_solution(746739764835895090)
XLA Ops:
  7.2 0.8 convert_reduce_fusion.4
  8.1 1.0 select_reduce_fusion
  9.1 0.7 compare_select_fusion
  10.1 0.7 iota_compare_fusion.2
  10.8 0.7 bitcast_convert_fusion.1
  11.5 1.0 fusion.31
  12.5 1.2 fusion.45
  13.8 0.2 fusion.26
  14.0 0.3 fusion.16
  14.7 1.2 gather_fusion
  15.9 0.7 reshape.179
  16.7 0.2 fusion.28
  16.9 2.1 pad_maximum_fusion
  19.0 19.7 %all-to-all-start = ((bf16[64,2,4224]{2,1,0:T(2,128)(2,1)}), bf16[64,2,4224]{2,1,0:T(2,128)(2,1)S(1)}, u32[]{:S(2)}, u32[]{:S(2)}) async-start(bf16[64,2,4224]{2,1,0:T(2,128)(2,1)} %pad_maximum_fusion), calls=%async_computation | async-start | bytes 2162688 | tf_op jit(solution)/shard_map/all_to_all | solution.py:133
  38.8 4.9 %collective-permute-start = (bf16[96,4096]{1,0:T(8,128)(2,1)S(1)}, bf16[96,4096]{1,0:T(8,128)(2,1)S(1)}, u32[]{:S(2)}, u32[]{:S(2)}) collective-permute-start(bf16[96,4096]{1,0:T(8,128)(2,1)S(1)} %bitcast.92), channel_id=1, source_target_pairs={{0,256},{8,264},{16,272},{24,280},{32,288},{40,296},{48,304},{56,3... | collective-permute-start | bytes 2359304 | tf_op jit(solution)/shard_map/ppermute | solution.py:14
  43.7 1.9 collective-permute-start.1
  45.6 4.9 %collective-permute-start.2 = (bf16[768,512]{1,0:T(8,128)(2,1)S(1)}, bf16[768,512]{1,0:T(8,128)(2,1)}, u32[]{:S(2)}, u32[]{:S(2)}) collective-permute-start(bf16[768,512]{1,0:T(8,128)(2,1)S(1)} %bitcast.90), channel_id=1, source_target_pairs={{0,256},{8,264},{16,272},{24,280},{32,288},{40,296},{48,304},{56,3... | collective-permute-start | bytes 2359304 | tf_op jit(solution)/shard_map/ppermute | solution.py:14
  50.5 14.3 %collective-permute-done = bf16[96,4096]{1,0:T(8,128)(2,1)S(1)} collective-permute-done((bf16[96,4096]{1,0:T(8,128)(2,1)S(1)}, bf16[96,4096]{1,0:T(8,128)(2,1)S(1)}, u32[]{:S(2)}, u32[]{:S(2)}) %collective-permute-start) | collective-permute-done | bytes 786464 | tf_op jit(solution)/shard_map/ppermute | solution.py:14
  64.8 23.2 %collective-permute-done.1 = bf16[96,4096]{1,0:T(8,128)(2,1)S(1)} collective-permute-done((bf16[96,4096]{1,0:T(8,128)(2,1)}, bf16[96,4096]{1,0:T(8,128)(2,1)S(1)}, u32[]{:S(2)}, u32[]{:S(2)}) %collective-permute-start.1) | collective-permute-done | bytes 786464 | tf_op jit(solution)/shard_map/ppermute | solution.py:14
  88.0 0.9 copy-done.6
  88.9 16.7 %collective-permute-done.2 = bf16[768,512]{1,0:T(8,128)(2,1)} collective-permute-done((bf16[768,512]{1,0:T(8,128)(2,1)S(1)}, bf16[768,512]{1,0:T(8,128)(2,1)}, u32[]{:S(2)}, u32[]{:S(2)}) %collective-permute-start.2) | collective-permute-done | bytes 786464 | tf_op jit(solution)/shard_map/ppermute | solution.py:14
  105.6 1.2 copy.72
  106.9 0.6 dynamic_slice.10
  108.1 0.6 fusion.43
  109.4 99.9 %all-gather.6.cloned.1.call-done = bf16[512,2,4224]{2,0,1:T(8,128)(2,1)} async-done(((bf16[64,2,4224]{2,0,1:T(8,128)(2,1)}), bf16[512,2,4224]{2,0,1:T(8,128)(2,1)}) %all-gather.6.cloned.1.call-update) | async-done | bytes 8650768 | tf_op jit(solution)/shard_map/all_gather | solution.py:135
  209.3 5.9 %fusion.2 = f32[8,64,2,96]{3,1,2,0:T(8,128)S(1)} fusion(bf16[8,64,2,4224]{3,1,0,2:T(8,128)(2,1)} %bitcast.101, bf16[96,4096]{1,0:T(8,128)(2,1)S(1)} %bitcast.93), kind=kOutput, calls=%fused_computation.4 | convolution fusion | flops 830472192 | bytes 9830400 | tf_op jit(solution)/shard_map/desf,hf->desh/dot_general | solution.py:153
  215.2 1.9 convert_reduce_fusion
  217.5 0.3 reduce-window.9
  218.5 5.9 %fusion.10 = bf16[8,64,2,96]{3,1,2,0:T(8,128)(2,1)S(1)} fusion(bf16[8,64,2,4224]{3,1,0,2:T(8,128)(2,1)} %bitcast.103, bf16[96,4096]{1,0:T(8,128)(2,1)S(1)} %bitcast.95, f32[8,64,2,96]{3,1,2,0:T(8,128)S(1)} %fusion.2, bf16[8,64,2]{1,2,0:T(2,128)(2,1)S(1)} %copy.77), kind=kOutput, calls=%fused_computation.9 | convolution fusion | flops 831160320 | bytes 10029056 | tf_op jit(solution)/shard_map/desf,hf->desh/dot_general | solution.py:156
  224.4 0.3 copy.78
  224.7 0.8 copy.79
  225.5 41.1 %all-gather.4.cloned.1.call-done = bf16[8,1024,96]{1,2,0:T(8,128)(2,1)} async-done(((bf16[1,1024,96]{1,2,0:T(8,128)(2,1)}), bf16[8,1024,96]{1,2,0:T(8,128)(2,1)}) %all-gather.4.cloned.1.call-update) | async-done | bytes 1572880 | tf_op jit(solution)/shard_map/all_gather | solution.py:160
  266.6 2.4 bitcast_convert_fusion
  269.1 0.4 reshape.185
  269.5 2.2 copy.80
  271.7 21.8 %all-to-all-start.1 = ((bf16[8,64,2,512]{3,2,0,1:T(2,128)(2,1)}), bf16[8,64,2,512]{3,2,0,1:T(2,128)(2,1)S(1)}, u32[]{:S(2)}, u32[]{:S(2)}) async-start(bf16[8,64,2,512]{3,2,0,1:T(2,128)(2,1)} %copy.80), calls=%async_computation.1 | async-start | bytes 2097152 | tf_op jit(solution)/shard_map/all_to_all | solution.py:170
  294.3 1.0 select_bitcast_fusion
  295.3 1.0 select_bitcast_fusion.2
  296.3 49.1 %all-to-all-done.1 = bf16[8,64,2,512]{3,2,0,1:T(2,128)(2,1)S(1)} async-done(((bf16[8,64,2,512]{3,2,0,1:T(2,128)(2,1)}), bf16[8,64,2,512]{3,2,0,1:T(2,128)(2,1)S(1)}, u32[]{:S(2)}, u32[]{:S(2)}) %all-to-all-start.1) | async-done | bytes 1048608 | tf_op jit(solution)/shard_map/all_to_all | solution.py:170
  345.4 1.8 copy.81
  347.2 3.6 all-to-all-start.2
  350.7 1.0 select_bitcast_fusion.1
  353.0 12.6 %all-to-all-done.2 = bf16[8,64,2,512]{3,2,1,0:T(2,128)(2,1)S(1)} async-done(((bf16[8,64,2,512]{3,2,1,0:T(2,128)(2,1)}), bf16[8,64,2,512]{3,2,1,0:T(2,128)(2,1)S(1)}, u32[]{:S(2)}, u32[]{:S(2)}) %all-to-all-start.2) | async-done | bytes 1048608 | tf_op jit(solution)/shard_map/all_to_all | solution.py:169
  365.6 1.1 copy.82
  366.7 0.4 copy.90
  367.1 0.9 gather_fusion.1
  368.0 0.4 fusion.17
  368.4 0.7 add_convert_fusion
  (64 shorter events, 2.2 us)
Async XLA Ops:
  7.2 6.9 %copy-start = (bf16[8,16,512]{2,1,0:T(8,128)(2,1)S(1)}, bf16[8,16,512]{2,1,0:T(8,128)(2,1)}, u32[]{:S(2)}) copy-start(bf16[8,16,512]{2,1,0:T(8,128)(2,1)} %param.18) | copy-start | bytes 393220
  7.2 7.1 %copy-start.9 = (bf16[8,4096]{1,0:T(8,128)(2,1)S(1)}, bf16[8,4096]{1,0:T(8,128)(2,1)}, u32[]{:S(2)}) copy-start(bf16[8,4096]{1,0:T(8,128)(2,1)} %param.15) | copy-start | bytes 196612
  7.2 7.4 %copy-start.10 = (f32[4096]{0:T(1024)S(1)}, f32[4096]{0:T(1024)}, u32[]{:S(2)}) copy-start(f32[4096]{0:T(1024)} %param.22) | copy-start | bytes 49156
  16.9 28.8 %copy-start.1 = (bf16[1,768,512]{2,1,0:T(8,128)(2,1)S(1)}, bf16[1,768,512]{2,1,0:T(8,128)(2,1)}, u32[]{:S(2)}) copy-start(bf16[1,768,512]{2,1,0:T(8,128)(2,1)} %param.29) | copy-start | bytes 2359300
  19.0 19.8 %copy-start.2 = (bf16[1,96,4096]{2,1,0:T(8,128)(2,1)S(1)}, bf16[1,96,4096]{2,1,0:T(8,128)(2,1)}, u32[]{:S(2)}) copy-start(bf16[1,96,4096]{2,1,0:T(8,128)(2,1)} %param.27) | copy-start | bytes 2359300
  19.0 86.6 %all-to-all-start = ((bf16[64,2,4224]{2,1,0:T(2,128)(2,1)}), bf16[64,2,4224]{2,1,0:T(2,128)(2,1)S(1)}, u32[]{:S(2)}, u32[]{:S(2)}) async-start(bf16[64,2,4224]{2,1,0:T(2,128)(2,1)} %pad_maximum_fusion), calls=%async_computation | async-start | bytes 2162688 | tf_op jit(solution)/shard_map/all_to_all | solution.py:133
  38.7 68.1 %copy-start.13 = (s32[64]{0:T(128)S(1)}, s32[64]{0:T(128)}, u32[]{:S(2)}) copy-start(s32[64]{0:T(128)} %param.26) | copy-start | bytes 772
  38.7 69.4 %copy-start.12 = (s32[64]{0:T(128)S(1)}, s32[64]{0:T(128)}, u32[]{:S(2)}) copy-start(s32[64]{0:T(128)} %param.25) | copy-start | bytes 772
  38.7 170.5 %all-gather.6.cloned.1.call-start = ((), (), s32[]{:S(2)}) async-start(), calls=%async_computation.4 | async-start | bytes 9732096 | tf_op jit(solution)/shard_map/all_gather | solution.py:135
  38.8 26.0 %collective-permute-start = (bf16[96,4096]{1,0:T(8,128)(2,1)S(1)}, bf16[96,4096]{1,0:T(8,128)(2,1)S(1)}, u32[]{:S(2)}, u32[]{:S(2)}) collective-permute-start(bf16[96,4096]{1,0:T(8,128)(2,1)S(1)} %bitcast.92), channel_id=1, source_target_pairs={{0,256},{8,264},{16,272},{24,280},{32,288},{40,296},{48,304},{56,3... | collective-permute-start | bytes 2359304 | tf_op jit(solution)/shard_map/ppermute | solution.py:14
  43.7 44.3 %collective-permute-start.1 = (bf16[96,4096]{1,0:T(8,128)(2,1)}, bf16[96,4096]{1,0:T(8,128)(2,1)S(1)}, u32[]{:S(2)}, u32[]{:S(2)}) collective-permute-start(bf16[96,4096]{1,0:T(8,128)(2,1)} %bitcast.94), channel_id=1, source_target_pairs={{0,256},{8,264},{16,272},{24,280},{32,288},{40,296},{48,304},{56,3... | collective-permute-start | bytes 2359304 | tf_op jit(solution)/shard_map/ppermute | solution.py:14
  45.6 59.9 %collective-permute-start.2 = (bf16[768,512]{1,0:T(8,128)(2,1)S(1)}, bf16[768,512]{1,0:T(8,128)(2,1)}, u32[]{:S(2)}, u32[]{:S(2)}) collective-permute-start(bf16[768,512]{1,0:T(8,128)(2,1)S(1)} %bitcast.90), channel_id=1, source_target_pairs={{0,256},{8,264},{16,272},{24,280},{32,288},{40,296},{48,304},{56,3... | collective-permute-start | bytes 2359304 | tf_op jit(solution)/shard_map/ppermute | solution.py:14
  64.8 23.2 %copy-start.7 = (bf16[96,4096]{1,0:T(8,128)(2,1)}, bf16[96,4096]{1,0:T(8,128)(2,1)S(1)}, u32[]{:S(2)}) copy-start(bf16[96,4096]{1,0:T(8,128)(2,1)S(1)} %collective-permute-done) | copy-start | bytes 2359300
  88.0 0.9 copy-start.6
  106.8 159.8 %all-gather.4.cloned.1.call-start = ((), (), s32[]{:S(2)}) async-start(), calls=%async_computation.3 | async-start | bytes 1769472 | tf_op jit(solution)/shard_map/all_gather | solution.py:160
  209.3 9.3 %copy-start.4 = (bf16[1,96,4096]{2,1,0:T(8,128)(2,1)S(1)}, bf16[1,96,4096]{2,1,0:T(8,128)(2,1)}, u32[]{:S(2)}) copy-start(bf16[1,96,4096]{2,1,0:T(8,128)(2,1)} %param.28) | copy-start | bytes 2359300
  271.7 23.6 %copy-start.3 = (bf16[1,96,4096]{2,1,0:T(8,128)(2,1)S(1)}, bf16[1,96,4096]{2,1,0:T(8,128)(2,1)}, u32[]{:S(2)}) copy-start(bf16[1,96,4096]{2,1,0:T(8,128)(2,1)} %param.27) | copy-start | bytes 2359300
  271.7 73.7 %all-to-all-start.1 = ((bf16[8,64,2,512]{3,2,0,1:T(2,128)(2,1)}), bf16[8,64,2,512]{3,2,0,1:T(2,128)(2,1)S(1)}, u32[]{:S(2)}, u32[]{:S(2)}) async-start(bf16[8,64,2,512]{3,2,0,1:T(2,128)(2,1)} %copy.80), calls=%async_computation.1 | async-start | bytes 2097152 | tf_op jit(solution)/shard_map/all_to_all | solution.py:170
  293.6 1.7 copy-start.8
  296.3 54.5 %copy-start.5 = (bf16[1,96,4096]{2,1,0:T(8,128)(2,1)S(1)}, bf16[1,96,4096]{2,1,0:T(8,128)(2,1)}, u32[]{:S(2)}) copy-start(bf16[1,96,4096]{2,1,0:T(8,128)(2,1)} %param.28) | copy-start | bytes 2359300
  347.2 18.4 %all-to-all-start.2 = ((bf16[8,64,2,512]{3,2,1,0:T(2,128)(2,1)}), bf16[8,64,2,512]{3,2,1,0:T(2,128)(2,1)S(1)}, u32[]{:S(2)}, u32[]{:S(2)}) async-start(bf16[8,64,2,512]{3,2,1,0:T(2,128)(2,1)} %copy.81), calls=%async_computation.2 | async-start | bytes 2097152 | tf_op jit(solution)/shard_map/all_to_all | solution.py:169
  367.1 0.9 copy-start.11
Sparse Core Ops, SparseCore 0:
  106.9 102.3 all-gather.5
  225.7 40.9 all-gather.3

commit v11 on v6

--- a/solution.py
+++ b/solution.py
@@ -156,8 +156,13 @@
     hidden = (jax.nn.silu(gate_val) * up_val).astype(jnp.bfloat16)
     hidden_kept = hidden * kept_mask[..., None].astype(jnp.bfloat16)
     unit_count = hidden_kept.shape[-1]
-    hidden_all = lax.all_gather(
-        hidden_kept.reshape(1, groups * experts * slot_cap, unit_count), "dp", axis=0, tiled=True
+    hidden_block = hidden_kept.reshape(1, groups * experts * slot_cap, unit_count)
+    hidden_all = lax.all_to_all(
+        jnp.broadcast_to(hidden_block, (groups,) + hidden_block.shape[1:]),
+        "dp",
+        split_axis=0,
+        concat_axis=0,
+        tiled=True,
     )
     feature_cols = own_weights[2].shape[1]
     down_split = own_weights[2].reshape(groups, unit_count, feature_cols)

time: 365 us -> 338 us (0.926)
  waiting for transfers between devices: 193 us -> 151 us
  blocking collectives: 72.5 us -> 95.1 us
  starting transfers between devices: 37.2 us -> 32.5 us
    all_gather x1 -> x0, waiting for transfers between devices: 41.1 us -> none  [per_device(): lax.all_gather(hidden_kept.reshape(1, groups * experts * slot_cap, unit_c...]
    all_to_all x0 -> x1, blocking collectives: none -> 22.6 us  [per_device(): lax.all_to_all(jnp.broadcast_to(hidden_block, (groups,) + hidden_block.sh...]
    all_to_all x1, starting transfers between devices: 21.7 us -> 17.2 us  [per_device(): lax.all_to_all(results, 'expert', split_axis=1, concat_axis=1, tiled=True)]
  transfers between devices with their start and end apart: 7 -> 6, of which waited for: 7 -> 6; matrix products, arithmetic and copies ran while one was open for 2% -> 2% of each run, Pallas kernels for 0% -> 0%
where the time goes in v11:
time: 338 us
  waiting for transfers between devices  151 us (45%)
  blocking collectives  95.1 us (28%)
  starting transfers between devices  32.5 us (10%)
  between operations  18.9 us (6%)
  matrix products  15.2 us (4%)
  local copies, waits for them, and re-layouts  13 us (4%)
  other arithmetic  12.3 us (4%)
    all_gather x1, waiting for transfers between devices, per_device(): column = lax.all_gather(arrived[None], 'dp', axis=0, tiled=True)  95.2 us
    all_to_all x1, blocking collectives, per_device(): lax.all_to_all(payload, 'expert', split_axis=0, concat_axis=0, tiled=True)  72.5 us
    ppermute x3, waiting for transfers between devices, swapped(): return lax.ppermute(value, axis, pairs)  45.1 us
    all_to_all x1, blocking collectives, per_device(): lax.all_to_all(jnp.broadcast_to(hidden_block, (groups,) + hidden_block.sh...  22.6 us
    all_to_all x1, starting transfers between devices, per_device(): lax.all_to_all(results, 'expert', split_axis=1, concat_axis=1, tiled=True)  17.2 us
    ppermute x3, starting transfers between devices, swapped(): return lax.ppermute(value, axis, pairs)  11.7 us
    all_to_all x1, waiting for transfers between devices, per_device(): lax.all_to_all(lax.all_to_all(results, 'expert', split_axis=1, concat_axi...  8.75 us
  transfers between devices with their start and end apart: 6, of which 6 were waited for; matrix products, arithmetic and copies ran while one was open for 2% of the time, Pallas kernels for 0%

profile of v11, /device:TPU:1, one launch (start us, length us, event | category | flops | bytes accessed | tf_op | source)
XLA Modules:
  0.0 337.7 jit_solution(5196514695957555498)
XLA Ops:
  7.3 0.8 convert_reduce_fusion.4
  8.1 1.0 select_reduce_fusion
  9.1 0.7 compare_select_fusion
  10.1 0.7 iota_compare_fusion.2
  10.8 0.7 bitcast_convert_fusion.1
  11.5 1.0 fusion.31
  12.5 1.2 fusion.45
  13.8 0.2 fusion.26
  14.0 0.3 fusion.16
  14.3 0.2 multiply_reduce_fusion
  14.7 1.2 gather_fusion
  15.9 0.7 reshape.178
  16.7 0.2 fusion.28
  16.9 1.1 pad_maximum_fusion
  17.9 72.5 %all_to_all.30 = bf16[64,2,4224]{2,1,0:T(2,128)(2,1)S(1)} all-to-all(bf16[64,2,4224]{2,1,0:T(2,128)(2,1)S(1)} %pad_maximum_fusion), channel_id=1, replica_groups=mesh['expert'=64,'dp'=8] {'expert'}, dimensions={0} | all-to-all | bytes 2162688 | tf_op jit(solution)/shard_map/all_to_all | solution.py:133
  90.5 1.2 copy.72
  91.7 0.6 dynamic_slice.10
  92.9 0.6 fusion.43
  94.2 95.2 %all-gather.3.cloned.1.call-done = bf16[512,2,4224]{2,0,1:T(8,128)(2,1)} async-done(((bf16[64,2,4224]{2,0,1:T(8,128)(2,1)}), bf16[512,2,4224]{2,0,1:T(8,128)(2,1)}) %all-gather.3.cloned.1.call-update) | async-done | bytes 8650768 | tf_op jit(solution)/shard_map/all_gather | solution.py:134
  189.4 1.9 convert_reduce_fusion
  191.6 0.3 reduce-window.9
  191.9 0.2 reshape.180
  192.2 5.9 %fusion.2 = f32[8,64,2,96]{3,1,2,0:T(8,128)S(1)} fusion(bf16[8,64,2,4224]{3,1,0,2:T(8,128)(2,1)} %bitcast.102, bf16[96,4096]{1,0:T(8,128)(2,1)S(1)} %bitcast.92), kind=kOutput, calls=%fused_computation.4 | convolution fusion | flops 830472192 | bytes 9830400 | tf_op jit(solution)/shard_map/desf,hf->desh/dot_general | solution.py:152
  198.6 5.9 %fusion.10 = bf16[8,64,2,96]{3,1,2,0:T(8,128)(2,1)S(1)} fusion(bf16[8,64,2,4224]{3,1,0,2:T(8,128)(2,1)} %bitcast.103, bf16[96,4096]{1,0:T(8,128)(2,1)S(1)} %bitcast.95, f32[8,64,2,96]{3,1,2,0:T(8,128)S(1)} %fusion.2, bf16[8,64,2]{1,2,0:T(2,128)(2,1)S(1)} %copy.77), kind=kOutput, calls=%fused_computation.9 | convolution fusion | flops 831160320 | bytes 10029056 | tf_op jit(solution)/shard_map/desf,hf->desh/dot_general | solution.py:155
  204.5 0.3 copy.78
  205.1 22.6 %all_to_all.31 = bf16[8,1024,96]{1,2,0:T(8,128)(2,1)S(1)} all-to-all(bf16[8,1024,96]{1,2,0:T(8,128)(2,1)S(1)} %broadcast_in_dim.105), channel_id=1, replica_groups=mesh['expert'=64,'dp'=8] {'dp'}, dimensions={0} | all-to-all | bytes 3145728 | tf_op jit(solution)/shard_map/all_to_all | solution.py:160
  227.7 1.0 bitcast_convert_fusion
  228.8 0.4 reshape.183
  229.2 2.2 copy.80
  231.4 17.2 %all-to-all-start.2 = ((bf16[8,64,2,512]{3,2,0,1:T(2,128)(2,1)}), bf16[8,64,2,512]{3,2,0,1:T(2,128)(2,1)S(1)}, u32[]{:S(2)}, u32[]{:S(2)}) async-start(bf16[8,64,2,512]{3,2,0,1:T(2,128)(2,1)} %copy.80), calls=%async_computation.2 | async-start | bytes 2097152 | tf_op jit(solution)/shard_map/all_to_all | solution.py:174
  248.6 4.9 %collective-permute-start.2 = (bf16[768,512]{1,0:T(8,128)(2,1)S(1)}, bf16[768,512]{1,0:T(8,128)(2,1)}, u32[]{:S(2)}, u32[]{:S(2)}) collective-permute-start(bf16[768,512]{1,0:T(8,128)(2,1)S(1)} %bitcast.91), channel_id=1, source_target_pairs={{0,256},{8,264},{16,272},{24,280},{32,288},{40,296},{48,304},{56,3... | collective-permute-start | bytes 2359304 | tf_op jit(solution)/shard_map/ppermute | solution.py:14
  253.5 1.9 collective-permute-start
  255.5 4.9 %collective-permute-start.1 = (bf16[96,4096]{1,0:T(8,128)(2,1)}, bf16[96,4096]{1,0:T(8,128)(2,1)}, u32[]{:S(2)}, u32[]{:S(2)}) collective-permute-start(bf16[96,4096]{1,0:T(8,128)(2,1)} %bitcast.94), channel_id=1, source_target_pairs={{0,256},{8,264},{16,272},{24,280},{32,288},{40,296},{48,304},{56,3... | collective-permute-start | bytes 2359304 | tf_op jit(solution)/shard_map/ppermute | solution.py:14
  261.1 13.7 %collective-permute-done.2 = bf16[768,512]{1,0:T(8,128)(2,1)} collective-permute-done((bf16[768,512]{1,0:T(8,128)(2,1)S(1)}, bf16[768,512]{1,0:T(8,128)(2,1)}, u32[]{:S(2)}, u32[]{:S(2)}) %collective-permute-start.2) | collective-permute-done | bytes 786464 | tf_op jit(solution)/shard_map/ppermute | solution.py:14
  274.7 1.0 select_bitcast_fusion
  275.7 22.2 %collective-permute-done = bf16[96,4096]{1,0:T(8,128)(2,1)} collective-permute-done((bf16[96,4096]{1,0:T(8,128)(2,1)S(1)}, bf16[96,4096]{1,0:T(8,128)(2,1)}, u32[]{:S(2)}, u32[]{:S(2)}) %collective-permute-start) | collective-permute-done | bytes 786464 | tf_op jit(solution)/shard_map/ppermute | solution.py:14
  297.9 1.0 select_bitcast_fusion.2
  298.8 1.6 all-to-all-done.2
  300.5 1.8 copy.81
  302.3 3.6 %all-to-all-start.3 = ((bf16[8,64,2,512]{3,2,1,0:T(2,128)(2,1)}), bf16[8,64,2,512]{3,2,1,0:T(2,128)(2,1)S(1)}, u32[]{:S(2)}, u32[]{:S(2)}) async-start(bf16[8,64,2,512]{3,2,1,0:T(2,128)(2,1)} %copy.81), calls=%async_computation.3 | async-start | bytes 2097152 | tf_op jit(solution)/shard_map/all_to_all | solution.py:173
  305.8 9.2 %collective-permute-done.1 = bf16[96,4096]{1,0:T(8,128)(2,1)} collective-permute-done((bf16[96,4096]{1,0:T(8,128)(2,1)}, bf16[96,4096]{1,0:T(8,128)(2,1)}, u32[]{:S(2)}, u32[]{:S(2)}) %collective-permute-start.1) | collective-permute-done | bytes 786464 | tf_op jit(solution)/shard_map/ppermute | solution.py:14
  315.1 1.0 select_bitcast_fusion.1
  317.4 8.7 %all-to-all-done.3 = bf16[8,64,2,512]{3,2,1,0:T(2,128)(2,1)S(1)} async-done(((bf16[8,64,2,512]{3,2,1,0:T(2,128)(2,1)}), bf16[8,64,2,512]{3,2,1,0:T(2,128)(2,1)S(1)}, u32[]{:S(2)}, u32[]{:S(2)}) %all-to-all-start.3) | async-done | bytes 1048608 | tf_op jit(solution)/shard_map/all_to_all | solution.py:173
  326.1 1.1 copy.82
  327.2 0.4 copy.90
  327.6 0.9 gather_fusion.1
  328.5 0.4 fusion.17
  329.0 0.7 add_convert_fusion
  (56 shorter events, 2.0 us)
Async XLA Ops:
  7.2 6.9 %copy-start = (bf16[8,16,512]{2,1,0:T(8,128)(2,1)S(1)}, bf16[8,16,512]{2,1,0:T(8,128)(2,1)}, u32[]{:S(2)}) copy-start(bf16[8,16,512]{2,1,0:T(8,128)(2,1)} %param.18) | copy-start | bytes 393220
  7.2 7.1 %copy-start.6 = (bf16[8,4096]{1,0:T(8,128)(2,1)S(1)}, bf16[8,4096]{1,0:T(8,128)(2,1)}, u32[]{:S(2)}) copy-start(bf16[8,4096]{1,0:T(8,128)(2,1)} %param.15) | copy-start | bytes 196612
  7.2 7.4 %copy-start.7 = (f32[4096]{0:T(1024)S(1)}, f32[4096]{0:T(1024)}, u32[]{:S(2)}) copy-start(f32[4096]{0:T(1024)} %param.22) | copy-start | bytes 49156
  7.2 182.2 %all-gather.3.cloned.1.call-start = ((), (), s32[]{:S(2)}) async-start(), calls=%async_computation.4 | async-start | bytes 9732096 | tf_op jit(solution)/shard_map/all_gather | solution.py:134
  90.5 1.2 copy-start.10
  90.5 2.5 copy-start.9
  90.5 101.8 %copy-start.2 = (bf16[1,96,4096]{2,1,0:T(8,128)(2,1)S(1)}, bf16[1,96,4096]{2,1,0:T(8,128)(2,1)}, u32[]{:S(2)}) copy-start(bf16[1,96,4096]{2,1,0:T(8,128)(2,1)} %param.27) | copy-start | bytes 2359300
  192.2 6.4 %copy-start.4 = (bf16[1,96,4096]{2,1,0:T(8,128)(2,1)S(1)}, bf16[1,96,4096]{2,1,0:T(8,128)(2,1)}, u32[]{:S(2)}) copy-start(bf16[1,96,4096]{2,1,0:T(8,128)(2,1)} %param.28) | copy-start | bytes 2359300
  204.9 22.8 %copy-start.1 = (bf16[1,768,512]{2,1,0:T(8,128)(2,1)S(1)}, bf16[1,768,512]{2,1,0:T(8,128)(2,1)}, u32[]{:S(2)}) copy-start(bf16[1,768,512]{2,1,0:T(8,128)(2,1)} %param.29) | copy-start | bytes 2359300
  229.2 24.3 %copy-start.3 = (bf16[1,96,4096]{2,1,0:T(8,128)(2,1)S(1)}, bf16[1,96,4096]{2,1,0:T(8,128)(2,1)}, u32[]{:S(2)}) copy-start(bf16[1,96,4096]{2,1,0:T(8,128)(2,1)} %param.27) | copy-start | bytes 2359300
  231.4 69.1 %all-to-all-start.2 = ((bf16[8,64,2,512]{3,2,0,1:T(2,128)(2,1)}), bf16[8,64,2,512]{3,2,0,1:T(2,128)(2,1)S(1)}, u32[]{:S(2)}, u32[]{:S(2)}) async-start(bf16[8,64,2,512]{3,2,0,1:T(2,128)(2,1)} %copy.80), calls=%async_computation.2 | async-start | bytes 2097152 | tf_op jit(solution)/shard_map/all_to_all | solution.py:174
  248.6 26.1 %collective-permute-start.2 = (bf16[768,512]{1,0:T(8,128)(2,1)S(1)}, bf16[768,512]{1,0:T(8,128)(2,1)}, u32[]{:S(2)}, u32[]{:S(2)}) collective-permute-start(bf16[768,512]{1,0:T(8,128)(2,1)S(1)} %bitcast.91), channel_id=1, source_target_pairs={{0,256},{8,264},{16,272},{24,280},{32,288},{40,296},{48,304},{56,3... | collective-permute-start | bytes 2359304 | tf_op jit(solution)/shard_map/ppermute | solution.py:14
  253.5 44.3 %collective-permute-start = (bf16[96,4096]{1,0:T(8,128)(2,1)S(1)}, bf16[96,4096]{1,0:T(8,128)(2,1)}, u32[]{:S(2)}, u32[]{:S(2)}) collective-permute-start(bf16[96,4096]{1,0:T(8,128)(2,1)S(1)} %bitcast.93), channel_id=1, source_target_pairs={{0,256},{8,264},{16,272},{24,280},{32,288},{40,296},{48,304},{56,3... | collective-permute-start | bytes 2359304 | tf_op jit(solution)/shard_map/ppermute | solution.py:14
  255.5 59.6 %collective-permute-start.1 = (bf16[96,4096]{1,0:T(8,128)(2,1)}, bf16[96,4096]{1,0:T(8,128)(2,1)}, u32[]{:S(2)}, u32[]{:S(2)}) collective-permute-start(bf16[96,4096]{1,0:T(8,128)(2,1)} %bitcast.94), channel_id=1, source_target_pairs={{0,256},{8,264},{16,272},{24,280},{32,288},{40,296},{48,304},{56,3... | collective-permute-start | bytes 2359304 | tf_op jit(solution)/shard_map/ppermute | solution.py:14
  298.8 16.2 %copy-start.5 = (bf16[1,96,4096]{2,1,0:T(8,128)(2,1)S(1)}, bf16[1,96,4096]{2,1,0:T(8,128)(2,1)}, u32[]{:S(2)}) copy-start(bf16[1,96,4096]{2,1,0:T(8,128)(2,1)} %param.28) | copy-start | bytes 2359300
  302.3 23.8 %all-to-all-start.3 = ((bf16[8,64,2,512]{3,2,1,0:T(2,128)(2,1)}), bf16[8,64,2,512]{3,2,1,0:T(2,128)(2,1)S(1)}, u32[]{:S(2)}, u32[]{:S(2)}) async-start(bf16[8,64,2,512]{3,2,1,0:T(2,128)(2,1)} %copy.81), calls=%async_computation.3 | async-start | bytes 2097152 | tf_op jit(solution)/shard_map/all_to_all | solution.py:173
  327.6 0.9 copy-start.8
Sparse Core Ops, SparseCore 0:
  91.8 97.5 all-gather.2

commit v12 on v11

--- a/solution.py
+++ b/solution.py
@@ -131,7 +131,13 @@
     ).astype(jnp.bfloat16)
     payload = jnp.concatenate([outgoing, side], axis=-1)
     arrived = lax.all_to_all(payload, "expert", split_axis=0, concat_axis=0, tiled=True)
-    column = lax.all_gather(arrived[None], "dp", axis=0, tiled=True)
+    column = lax.all_to_all(
+        jnp.broadcast_to(arrived[None], (groups,) + arrived.shape),
+        "dp",
+        split_axis=0,
+        concat_axis=0,
+        tiled=True,
+    )
     marks = column[:, :, :, width].astype(jnp.float32)
     partner_total = jnp.sum(column[:, :, :, width + 1].astype(jnp.float32))
     occupied_flat = jnp.transpose(marks, (1, 0, 2)).reshape(-1)

time: 338 us -> 329 us (0.973)
  between operations: 18.9 us -> 5.54 us
  local copies, waits for them, and re-layouts: 13 us -> 19.7 us
    all_gather x1 -> x0, waiting for transfers between devices: 95.2 us -> none  [per_device(): column = lax.all_gather(arrived[None], 'dp', axis=0, tiled=True)]
    all_to_all x0 -> x1, waiting for transfers between devices: none -> 94.1 us  [per_device(): lax.all_to_all(jnp.broadcast_to(arrived[None], (groups,) + arrived.shape)...]
    all_to_all x1, starting transfers between devices: 17.2 us -> 11.6 us  [per_device(): lax.all_to_all(results, 'expert', split_axis=1, concat_axis=1, tiled=True)]
    all_to_all x0 -> x1, starting transfers between devices: none -> 5.1 us  [per_device(): lax.all_to_all(jnp.broadcast_to(arrived[None], (groups,) + arrived.shape)...]
    broadcast_in_dim x0 -> x1, local copies, waits for them, and re-layouts: none -> 4.41 us  [per_device(): jnp.broadcast_to(arrived[None], (groups,) + arrived.shape)]
where the time goes in v12:
time: 329 us; the launch traced here: 328 us
  waiting for transfers between devices  148 us (45%)
  blocking collectives  95.9 us (29%)
  starting transfers between devices  32 us (10%)
  local copies, waits for them, and re-layouts  19.7 us (6%)
  matrix products  15.2 us (5%)
  other arithmetic  11.3 us (3%)
  between operations  5.54 us (2%)
    all_to_all x1, waiting for transfers between devices, per_device(): lax.all_to_all(jnp.broadcast_to(arrived[None], (groups,) + arrived.shape)...  94.1 us
    all_to_all x1, blocking collectives, per_device(): lax.all_to_all(payload, 'expert', split_axis=0, concat_axis=0, tiled=True)  72.5 us
    ppermute x3, waiting for transfers between devices, swapped(): return lax.ppermute(value, axis, pairs)  45 us
    all_to_all x1, blocking collectives, per_device(): lax.all_to_all(jnp.broadcast_to(hidden_block, (groups,) + hidden_block.sh...  23.4 us
    ppermute x3, starting transfers between devices, swapped(): return lax.ppermute(value, axis, pairs)  11.7 us
    all_to_all x1, starting transfers between devices, per_device(): lax.all_to_all(results, 'expert', split_axis=1, concat_axis=1, tiled=True)  11.6 us
    all_to_all x1, waiting for transfers between devices, per_device(): lax.all_to_all(lax.all_to_all(results, 'expert', split_axis=1, concat_axi...  7.38 us
  transfers between devices with their start and end apart: 6, of which 6 were waited for; matrix products, arithmetic and copies ran while one was open for 2% of the time, Pallas kernels for 0%

profile of v12, /device:TPU:1, one launch (start us, length us, event | category | flops | bytes accessed | tf_op | source)
XLA Modules:
  0.0 327.7 jit_solution(11479092636574904556)
XLA Ops:
  0.7 0.8 iota_compare_fusion.2
  1.5 1.0 fusion.22
  2.5 1.2 fusion.38
  3.7 0.2 fusion.16
  4.0 0.7 bitcast_convert_fusion.1
  4.7 0.3 fusion.5
  5.3 0.3 select_reduce_fusion
  5.9 1.2 gather_fusion
  7.1 0.7 reshape.179
  8.1 0.2 fusion.19
  8.3 1.1 pad_maximum_fusion
  9.4 72.5 %all_to_all.35 = bf16[64,2,4224]{2,1,0:T(2,128)(2,1)S(1)} all-to-all(bf16[64,2,4224]{2,1,0:T(2,128)(2,1)S(1)} %pad_maximum_fusion), channel_id=1, replica_groups=mesh['expert'=64,'dp'=8] {'expert'}, dimensions={0} | all-to-all | bytes 2162688 | tf_op jit(solution)/shard_map/all_to_all | solution.py:133
  82.0 4.4 %broadcast_in_dim.106 = bf16[8,64,2,4224]{3,1,2,0:T(8,128)(2,1)} broadcast(bf16[64,2,4224]{2,0,1:T(8,128)(2,1)S(1)} %copy.71), dimensions={1,2,3} | broadcast | bytes 9732096 | tf_op jit(solution)/shard_map/broadcast_in_dim | solution.py:135
  86.4 5.1 %all-to-all-start.1 = ((bf16[8,64,2,4224]{3,1,2,0:T(8,128)(2,1)}), bf16[8,64,2,4224]{3,1,2,0:T(8,128)(2,1)}, u32[]{:S(2)}, u32[]{:S(2)}) async-start(bf16[8,64,2,4224]{3,1,2,0:T(8,128)(2,1)} %broadcast_in_dim.106), calls=%async_computation.1 | async-start | bytes 17301504 | tf_op jit(solution)/shard_map/all_to_all | solution.py:134
  91.6 0.6 dynamic_slice.10
  92.8 0.6 fusion.36
  94.1 94.1 %all-to-all-done.1 = bf16[8,64,2,4224]{3,1,2,0:T(8,128)(2,1)} async-done(((bf16[8,64,2,4224]{3,1,2,0:T(8,128)(2,1)}), bf16[8,64,2,4224]{3,1,2,0:T(8,128)(2,1)}, u32[]{:S(2)}, u32[]{:S(2)}) %all-to-all-start.1) | async-done | bytes 8650784 | tf_op jit(solution)/shard_map/all_to_all | solution.py:134
  188.1 1.0 slice_convert_fusion
  189.1 3.1 copy.85
  192.4 0.3 reduce-window.9
  192.7 0.2 reshape.181
  193.7 5.9 %fusion.8 = f32[8,64,2,96]{3,1,2,0:T(8,128)S(1)} fusion(bf16[8,64,2,4224]{3,1,2,0:T(8,128)(2,1)} %all-to-all-done.1, bf16[96,4096]{1,0:T(8,128)(2,1)S(1)} %bitcast.109), kind=kOutput, calls=%fused_computation.16 | convolution fusion | flops 830472192 | bytes 9830400 | tf_op jit(solution)/shard_map/desf,hf->desh/dot_general | solution.py:158
  199.6 5.9 %fusion.1 = bf16[8,64,2,96]{3,1,2,0:T(8,128)(2,1)S(1)} fusion(bf16[8,64,2,4224]{3,1,2,0:T(8,128)(2,1)} %all-to-all-done.1, bf16[96,4096]{1,0:T(8,128)(2,1)S(1)} %bitcast.106, f32[8,64,2,96]{3,1,2,0:T(8,128)S(1)} %fusion.8, bf16[8,64,2]{1,2,0:T(2,128)(2,1)S(1)} %copy.75), kind=kOutput, calls=%fused_computation.5 | convolution fusion | flops 831160320 | bytes 10029056 | tf_op jit(solution)/shard_map/desf,hf->desh/dot_general | solution.py:161
  205.5 0.3 copy.76
  206.1 23.4 %all_to_all.36 = bf16[8,1024,96]{1,2,0:T(8,128)(2,1)S(1)} all-to-all(bf16[8,1024,96]{1,2,0:T(8,128)(2,1)S(1)} %broadcast_in_dim.108), channel_id=1, replica_groups=mesh['expert'=64,'dp'=8] {'dp'}, dimensions={0} | all-to-all | bytes 3145728 | tf_op jit(solution)/shard_map/all_to_all | solution.py:166
  229.6 1.0 bitcast_convert_fusion
  230.6 0.4 reshape.184
  231.0 2.2 copy.78
  233.3 11.6 %all-to-all-start.3 = ((bf16[8,64,2,512]{3,2,0,1:T(2,128)(2,1)}), bf16[8,64,2,512]{3,2,0,1:T(2,128)(2,1)S(1)}, u32[]{:S(2)}, u32[]{:S(2)}) async-start(bf16[8,64,2,512]{3,2,0,1:T(2,128)(2,1)} %copy.78), calls=%async_computation.3 | async-start | bytes 2097152 | tf_op jit(solution)/shard_map/all_to_all | solution.py:180
  244.9 4.9 %collective-permute-start.2 = (bf16[768,512]{1,0:T(8,128)(2,1)S(1)}, bf16[768,512]{1,0:T(8,128)(2,1)}, u32[]{:S(2)}, u32[]{:S(2)}) collective-permute-start(bf16[768,512]{1,0:T(8,128)(2,1)S(1)} %bitcast.105), channel_id=1, source_target_pairs={{0,256},{8,264},{16,272},{24,280},{32,288},{40,296},{48,304},{56,3... | collective-permute-start | bytes 2359304 | tf_op jit(solution)/shard_map/ppermute | solution.py:14
  249.8 1.9 collective-permute-start.1
  251.7 4.9 %collective-permute-start = (bf16[96,4096]{1,0:T(8,128)(2,1)}, bf16[96,4096]{1,0:T(8,128)(2,1)}, u32[]{:S(2)}, u32[]{:S(2)}) collective-permute-start(bf16[96,4096]{1,0:T(8,128)(2,1)} %bitcast.108), channel_id=1, source_target_pairs={{0,256},{8,264},{16,272},{24,280},{32,288},{40,296},{48,304},{56,3... | collective-permute-start | bytes 2359304 | tf_op jit(solution)/shard_map/ppermute | solution.py:14
  257.3 13.7 %collective-permute-done.2 = bf16[768,512]{1,0:T(8,128)(2,1)} collective-permute-done((bf16[768,512]{1,0:T(8,128)(2,1)S(1)}, bf16[768,512]{1,0:T(8,128)(2,1)}, u32[]{:S(2)}, u32[]{:S(2)}) %collective-permute-start.2) | collective-permute-done | bytes 786464 | tf_op jit(solution)/shard_map/ppermute | solution.py:14
  271.0 1.0 select_bitcast_fusion
  272.0 22.2 %collective-permute-done.1 = bf16[96,4096]{1,0:T(8,128)(2,1)} collective-permute-done((bf16[96,4096]{1,0:T(8,128)(2,1)S(1)}, bf16[96,4096]{1,0:T(8,128)(2,1)}, u32[]{:S(2)}, u32[]{:S(2)}) %collective-permute-start.1) | collective-permute-done | bytes 786464 | tf_op jit(solution)/shard_map/ppermute | solution.py:14
  294.1 1.0 select_bitcast_fusion.1
  295.1 1.6 all-to-all-done.3
  296.7 1.9 copy.79
  298.6 3.6 %all-to-all-start.4 = ((bf16[8,64,2,512]{3,2,1,0:T(2,128)(2,1)}), bf16[8,64,2,512]{3,2,1,0:T(2,128)(2,1)S(1)}, u32[]{:S(2)}, u32[]{:S(2)}) async-start(bf16[8,64,2,512]{3,2,1,0:T(2,128)(2,1)} %copy.79), calls=%async_computation.4 | async-start | bytes 2097152 | tf_op jit(solution)/shard_map/all_to_all | solution.py:179
  302.2 9.2 %collective-permute-done = bf16[96,4096]{1,0:T(8,128)(2,1)} collective-permute-done((bf16[96,4096]{1,0:T(8,128)(2,1)}, bf16[96,4096]{1,0:T(8,128)(2,1)}, u32[]{:S(2)}, u32[]{:S(2)}) %collective-permute-start) | collective-permute-done | bytes 786464 | tf_op jit(solution)/shard_map/ppermute | solution.py:14
  311.3 1.0 select_bitcast_fusion.2
  312.3 1.9 fusion.17
  315.6 7.4 %all-to-all-done.4 = bf16[8,64,2,512]{3,2,1,0:T(2,128)(2,1)S(1)} async-done(((bf16[8,64,2,512]{3,2,1,0:T(2,128)(2,1)}), bf16[8,64,2,512]{3,2,1,0:T(2,128)(2,1)S(1)}, u32[]{:S(2)}, u32[]{:S(2)}) %all-to-all-start.4) | async-done | bytes 1048608 | tf_op jit(solution)/shard_map/all_to_all | solution.py:179
  323.0 1.1 copy.80
  324.1 0.4 copy.89
  324.5 0.9 gather_fusion.1
  325.4 0.4 fusion.6
  325.8 0.7 add_convert_fusion
  (60 shorter events, 2.4 us)
Async XLA Ops:
  0.6 4.1 %copy-start = (bf16[8,16,512]{2,1,0:T(8,128)(2,1)S(1)}, bf16[8,16,512]{2,1,0:T(8,128)(2,1)}, u32[]{:S(2)}) copy-start(bf16[8,16,512]{2,1,0:T(8,128)(2,1)} %param.18) | copy-start | bytes 393220
  0.6 4.3 %copy-start.6 = (bf16[8,4096]{1,0:T(8,128)(2,1)S(1)}, bf16[8,4096]{1,0:T(8,128)(2,1)}, u32[]{:S(2)}) copy-start(bf16[8,4096]{1,0:T(8,128)(2,1)} %param.15) | copy-start | bytes 196612
  0.7 4.5 %copy-start.7 = (s32[8,8]{1,0:T(8,128)S(1)}, s32[8,8]{1,0:T(8,128)}, u32[]{:S(2)}) copy-start(s32[8,8]{1,0:T(8,128)} %param.23) | copy-start | bytes 772
  0.7 5.1 %copy-start.8 = (f32[4096]{0:T(1024)S(1)}, f32[4096]{0:T(1024)}, u32[]{:S(2)}) copy-start(f32[4096]{0:T(1024)} %param.22) | copy-start | bytes 49156
  86.4 5.1 %copy-start.11 = (s32[64]{0:T(128)S(1)}, s32[64]{0:T(128)}, u32[]{:S(2)}) copy-start(s32[64]{0:T(128)} %param.26) | copy-start | bytes 772
  86.4 6.4 %copy-start.10 = (s32[64]{0:T(128)S(1)}, s32[64]{0:T(128)}, u32[]{:S(2)}) copy-start(s32[64]{0:T(128)} %param.25) | copy-start | bytes 772
  86.4 101.7 %all-to-all-start.1 = ((bf16[8,64,2,4224]{3,1,2,0:T(8,128)(2,1)}), bf16[8,64,2,4224]{3,1,2,0:T(8,128)(2,1)}, u32[]{:S(2)}, u32[]{:S(2)}) async-start(bf16[8,64,2,4224]{3,1,2,0:T(8,128)(2,1)} %broadcast_in_dim.106), calls=%async_computation.1 | async-start | bytes 17301504 | tf_op jit(solution)/shard_map/all_to_all | solution.py:134
  91.5 102.2 %copy-start.4 = (bf16[1,96,4096]{2,1,0:T(8,128)(2,1)S(1)}, bf16[1,96,4096]{2,1,0:T(8,128)(2,1)}, u32[]{:S(2)}) copy-start(bf16[1,96,4096]{2,1,0:T(8,128)(2,1)} %param.27) | copy-start | bytes 2359300
  193.7 5.9 %copy-start.2 = (bf16[1,96,4096]{2,1,0:T(8,128)(2,1)S(1)}, bf16[1,96,4096]{2,1,0:T(8,128)(2,1)}, u32[]{:S(2)}) copy-start(bf16[1,96,4096]{2,1,0:T(8,128)(2,1)} %param.28) | copy-start | bytes 2359300
  205.9 23.6 %copy-start.1 = (bf16[1,768,512]{2,1,0:T(8,128)(2,1)S(1)}, bf16[1,768,512]{2,1,0:T(8,128)(2,1)}, u32[]{:S(2)}) copy-start(bf16[1,768,512]{2,1,0:T(8,128)(2,1)} %param.29) | copy-start | bytes 2359300
  231.0 18.8 %copy-start.3 = (bf16[1,96,4096]{2,1,0:T(8,128)(2,1)S(1)}, bf16[1,96,4096]{2,1,0:T(8,128)(2,1)}, u32[]{:S(2)}) copy-start(bf16[1,96,4096]{2,1,0:T(8,128)(2,1)} %param.28) | copy-start | bytes 2359300
  233.3 63.5 %all-to-all-start.3 = ((bf16[8,64,2,512]{3,2,0,1:T(2,128)(2,1)}), bf16[8,64,2,512]{3,2,0,1:T(2,128)(2,1)S(1)}, u32[]{:S(2)}, u32[]{:S(2)}) async-start(bf16[8,64,2,512]{3,2,0,1:T(2,128)(2,1)} %copy.78), calls=%async_computation.3 | async-start | bytes 2097152 | tf_op jit(solution)/shard_map/all_to_all | solution.py:180
  244.9 26.1 %collective-permute-start.2 = (bf16[768,512]{1,0:T(8,128)(2,1)S(1)}, bf16[768,512]{1,0:T(8,128)(2,1)}, u32[]{:S(2)}, u32[]{:S(2)}) collective-permute-start(bf16[768,512]{1,0:T(8,128)(2,1)S(1)} %bitcast.105), channel_id=1, source_target_pairs={{0,256},{8,264},{16,272},{24,280},{32,288},{40,296},{48,304},{56,3... | collective-permute-start | bytes 2359304 | tf_op jit(solution)/shard_map/ppermute | solution.py:14
  249.8 44.3 %collective-permute-start.1 = (bf16[96,4096]{1,0:T(8,128)(2,1)S(1)}, bf16[96,4096]{1,0:T(8,128)(2,1)}, u32[]{:S(2)}, u32[]{:S(2)}) collective-permute-start(bf16[96,4096]{1,0:T(8,128)(2,1)S(1)} %bitcast.107), channel_id=1, source_target_pairs={{0,256},{8,264},{16,272},{24,280},{32,288},{40,296},{48,304},{56,3... | collective-permute-start | bytes 2359304 | tf_op jit(solution)/shard_map/ppermute | solution.py:14
  251.7 59.6 %collective-permute-start = (bf16[96,4096]{1,0:T(8,128)(2,1)}, bf16[96,4096]{1,0:T(8,128)(2,1)}, u32[]{:S(2)}, u32[]{:S(2)}) collective-permute-start(bf16[96,4096]{1,0:T(8,128)(2,1)} %bitcast.108), channel_id=1, source_target_pairs={{0,256},{8,264},{16,272},{24,280},{32,288},{40,296},{48,304},{56,3... | collective-permute-start | bytes 2359304 | tf_op jit(solution)/shard_map/ppermute | solution.py:14
  295.1 16.2 %copy-start.5 = (bf16[1,96,4096]{2,1,0:T(8,128)(2,1)S(1)}, bf16[1,96,4096]{2,1,0:T(8,128)(2,1)}, u32[]{:S(2)}) copy-start(bf16[1,96,4096]{2,1,0:T(8,128)(2,1)} %param.27) | copy-start | bytes 2359300
  298.6 24.4 %all-to-all-start.4 = ((bf16[8,64,2,512]{3,2,1,0:T(2,128)(2,1)}), bf16[8,64,2,512]{3,2,1,0:T(2,128)(2,1)S(1)}, u32[]{:S(2)}, u32[]{:S(2)}) async-start(bf16[8,64,2,512]{3,2,1,0:T(2,128)(2,1)} %copy.79), calls=%async_computation.4 | async-start | bytes 2097152 | tf_op jit(solution)/shard_map/all_to_all | solution.py:179
  324.5 0.9 copy-start.9

commit v13 on v12

--- a/solution.py
+++ b/solution.py
@@ -78,7 +78,14 @@
         widening_projection_matrix[0],
         output_projection_matrix[0],
     )
-    partner = swapped(own_weights, "expert", far_bit)
+    packed = jnp.concatenate([w.reshape(-1) for w in own_weights])
+    arrived_weights = swapped(packed, "expert", far_bit)
+    sizes = [w.size for w in own_weights]
+    partner = (
+        arrived_weights[: sizes[0]].reshape(own_weights[0].shape),
+        arrived_weights[sizes[0] : sizes[0] + sizes[1]].reshape(own_weights[1].shape),
+        arrived_weights[sizes[0] + sizes[1] :].reshape(own_weights[2].shape),
+    )
     take_other = swap_indicator[my_index] == 1
     retained_specialist = jnp.where(take_other, (my_index + half_axis) % experts, my_index)
 

time: 329 us -> 352 us (1.070)
  blocking collectives: 95.9 us -> 0 us
  waiting for transfers between devices: 148 us -> 223 us
  local copies, waits for them, and re-layouts: 19.7 us -> 35.9 us
  starting transfers between devices: 32 us -> 47.6 us
  other arithmetic: 11.3 us -> 20.5 us
    all_to_all x2 -> x0, blocking collectives: 95.9 us -> none  [the longest x1 72.5 us: per_device(): lax.all_to_all(payload, 'expert', split_axis=0, concat_axis=0, tiled=True)]
    all_to_all x0 -> x2, waiting for transfers between devices: none -> 89.6 us  [the longest x1 48.7 us: per_device(): lax.all_to_all(payload, 'expert', split_axis=0, concat_axis=0, tiled=True)]
    ppermute x3 -> x1, waiting for transfers between devices: 45 us -> 0.01 us  [swapped(): return lax.ppermute(value, axis, pairs)]
    all_to_all x1, waiting for transfers between devices: 1.63 us -> 41.2 us  [per_device(): lax.all_to_all(results, 'expert', split_axis=1, concat_axis=1, tiled=True)]
    all_to_all x0 -> x2, starting transfers between devices: none -> 24 us  [the longest x1 19.7 us: per_device(): lax.all_to_all(payload, 'expert', split_axis=0, concat_axis=0, tiled=True)]
    all_to_all x1, waiting for transfers between devices: 94.1 us -> 81.8 us  [per_device(): lax.all_to_all(jnp.broadcast_to(arrived[None], (groups,) + arrived.shape)...]
    slice x0 -> x4, local copies, waits for them, and re-layouts: none -> 9.63 us  [the longest x2 5.31 us: per_device(): arrived_weights[sizes[0] + sizes[1]:].reshape(own_weights[2].shape)]
    concatenate x0 -> x1, other arithmetic: none -> 8.89 us  [per_device(): packed = jnp.concatenate([w.reshape(-1) for w in own_weights])]
  transfers between devices with their start and end apart: 6 -> 6, of which waited for: 6 -> 5; matrix products, arithmetic and copies ran while one was open for 2% -> 16% of each run, Pallas kernels for 0% -> 0%
where the time goes in v13:
time: 352 us; the launch traced here: 350 us
  waiting for transfers between devices  223 us (63%)
  starting transfers between devices  47.6 us (14%)
  local copies, waits for them, and re-layouts  35.9 us (10%)
  other arithmetic  20.5 us (6%)
  matrix products  17.5 us (5%)
  between operations  5.56 us (2%)
    all_to_all x1, waiting for transfers between devices, per_device(): lax.all_to_all(jnp.broadcast_to(arrived[None], (groups,) + arrived.shape)...  81.8 us
    all_to_all x1, waiting for transfers between devices, per_device(): lax.all_to_all(payload, 'expert', split_axis=0, concat_axis=0, tiled=True)  48.7 us
    all_to_all x1, waiting for transfers between devices, per_device(): lax.all_to_all(results, 'expert', split_axis=1, concat_axis=1, tiled=True)  41.2 us
    all_to_all x1, waiting for transfers between devices, per_device(): lax.all_to_all(jnp.broadcast_to(hidden_block, (groups,) + hidden_block.sh...  40.9 us
    all_to_all x1, starting transfers between devices, per_device(): lax.all_to_all(payload, 'expert', split_axis=0, concat_axis=0, tiled=True)  19.7 us
    all_to_all x1, starting transfers between devices, per_device(): lax.all_to_all(results, 'expert', split_axis=1, concat_axis=1, tiled=True)  11.1 us
    all_to_all x1, waiting for transfers between devices, per_device(): lax.all_to_all(lax.all_to_all(results, 'expert', split_axis=1, concat_axi...  10.1 us
    concatenate x1, other arithmetic, per_device(): packed = jnp.concatenate([w.reshape(-1) for w in own_weights])  8.89 us
  transfers between devices with their start and end apart: 6, of which 5 were waited for; matrix products, arithmetic and copies ran while one was open for 16% of the time, Pallas kernels for 0%

profile of v13, /device:TPU:1, one launch (start us, length us, event | category | flops | bytes accessed | tf_op | source)
XLA Modules:
  0.0 349.9 jit_solution(3361227535321708672)
XLA Ops:
  0.7 0.8 iota_compare_fusion.2
  1.5 1.0 fusion.23
  2.5 1.2 fusion.40
  4.0 0.7 bitcast_convert_fusion.1
  5.3 0.3 select_reduce_fusion
  5.9 1.2 gather_fusion
  7.1 0.7 reshape.206
  8.3 2.1 pad_maximum_fusion.1
  10.4 19.7 %all-to-all-start = ((bf16[64,2,4224]{2,1,0:T(2,128)(2,1)}), bf16[64,2,4224]{2,1,0:T(2,128)(2,1)S(1)}, u32[]{:S(2)}, u32[]{:S(2)}) async-start(bf16[64,2,4224]{2,1,0:T(2,128)(2,1)} %pad_maximum_fusion.1), calls=%async_computation | async-start | bytes 2162688 | tf_op jit(solution)/shard_map/all_to_all | solution.py:140
  30.1 2.2 copy.90
  32.3 1.0 copy.91
  33.4 1.2 copy.92
  34.6 48.7 %all-to-all-done = bf16[64,2,4224]{2,1,0:T(2,128)(2,1)S(1)} async-done(((bf16[64,2,4224]{2,1,0:T(2,128)(2,1)}), bf16[64,2,4224]{2,1,0:T(2,128)(2,1)S(1)}, u32[]{:S(2)}, u32[]{:S(2)}) %all-to-all-start) | async-done | bytes 1081376 | tf_op jit(solution)/shard_map/all_to_all | solution.py:140
  83.4 4.4 %broadcast_in_dim.106 = bf16[8,64,2,4224]{3,1,2,0:T(8,128)(2,1)} broadcast(bf16[64,2,4224]{2,0,1:T(8,128)(2,1)S(1)} %copy.71), dimensions={1,2,3} | broadcast | bytes 9732096 | tf_op jit(solution)/shard_map/broadcast_in_dim | solution.py:142
  87.8 5.1 %all-to-all-start.1 = ((bf16[8,64,2,4224]{3,1,2,0:T(8,128)(2,1)}), bf16[8,64,2,4224]{3,1,2,0:T(8,128)(2,1)}, u32[]{:S(2)}, u32[]{:S(2)}) async-start(bf16[8,64,2,4224]{3,1,2,0:T(8,128)(2,1)} %broadcast_in_dim.106), calls=%async_computation.1 | async-start | bytes 17301504 | tf_op jit(solution)/shard_map/all_to_all | solution.py:141
  92.9 8.9 %pad_maximum_fusion = bf16[1179648]{0:T(1024)(128)(2,1)} fusion(bf16[393216]{0:T(1024)(128)(2,1)} %bitcast.118, bf16[393216]{0:T(1024)(128)(2,1)S(1)} %bitcast.117, bf16[393216]{0:T(1024)(128)(2,1)S(1)} %bitcast.116), kind=kLoop, calls=%fused_computation.2 | loop fusion | flops 7077888 | bytes 4718592 | tf_op jit(solution)/shard_map/concatenate | solution.py:81
  101.8 3.3 collective-permute-start
  105.1 0.6 dynamic_slice.10
  106.4 0.6 fusion.38
  107.7 81.8 %all-to-all-done.1 = bf16[8,64,2,4224]{3,1,2,0:T(8,128)(2,1)} async-done(((bf16[8,64,2,4224]{3,1,2,0:T(8,128)(2,1)}), bf16[8,64,2,4224]{3,1,2,0:T(8,128)(2,1)}, u32[]{:S(2)}, u32[]{:S(2)}) %all-to-all-start.1) | async-done | bytes 8650784 | tf_op jit(solution)/shard_map/all_to_all | solution.py:141
  189.5 1.0 slice_convert_fusion
  190.5 3.1 copy.85
  193.8 0.3 reduce-window.9
  195.1 5.8 %fusion.8 = f32[8,64,2,96]{3,1,2,0:T(8,128)S(1)} fusion(bf16[8,64,2,4224]{3,1,2,0:T(8,128)(2,1)} %all-to-all-done.1, bf16[96,4096]{1,0:T(8,128)(2,1)S(1)} %bitcast.115), kind=kOutput, calls=%fused_computation.17 | convolution fusion | flops 830472192 | bytes 9830400 | tf_op jit(solution)/shard_map/desf,hf->desh/dot_general | solution.py:165
  200.9 5.9 %fusion.1 = bf16[8,64,2,96]{3,1,2,0:T(8,128)(2,1)S(1)} fusion(bf16[8,64,2,4224]{3,1,2,0:T(8,128)(2,1)} %all-to-all-done.1, bf16[96,4096]{1,0:T(8,128)(2,1)S(1)} %bitcast.113, f32[8,64,2,96]{3,1,2,0:T(8,128)S(1)} %fusion.8, bf16[8,64,2]{1,2,0:T(2,128)(2,1)S(1)} %copy.75), kind=kOutput, calls=%fused_computation.6 | convolution fusion | flops 831160320 | bytes 10029056 | tf_op jit(solution)/shard_map/desf,hf->desh/dot_general | solution.py:168
  207.2 1.4 broadcast_in_dim.108
  208.6 4.3 %all-to-all-start.2 = ((bf16[8,1024,96]{1,2,0:T(8,128)(2,1)}), bf16[8,1024,96]{1,2,0:T(8,128)(2,1)}, u32[]{:S(2)}, u32[]{:S(2)}) async-start(bf16[8,1024,96]{1,2,0:T(8,128)(2,1)} %broadcast_in_dim.108), calls=%async_computation.2 | async-start | bytes 3145728 | tf_op jit(solution)/shard_map/all_to_all | solution.py:173
  213.6 40.9 %all-to-all-done.2 = bf16[8,1024,96]{1,2,0:T(8,128)(2,1)} async-done(((bf16[8,1024,96]{1,2,0:T(8,128)(2,1)}), bf16[8,1024,96]{1,2,0:T(8,128)(2,1)}, u32[]{:S(2)}, u32[]{:S(2)}) %all-to-all-start.2) | async-done | bytes 1572896 | tf_op jit(solution)/shard_map/all_to_all | solution.py:173
  254.5 3.4 bitcast_convert_fusion
  257.9 1.5 reshape.211
  259.4 2.2 copy.78
  261.6 11.1 %all-to-all-start.3 = ((bf16[8,64,2,512]{3,2,0,1:T(2,128)(2,1)}), bf16[8,64,2,512]{3,2,0,1:T(2,128)(2,1)S(1)}, u32[]{:S(2)}, u32[]{:S(2)}) async-start(bf16[8,64,2,512]{3,2,0,1:T(2,128)(2,1)} %copy.78), calls=%async_computation.3 | async-start | bytes 2097152 | tf_op jit(solution)/shard_map/all_to_all | solution.py:187
  272.7 3.1 fusion.37
  275.8 2.2 slice.67
  277.9 2.1 slice.69
  280.1 2.3 slice.71
  282.3 1.0 fusion.12
  283.3 41.2 %all-to-all-done.3 = bf16[8,64,2,512]{3,2,0,1:T(2,128)(2,1)S(1)} async-done(((bf16[8,64,2,512]{3,2,0,1:T(2,128)(2,1)}), bf16[8,64,2,512]{3,2,0,1:T(2,128)(2,1)S(1)}, u32[]{:S(2)}, u32[]{:S(2)}) %all-to-all-start.3) | async-done | bytes 1048608 | tf_op jit(solution)/shard_map/all_to_all | solution.py:187
  324.5 1.9 copy.79
  326.4 4.0 %all-to-all-start.4 = ((bf16[8,64,2,512]{3,2,1,0:T(2,128)(2,1)}), bf16[8,64,2,512]{3,2,1,0:T(2,128)(2,1)S(1)}, u32[]{:S(2)}, u32[]{:S(2)}) async-start(bf16[8,64,2,512]{3,2,1,0:T(2,128)(2,1)} %copy.79), calls=%async_computation.4 | async-start | bytes 2097152 | tf_op jit(solution)/shard_map/all_to_all | solution.py:186
  330.5 1.3 select_bitcast_fusion
  331.8 1.9 fusion.18
  335.0 10.1 %all-to-all-done.4 = bf16[8,64,2,512]{3,2,1,0:T(2,128)(2,1)S(1)} async-done(((bf16[8,64,2,512]{3,2,1,0:T(2,128)(2,1)}), bf16[8,64,2,512]{3,2,1,0:T(2,128)(2,1)S(1)}, u32[]{:S(2)}, u32[]{:S(2)}) %all-to-all-start.4) | async-done | bytes 1048608 | tf_op jit(solution)/shard_map/all_to_all | solution.py:186
  345.2 1.1 copy.80
  346.3 0.4 copy.89
  346.7 0.9 gather_fusion.1
  347.6 0.4 fusion.6
  348.1 0.7 add_convert_fusion
  (73 shorter events, 3.4 us)
Async XLA Ops:
  0.6 4.1 %copy-start = (bf16[8,16,512]{2,1,0:T(8,128)(2,1)S(1)}, bf16[8,16,512]{2,1,0:T(8,128)(2,1)}, u32[]{:S(2)}) copy-start(bf16[8,16,512]{2,1,0:T(8,128)(2,1)} %param.18) | copy-start | bytes 393220
  0.6 4.3 %copy-start.9 = (bf16[8,4096]{1,0:T(8,128)(2,1)S(1)}, bf16[8,4096]{1,0:T(8,128)(2,1)}, u32[]{:S(2)}) copy-start(bf16[8,4096]{1,0:T(8,128)(2,1)} %param.15) | copy-start | bytes 196612
  0.7 4.5 %copy-start.11 = (s32[8,8]{1,0:T(8,128)S(1)}, s32[8,8]{1,0:T(8,128)}, u32[]{:S(2)}) copy-start(s32[8,8]{1,0:T(8,128)} %param.23) | copy-start | bytes 772
  0.7 5.1 %copy-start.12 = (f32[4096]{0:T(1024)S(1)}, f32[4096]{0:T(1024)}, u32[]{:S(2)}) copy-start(f32[4096]{0:T(1024)} %param.22) | copy-start | bytes 49156
  5.0 0.8 copy-start.7
  10.4 21.9 %copy-start.2 = (bf16[1,96,4096]{2,1,0:T(8,128)(2,1)S(1)}, bf16[1,96,4096]{2,1,0:T(8,128)(2,1)}, u32[]{:S(2)}) copy-start(bf16[1,96,4096]{2,1,0:T(8,128)(2,1)} %param.28) | copy-start | bytes 2359300
  10.4 23.0 %copy-start.1 = (bf16[1,768,512]{2,1,0:T(8,128)(2,1)S(1)}, bf16[1,768,512]{2,1,0:T(8,128)(2,1)}, u32[]{:S(2)}) copy-start(bf16[1,768,512]{2,1,0:T(8,128)(2,1)} %param.29) | copy-start | bytes 2359300
  10.4 72.8 %all-to-all-start = ((bf16[64,2,4224]{2,1,0:T(2,128)(2,1)}), bf16[64,2,4224]{2,1,0:T(2,128)(2,1)S(1)}, u32[]{:S(2)}, u32[]{:S(2)}) async-start(bf16[64,2,4224]{2,1,0:T(2,128)(2,1)} %pad_maximum_fusion.1), calls=%async_computation | async-start | bytes 2162688 | tf_op jit(solution)/shard_map/all_to_all | solution.py:140
  87.8 5.1 %copy-start.5 = (bf16[12,32,8,128]{3,1,2,0:T(8,128)(2,1)S(1)}, bf16[12,32,8,128]{3,1,2,0:T(8,128)(2,1)}, u32[]{:S(2)}) copy-start(bf16[12,32,8,128]{3,1,2,0:T(8,128)(2,1)} %copy.90) | copy-start | bytes 2359300
  87.8 5.1 %copy-start.6 = (bf16[12,32,8,128]{3,1,2,0:T(8,128)(2,1)S(1)}, bf16[12,32,8,128]{3,1,2,0:T(8,128)(2,1)}, u32[]{:S(2)}) copy-start(bf16[12,32,8,128]{3,1,2,0:T(8,128)(2,1)} %copy.91) | copy-start | bytes 2359300
  87.8 101.7 %all-to-all-start.1 = ((bf16[8,64,2,4224]{3,1,2,0:T(8,128)(2,1)}), bf16[8,64,2,4224]{3,1,2,0:T(8,128)(2,1)}, u32[]{:S(2)}, u32[]{:S(2)}) async-start(bf16[8,64,2,4224]{3,1,2,0:T(8,128)(2,1)} %broadcast_in_dim.106), calls=%async_computation.1 | async-start | bytes 17301504 | tf_op jit(solution)/shard_map/all_to_all | solution.py:141
  92.9 12.2 %copy-start.15 = (s32[64]{0:T(128)S(1)}, s32[64]{0:T(128)}, u32[]{:S(2)}) copy-start(s32[64]{0:T(128)} %param.26) | copy-start | bytes 772
  92.9 13.5 %copy-start.14 = (s32[64]{0:T(128)S(1)}, s32[64]{0:T(128)}, u32[]{:S(2)}) copy-start(s32[64]{0:T(128)} %param.25) | copy-start | bytes 772
  101.8 93.3 %copy-start.3 = (bf16[1,96,4096]{2,1,0:T(8,128)(2,1)S(1)}, bf16[1,96,4096]{2,1,0:T(8,128)(2,1)}, u32[]{:S(2)}) copy-start(bf16[1,96,4096]{2,1,0:T(8,128)(2,1)} %param.27) | copy-start | bytes 2359300
  101.8 170.9 %collective-permute-start = (bf16[1179648]{0:T(1024)(128)(2,1)}, bf16[1179648]{0:T(1024)(128)(2,1)}, u32[]{:S(2)}, u32[]{:S(2)}) collective-permute-start(bf16[1179648]{0:T(1024)(128)(2,1)} %pad_maximum_fusion), channel_id=1, source_target_pairs={{0,256},{8,264},{16,272},{24,280},{32,288},{40,296},{48,304},{56,3... | collective-permute-start | bytes 7077896 | tf_op jit(solution)/shard_map/ppermute | solution.py:14
  208.6 46.0 %all-to-all-start.2 = ((bf16[8,1024,96]{1,2,0:T(8,128)(2,1)}), bf16[8,1024,96]{1,2,0:T(8,128)(2,1)}, u32[]{:S(2)}, u32[]{:S(2)}) async-start(bf16[8,1024,96]{1,2,0:T(8,128)(2,1)} %broadcast_in_dim.108), calls=%async_computation.2 | async-start | bytes 3145728 | tf_op jit(solution)/shard_map/all_to_all | solution.py:173
  261.6 62.9 %all-to-all-start.3 = ((bf16[8,64,2,512]{3,2,0,1:T(2,128)(2,1)}), bf16[8,64,2,512]{3,2,0,1:T(2,128)(2,1)S(1)}, u32[]{:S(2)}, u32[]{:S(2)}) async-start(bf16[8,64,2,512]{3,2,0,1:T(2,128)(2,1)} %copy.78), calls=%async_computation.3 | async-start | bytes 2097152 | tf_op jit(solution)/shard_map/all_to_all | solution.py:187
  283.3 47.2 %copy-start.4 = (bf16[96,4096]{1,0:T(8,128)(2,1)S(1)}, bf16[96,4096]{1,0:T(8,128)(2,1)}, u32[]{:S(2)}) copy-start(bf16[96,4096]{1,0:T(8,128)(2,1)} %slice.67) | copy-start | bytes 2359300
  326.4 18.7 %all-to-all-start.4 = ((bf16[8,64,2,512]{3,2,1,0:T(2,128)(2,1)}), bf16[8,64,2,512]{3,2,1,0:T(2,128)(2,1)S(1)}, u32[]{:S(2)}, u32[]{:S(2)}) async-start(bf16[8,64,2,512]{3,2,1,0:T(2,128)(2,1)} %copy.79), calls=%async_computation.4 | async-start | bytes 2097152 | tf_op jit(solution)/shard_map/all_to_all | solution.py:186
  346.7 0.9 copy-start.13
  346.7 1.4 copy-start.8
  346.7 1.4 copy-start.10

commit v14 on v12

--- a/solution.py
+++ b/solution.py
@@ -78,7 +78,21 @@
         widening_projection_matrix[0],
         output_projection_matrix[0],
     )
-    partner = swapped(own_weights, "expert", far_bit)
+    def x_step(direction):
+        pairs = []
+        for source in range(experts * groups):
+            e, d = divmod(source, groups)
+            x = 2 * (e // half_axis) + d // (groups // 2)
+            nx = (x + direction) % 4
+            e2 = (nx // 2) * half_axis + e % half_axis
+            d2 = (nx % 2) * (groups // 2) + d % (groups // 2)
+            pairs.append((source, e2 * groups + d2))
+        return pairs
+
+    both = ("expert", "dp")
+    gate_far = lax.ppermute(lax.ppermute(own_weights[0], both, x_step(1)), both, x_step(1))
+    up_far = lax.ppermute(lax.ppermute(own_weights[1], both, x_step(-1)), both, x_step(-1))
+    partner = (gate_far, up_far, swapped(own_weights[2], "expert", far_bit))
     take_other = swap_indicator[my_index] == 1
     retained_specialist = jnp.where(take_other, (my_index + half_axis) % experts, my_index)
 

time: 329 us -> 342 us (1.040)
  starting transfers between devices: 32 us -> 37.9 us
  waiting for transfers between devices: 148 us -> 152 us
    ppermute x0 -> x4, waiting for transfers between devices: none -> 51.2 us  [the longest x1 38.6 us: per_device(): lax.ppermute(own_weights[1], both, x_step(-1))]
    ppermute x3 -> x1, waiting for transfers between devices: 45 us -> 0.01 us  [swapped(): return lax.ppermute(value, axis, pairs)]
    ppermute x0 -> x4, starting transfers between devices: none -> 14 us  [the longest x1 5.56 us: per_device(): lax.ppermute(lax.ppermute(own_weights[1], both, x_step(-1)), both, x_step...]
    ppermute x3 -> x1, starting transfers between devices: 11.7 us -> 3.62 us  [swapped(): return lax.ppermute(value, axis, pairs)]
  transfers between devices with their start and end apart: 6 -> 8, of which waited for: 6 -> 4; matrix products, arithmetic and copies ran while one was open for 2% -> 2% of each run, Pallas kernels for 0% -> 0%
where the time goes in v14:
time: 342 us; the launch traced here: 337 us
  waiting for transfers between devices  152 us (44%)
  blocking collectives  95.9 us (28%)
  starting transfers between devices  37.9 us (11%)
  local copies, waits for them, and re-layouts  19.7 us (6%)
  matrix products  15.2 us (4%)
  other arithmetic  11.3 us (3%)
  between operations  5.59 us (2%)
    all_to_all x1, waiting for transfers between devices, per_device(): lax.all_to_all(jnp.broadcast_to(arrived[None], (groups,) + arrived.shape)...  94.1 us
    all_to_all x1, blocking collectives, per_device(): lax.all_to_all(payload, 'expert', split_axis=0, concat_axis=0, tiled=True)  72.5 us
    ppermute x1, waiting for transfers between devices, per_device(): lax.ppermute(own_weights[1], both, x_step(-1))  38.6 us
    all_to_all x1, blocking collectives, per_device(): lax.all_to_all(jnp.broadcast_to(hidden_block, (groups,) + hidden_block.sh...  23.4 us
    ppermute x1, waiting for transfers between devices, per_device(): lax.ppermute(lax.ppermute(own_weights[1], both, x_step(-1)), both, x_step...  12.6 us
    all_to_all x1, starting transfers between devices, per_device(): lax.all_to_all(results, 'expert', split_axis=1, concat_axis=1, tiled=True)  11.6 us
  transfers between devices with their start and end apart: 8, of which 4 were waited for; matrix products, arithmetic and copies ran while one was open for 2% of the time, Pallas kernels for 0%

profile of v14, /device:TPU:1, one launch (start us, length us, event | category | flops | bytes accessed | tf_op | source)
XLA Modules:
  0.0 337.5 jit_solution(11668720135793197513)
XLA Ops:
  0.7 0.8 iota_compare_fusion.2
  1.5 1.0 fusion.22
  2.5 1.2 fusion.38
  3.7 0.2 fusion.16
  4.0 0.7 bitcast_convert_fusion.1
  4.7 0.3 fusion.5
  5.3 0.3 select_reduce_fusion
  5.9 1.2 gather_fusion
  7.1 0.7 reshape.179
  8.1 0.2 fusion.19
  8.3 1.1 pad_maximum_fusion
  9.4 72.5 %all_to_all.35 = bf16[64,2,4224]{2,1,0:T(2,128)(2,1)S(1)} all-to-all(bf16[64,2,4224]{2,1,0:T(2,128)(2,1)S(1)} %pad_maximum_fusion), channel_id=1, replica_groups=mesh['expert'=64,'dp'=8] {'expert'}, dimensions={0} | all-to-all | bytes 2162688 | tf_op jit(solution)/shard_map/all_to_all | solution.py:147
  82.0 4.4 %broadcast_in_dim.106 = bf16[8,64,2,4224]{3,1,2,0:T(8,128)(2,1)} broadcast(bf16[64,2,4224]{2,0,1:T(8,128)(2,1)S(1)} %copy.71), dimensions={1,2,3} | broadcast | bytes 9732096 | tf_op jit(solution)/shard_map/broadcast_in_dim | solution.py:149
  86.4 5.1 %all-to-all-start.1 = ((bf16[8,64,2,4224]{3,1,2,0:T(8,128)(2,1)}), bf16[8,64,2,4224]{3,1,2,0:T(8,128)(2,1)}, u32[]{:S(2)}, u32[]{:S(2)}) async-start(bf16[8,64,2,4224]{3,1,2,0:T(8,128)(2,1)} %broadcast_in_dim.106), calls=%async_computation.1 | async-start | bytes 17301504 | tf_op jit(solution)/shard_map/all_to_all | solution.py:148
  91.6 0.6 dynamic_slice.10
  92.8 0.6 fusion.36
  94.1 94.1 %all-to-all-done.1 = bf16[8,64,2,4224]{3,1,2,0:T(8,128)(2,1)} async-done(((bf16[8,64,2,4224]{3,1,2,0:T(8,128)(2,1)}), bf16[8,64,2,4224]{3,1,2,0:T(8,128)(2,1)}, u32[]{:S(2)}, u32[]{:S(2)}) %all-to-all-start.1) | async-done | bytes 8650784 | tf_op jit(solution)/shard_map/all_to_all | solution.py:148
  188.1 1.0 slice_convert_fusion
  189.1 3.1 copy.85
  192.4 0.3 reduce-window.9
  192.7 0.2 reshape.181
  193.7 5.9 %fusion.8 = f32[8,64,2,96]{3,1,2,0:T(8,128)S(1)} fusion(bf16[8,64,2,4224]{3,1,2,0:T(8,128)(2,1)} %all-to-all-done.1, bf16[96,4096]{1,0:T(8,128)(2,1)S(1)} %bitcast.109), kind=kOutput, calls=%fused_computation.16 | convolution fusion | flops 830472192 | bytes 9830400 | tf_op jit(solution)/shard_map/desf,hf->desh/dot_general | solution.py:172
  199.6 5.9 %fusion.1 = bf16[8,64,2,96]{3,1,2,0:T(8,128)(2,1)S(1)} fusion(bf16[8,64,2,4224]{3,1,2,0:T(8,128)(2,1)} %all-to-all-done.1, bf16[96,4096]{1,0:T(8,128)(2,1)S(1)} %bitcast.106, f32[8,64,2,96]{3,1,2,0:T(8,128)S(1)} %fusion.8, bf16[8,64,2]{1,2,0:T(2,128)(2,1)S(1)} %copy.75), kind=kOutput, calls=%fused_computation.5 | convolution fusion | flops 831160320 | bytes 10029056 | tf_op jit(solution)/shard_map/desf,hf->desh/dot_general | solution.py:175
  205.5 0.3 copy.76
  206.1 23.4 %all_to_all.36 = bf16[8,1024,96]{1,2,0:T(8,128)(2,1)S(1)} all-to-all(bf16[8,1024,96]{1,2,0:T(8,128)(2,1)S(1)} %broadcast_in_dim.108), channel_id=1, replica_groups=mesh['expert'=64,'dp'=8] {'dp'}, dimensions={0} | all-to-all | bytes 3145728 | tf_op jit(solution)/shard_map/all_to_all | solution.py:180
  229.6 1.0 bitcast_convert_fusion
  230.6 0.4 reshape.184
  231.0 2.2 copy.78
  233.3 11.6 %all-to-all-start.3 = ((bf16[8,64,2,512]{3,2,0,1:T(2,128)(2,1)}), bf16[8,64,2,512]{3,2,0,1:T(2,128)(2,1)S(1)}, u32[]{:S(2)}, u32[]{:S(2)}) async-start(bf16[8,64,2,512]{3,2,0,1:T(2,128)(2,1)} %copy.78), calls=%async_computation.3 | async-start | bytes 2097152 | tf_op jit(solution)/shard_map/all_to_all | solution.py:194
  244.9 4.6 %collective-permute-start.2 = (bf16[96,4096]{1,0:T(8,128)(2,1)S(1)}, bf16[96,4096]{1,0:T(8,128)(2,1)}, u32[]{:S(2)}, u32[]{:S(2)}) collective-permute-start(bf16[96,4096]{1,0:T(8,128)(2,1)S(1)} %bitcast.107), channel_id=1, source_target_pairs={{0,260},{1,261},{2,262},{3,263},{4,0},{5,1},{6,2},{7,3},{8,268},{9... | collective-permute-start | bytes 2359304 | tf_op jit(solution)/shard_map/ppermute | solution.py:94
  249.5 1.9 collective-permute-start
  251.5 3.6 %collective-permute-start.4 = (bf16[768,512]{1,0:T(8,128)(2,1)S(1)}, bf16[768,512]{1,0:T(8,128)(2,1)}, u32[]{:S(2)}, u32[]{:S(2)}) collective-permute-start(bf16[768,512]{1,0:T(8,128)(2,1)S(1)} %bitcast.105), channel_id=1, source_target_pairs={{0,256},{8,264},{16,272},{24,280},{32,288},{40,296},{48,304},{56,3... | collective-permute-start | bytes 2359304 | tf_op jit(solution)/shard_map/ppermute | solution.py:14
  255.1 38.6 %collective-permute-done.2 = bf16[96,4096]{1,0:T(8,128)(2,1)} collective-permute-done((bf16[96,4096]{1,0:T(8,128)(2,1)S(1)}, bf16[96,4096]{1,0:T(8,128)(2,1)}, u32[]{:S(2)}, u32[]{:S(2)}) %collective-permute-start.2) | collective-permute-done | bytes 786464 | tf_op jit(solution)/shard_map/ppermute | solution.py:94
  293.7 5.6 %collective-permute-start.3 = (bf16[96,4096]{1,0:T(8,128)(2,1)}, bf16[96,4096]{1,0:T(8,128)(2,1)}, u32[]{:S(2)}, u32[]{:S(2)}) collective-permute-start(bf16[96,4096]{1,0:T(8,128)(2,1)} %collective-permute-done.2), channel_id=1, source_target_pairs={{0,260},{1,261},{2,262},{3,263},{4,0},{5,1},{6,2},{7,3},{8,268},{9... | collective-permute-start | bytes 2359304 | tf_op jit(solution)/shard_map/ppermute | solution.py:94
  300.0 1.9 collective-permute-start.1
  301.9 1.0 select_bitcast_fusion
  302.9 12.6 %collective-permute-done.3 = bf16[96,4096]{1,0:T(8,128)(2,1)} collective-permute-done((bf16[96,4096]{1,0:T(8,128)(2,1)}, bf16[96,4096]{1,0:T(8,128)(2,1)}, u32[]{:S(2)}, u32[]{:S(2)}) %collective-permute-start.3) | collective-permute-done | bytes 786464 | tf_op jit(solution)/shard_map/ppermute | solution.py:94
  315.5 1.0 select_bitcast_fusion.1
  316.5 1.9 copy.79
  318.4 3.6 %all-to-all-start.4 = ((bf16[8,64,2,512]{3,2,1,0:T(2,128)(2,1)}), bf16[8,64,2,512]{3,2,1,0:T(2,128)(2,1)S(1)}, u32[]{:S(2)}, u32[]{:S(2)}) async-start(bf16[8,64,2,512]{3,2,1,0:T(2,128)(2,1)} %copy.79), calls=%async_computation.4 | async-start | bytes 2097152 | tf_op jit(solution)/shard_map/all_to_all | solution.py:193
  322.0 1.0 select_bitcast_fusion.2
  322.9 1.9 fusion.17
  326.2 6.6 %all-to-all-done.4 = bf16[8,64,2,512]{3,2,1,0:T(2,128)(2,1)S(1)} async-done(((bf16[8,64,2,512]{3,2,1,0:T(2,128)(2,1)}), bf16[8,64,2,512]{3,2,1,0:T(2,128)(2,1)S(1)}, u32[]{:S(2)}, u32[]{:S(2)}) %all-to-all-start.4) | async-done | bytes 1048608 | tf_op jit(solution)/shard_map/all_to_all | solution.py:193
  332.8 1.1 copy.80
  333.9 0.4 copy.89
  334.3 0.9 gather_fusion.1
  335.2 0.4 fusion.6
  335.6 0.7 add_convert_fusion
  (64 shorter events, 2.4 us)
Async XLA Ops:
  0.6 4.1 %copy-start = (bf16[8,16,512]{2,1,0:T(8,128)(2,1)S(1)}, bf16[8,16,512]{2,1,0:T(8,128)(2,1)}, u32[]{:S(2)}) copy-start(bf16[8,16,512]{2,1,0:T(8,128)(2,1)} %param.18) | copy-start | bytes 393220
  0.6 4.3 %copy-start.6 = (bf16[8,4096]{1,0:T(8,128)(2,1)S(1)}, bf16[8,4096]{1,0:T(8,128)(2,1)}, u32[]{:S(2)}) copy-start(bf16[8,4096]{1,0:T(8,128)(2,1)} %param.15) | copy-start | bytes 196612
  0.7 4.5 %copy-start.7 = (s32[8,8]{1,0:T(8,128)S(1)}, s32[8,8]{1,0:T(8,128)}, u32[]{:S(2)}) copy-start(s32[8,8]{1,0:T(8,128)} %param.23) | copy-start | bytes 772
  0.7 5.1 %copy-start.8 = (f32[4096]{0:T(1024)S(1)}, f32[4096]{0:T(1024)}, u32[]{:S(2)}) copy-start(f32[4096]{0:T(1024)} %param.22) | copy-start | bytes 49156
  86.4 5.1 %copy-start.11 = (s32[64]{0:T(128)S(1)}, s32[64]{0:T(128)}, u32[]{:S(2)}) copy-start(s32[64]{0:T(128)} %param.26) | copy-start | bytes 772
  86.4 6.4 %copy-start.10 = (s32[64]{0:T(128)S(1)}, s32[64]{0:T(128)}, u32[]{:S(2)}) copy-start(s32[64]{0:T(128)} %param.25) | copy-start | bytes 772
  86.4 101.7 %all-to-all-start.1 = ((bf16[8,64,2,4224]{3,1,2,0:T(8,128)(2,1)}), bf16[8,64,2,4224]{3,1,2,0:T(8,128)(2,1)}, u32[]{:S(2)}, u32[]{:S(2)}) async-start(bf16[8,64,2,4224]{3,1,2,0:T(8,128)(2,1)} %broadcast_in_dim.106), calls=%async_computation.1 | async-start | bytes 17301504 | tf_op jit(solution)/shard_map/all_to_all | solution.py:148
  91.5 102.2 %copy-start.4 = (bf16[1,96,4096]{2,1,0:T(8,128)(2,1)S(1)}, bf16[1,96,4096]{2,1,0:T(8,128)(2,1)}, u32[]{:S(2)}) copy-start(bf16[1,96,4096]{2,1,0:T(8,128)(2,1)} %param.27) | copy-start | bytes 2359300
  193.7 5.9 %copy-start.2 = (bf16[1,96,4096]{2,1,0:T(8,128)(2,1)S(1)}, bf16[1,96,4096]{2,1,0:T(8,128)(2,1)}, u32[]{:S(2)}) copy-start(bf16[1,96,4096]{2,1,0:T(8,128)(2,1)} %param.28) | copy-start | bytes 2359300
  205.9 23.6 %copy-start.1 = (bf16[1,768,512]{2,1,0:T(8,128)(2,1)S(1)}, bf16[1,768,512]{2,1,0:T(8,128)(2,1)}, u32[]{:S(2)}) copy-start(bf16[1,768,512]{2,1,0:T(8,128)(2,1)} %param.29) | copy-start | bytes 2359300
  231.0 13.9 %copy-start.3 = (bf16[1,96,4096]{2,1,0:T(8,128)(2,1)S(1)}, bf16[1,96,4096]{2,1,0:T(8,128)(2,1)}, u32[]{:S(2)}) copy-start(bf16[1,96,4096]{2,1,0:T(8,128)(2,1)} %param.28) | copy-start | bytes 2359300
  233.3 83.2 %all-to-all-start.3 = ((bf16[8,64,2,512]{3,2,0,1:T(2,128)(2,1)}), bf16[8,64,2,512]{3,2,0,1:T(2,128)(2,1)S(1)}, u32[]{:S(2)}, u32[]{:S(2)}) async-start(bf16[8,64,2,512]{3,2,0,1:T(2,128)(2,1)} %copy.78), calls=%async_computation.3 | async-start | bytes 2097152 | tf_op jit(solution)/shard_map/all_to_all | solution.py:194
  244.9 48.8 %collective-permute-start.2 = (bf16[96,4096]{1,0:T(8,128)(2,1)S(1)}, bf16[96,4096]{1,0:T(8,128)(2,1)}, u32[]{:S(2)}, u32[]{:S(2)}) collective-permute-start(bf16[96,4096]{1,0:T(8,128)(2,1)S(1)} %bitcast.107), channel_id=1, source_target_pairs={{0,260},{1,261},{2,262},{3,263},{4,0},{5,1},{6,2},{7,3},{8,268},{9... | collective-permute-start | bytes 2359304 | tf_op jit(solution)/shard_map/ppermute | solution.py:94
  249.5 50.4 %collective-permute-start = (bf16[96,4096]{1,0:T(8,128)(2,1)}, bf16[96,4096]{1,0:T(8,128)(2,1)}, u32[]{:S(2)}, u32[]{:S(2)}) collective-permute-start(bf16[96,4096]{1,0:T(8,128)(2,1)} %bitcast.108), channel_id=1, source_target_pairs={{0,4},{1,5},{2,6},{3,7},{4,256},{5,257},{6,258},{7,259},{8,12},{9,... | collective-permute-start | bytes 2359304 | tf_op jit(solution)/shard_map/ppermute | solution.py:93
  251.5 50.4 %collective-permute-start.4 = (bf16[768,512]{1,0:T(8,128)(2,1)S(1)}, bf16[768,512]{1,0:T(8,128)(2,1)}, u32[]{:S(2)}, u32[]{:S(2)}) collective-permute-start(bf16[768,512]{1,0:T(8,128)(2,1)S(1)} %bitcast.105), channel_id=1, source_target_pairs={{0,256},{8,264},{16,272},{24,280},{32,288},{40,296},{48,304},{56,3... | collective-permute-start | bytes 2359304 | tf_op jit(solution)/shard_map/ppermute | solution.py:14
  293.7 21.9 %collective-permute-start.3 = (bf16[96,4096]{1,0:T(8,128)(2,1)}, bf16[96,4096]{1,0:T(8,128)(2,1)}, u32[]{:S(2)}, u32[]{:S(2)}) collective-permute-start(bf16[96,4096]{1,0:T(8,128)(2,1)} %collective-permute-done.2), channel_id=1, source_target_pairs={{0,260},{1,261},{2,262},{3,263},{4,0},{5,1},{6,2},{7,3},{8,268},{9... | collective-permute-start | bytes 2359304 | tf_op jit(solution)/shard_map/ppermute | solution.py:94
  300.0 22.0 %collective-permute-start.1 = (bf16[96,4096]{1,0:T(8,128)(2,1)}, bf16[96,4096]{1,0:T(8,128)(2,1)}, u32[]{:S(2)}, u32[]{:S(2)}) collective-permute-start(bf16[96,4096]{1,0:T(8,128)(2,1)} %collective-permute-done), channel_id=1, source_target_pairs={{0,4},{1,5},{2,6},{3,7},{4,256},{5,257},{6,258},{7,259},{8,12},{9,... | collective-permute-start | bytes 2359304 | tf_op jit(solution)/shard_map/ppermute | solution.py:93
  316.5 5.5 %copy-start.5 = (bf16[1,96,4096]{2,1,0:T(8,128)(2,1)S(1)}, bf16[1,96,4096]{2,1,0:T(8,128)(2,1)}, u32[]{:S(2)}) copy-start(bf16[1,96,4096]{2,1,0:T(8,128)(2,1)} %param.27) | copy-start | bytes 2359300
  318.4 14.4 %all-to-all-start.4 = ((bf16[8,64,2,512]{3,2,1,0:T(2,128)(2,1)}), bf16[8,64,2,512]{3,2,1,0:T(2,128)(2,1)S(1)}, u32[]{:S(2)}, u32[]{:S(2)}) async-start(bf16[8,64,2,512]{3,2,1,0:T(2,128)(2,1)} %copy.79), calls=%async_computation.4 | async-start | bytes 2097152 | tf_op jit(solution)/shard_map/all_to_all | solution.py:193
  334.3 0.9 copy-start.9

commit v15 on v12

--- a/solution.py
+++ b/solution.py
@@ -176,13 +176,8 @@
         "gsn,gnf->sf", hidden_all, down_split, preferred_element_type=jnp.float32
     )
     results = summed.astype(jnp.bfloat16).reshape(groups, experts, slot_cap, feature_cols)
-    returned = lax.all_to_all(
-        lax.all_to_all(results, "expert", split_axis=1, concat_axis=1, tiled=True),
-        "dp",
-        split_axis=0,
-        concat_axis=3,
-        tiled=True,
-    )
+    joined = lax.all_to_all(results, "dp", split_axis=0, concat_axis=3, tiled=True)[0]
+    returned = lax.all_to_all(joined, "expert", split_axis=0, concat_axis=0, tiled=True)
     returned_flat = returned.reshape(experts * slot_cap, width)
     picked = returned_flat[slot_code]
     expert_mix = jnp.sum(routing_probabilities[:, :, None] * picked.astype(jnp.float32), axis=1)

time: 329 us -> 338 us (1.027)
  blocking collectives: 95.9 us -> 112 us
    all_to_all x0 -> x1, blocking collectives: none -> 15.8 us  [per_device(): lax.all_to_all(results, 'dp', split_axis=0, concat_axis=3, tiled=True)[0]]
    all_to_all x2 -> x1, waiting for transfers between devices: 9.02 us -> 0.01 us  [per_device(): lax.all_to_all(joined, 'expert', split_axis=0, concat_axis=0, tiled=True)]
    ppermute x3, waiting for transfers between devices: 45 us -> 52.1 us  [swapped(): return lax.ppermute(value, axis, pairs)]
    all_to_all x2 -> x1, starting transfers between devices: 15.2 us -> 13 us  [per_device(): lax.all_to_all(joined, 'expert', split_axis=0, concat_axis=0, tiled=True)]
  transfers between devices with their start and end apart: 6 -> 5, of which waited for: 6 -> 4; matrix products, arithmetic and copies ran while one was open for 2% -> 2% of each run, Pallas kernels for 0% -> 0%
where the time goes in v15:
time: 338 us; the launch traced here: 337 us
  waiting for transfers between devices  146 us (43%)
  blocking collectives  112 us (33%)
  starting transfers between devices  29.8 us (9%)
  local copies, waits for them, and re-layouts  16.9 us (5%)
  matrix products  15.2 us (4%)
  other arithmetic  11.3 us (3%)
  between operations  5.56 us (2%)
    all_to_all x1, waiting for transfers between devices, per_device(): lax.all_to_all(jnp.broadcast_to(arrived[None], (groups,) + arrived.shape)...  94.1 us
    all_to_all x1, blocking collectives, per_device(): lax.all_to_all(payload, 'expert', split_axis=0, concat_axis=0, tiled=True)  72.5 us
    ppermute x3, waiting for transfers between devices, swapped(): return lax.ppermute(value, axis, pairs)  52.1 us
    all_to_all x1, blocking collectives, per_device(): lax.all_to_all(jnp.broadcast_to(hidden_block, (groups,) + hidden_block.sh...  23.4 us
    all_to_all x1, blocking collectives, per_device(): lax.all_to_all(results, 'dp', split_axis=0, concat_axis=3, tiled=True)[0]  15.8 us
    all_to_all x1, starting transfers between devices, per_device(): lax.all_to_all(joined, 'expert', split_axis=0, concat_axis=0, tiled=True)  13 us
    ppermute x3, starting transfers between devices, swapped(): return lax.ppermute(value, axis, pairs)  11.7 us
  transfers between devices with their start and end apart: 5, of which 4 were waited for; matrix products, arithmetic and copies ran while one was open for 2% of the time, Pallas kernels for 0%

profile of v15, /device:TPU:1, one launch (start us, length us, event | category | flops | bytes accessed | tf_op | source)
XLA Modules:
  0.0 336.6 jit_solution(7019635245469037865)
XLA Ops:
  0.7 0.8 iota_compare_fusion.2
  1.5 1.0 fusion.22
  2.5 1.2 fusion.38
  3.7 0.2 fusion.16
  4.0 0.7 bitcast_convert_fusion.1
  4.7 0.3 fusion.5
  5.0 0.2 multiply_reduce_fusion
  5.3 0.3 select_reduce_fusion
  5.9 1.2 gather_fusion
  7.1 0.7 reshape.179
  8.1 0.2 fusion.19
  8.3 1.1 pad_maximum_fusion
  9.4 72.5 %all_to_all.35 = bf16[64,2,4224]{2,1,0:T(2,128)(2,1)S(1)} all-to-all(bf16[64,2,4224]{2,1,0:T(2,128)(2,1)S(1)} %pad_maximum_fusion), channel_id=1, replica_groups=mesh['expert'=64,'dp'=8] {'expert'}, dimensions={0} | all-to-all | bytes 2162688 | tf_op jit(solution)/shard_map/all_to_all | solution.py:133
  82.0 4.4 %broadcast_in_dim.106 = bf16[8,64,2,4224]{3,1,2,0:T(8,128)(2,1)} broadcast(bf16[64,2,4224]{2,0,1:T(8,128)(2,1)S(1)} %copy.58), dimensions={1,2,3} | broadcast | bytes 9732096 | tf_op jit(solution)/shard_map/broadcast_in_dim | solution.py:135
  86.4 5.1 %all-to-all-start.1 = ((bf16[8,64,2,4224]{3,1,2,0:T(8,128)(2,1)}), bf16[8,64,2,4224]{3,1,2,0:T(8,128)(2,1)}, u32[]{:S(2)}, u32[]{:S(2)}) async-start(bf16[8,64,2,4224]{3,1,2,0:T(8,128)(2,1)} %broadcast_in_dim.106), calls=%async_computation.1 | async-start | bytes 17301504 | tf_op jit(solution)/shard_map/all_to_all | solution.py:134
  91.6 0.6 dynamic_slice.10
  92.8 0.6 fusion.36
  94.1 94.1 %all-to-all-done.1 = bf16[8,64,2,4224]{3,1,2,0:T(8,128)(2,1)} async-done(((bf16[8,64,2,4224]{3,1,2,0:T(8,128)(2,1)}), bf16[8,64,2,4224]{3,1,2,0:T(8,128)(2,1)}, u32[]{:S(2)}, u32[]{:S(2)}) %all-to-all-start.1) | async-done | bytes 8650784 | tf_op jit(solution)/shard_map/all_to_all | solution.py:134
  188.1 1.0 slice_convert_fusion
  189.1 3.1 copy.72
  192.4 0.3 reduce-window.9
  192.7 0.2 reshape.181
  193.0 0.2 copy.59
  193.7 5.9 %fusion.8 = f32[8,64,2,96]{3,1,2,0:T(8,128)S(1)} fusion(bf16[8,64,2,4224]{3,1,2,0:T(8,128)(2,1)} %all-to-all-done.1, bf16[96,4096]{1,0:T(8,128)(2,1)S(1)} %bitcast.106), kind=kOutput, calls=%fused_computation.16 | convolution fusion | flops 830472192 | bytes 9830400 | tf_op jit(solution)/shard_map/desf,hf->desh/dot_general | solution.py:158
  199.6 5.9 %fusion.1 = bf16[8,64,2,96]{3,1,2,0:T(8,128)(2,1)S(1)} fusion(bf16[8,64,2,4224]{3,1,2,0:T(8,128)(2,1)} %all-to-all-done.1, bf16[96,4096]{1,0:T(8,128)(2,1)S(1)} %bitcast.103, f32[8,64,2,96]{3,1,2,0:T(8,128)S(1)} %fusion.8, bf16[8,64,2]{1,2,0:T(2,128)(2,1)S(1)} %copy.62), kind=kOutput, calls=%fused_computation.5 | convolution fusion | flops 831160320 | bytes 10029056 | tf_op jit(solution)/shard_map/desf,hf->desh/dot_general | solution.py:161
  205.5 0.3 copy.63
  206.1 23.4 %all_to_all.36 = bf16[8,1024,96]{1,2,0:T(8,128)(2,1)S(1)} all-to-all(bf16[8,1024,96]{1,2,0:T(8,128)(2,1)S(1)} %broadcast_in_dim.108), channel_id=1, replica_groups=mesh['expert'=64,'dp'=8] {'dp'}, dimensions={0} | all-to-all | bytes 3145728 | tf_op jit(solution)/shard_map/all_to_all | solution.py:166
  229.6 1.0 bitcast_convert_fusion
  230.6 0.4 reshape.184
  231.0 0.2 copy.65
  231.2 15.8 %all_to_all.37 = bf16[8,64,2,512]{3,1,2,0:T(8,128)(2,1)S(1)} all-to-all(bf16[8,64,2,512]{3,1,2,0:T(8,128)(2,1)S(1)} %copy.65), channel_id=1, replica_groups=mesh['expert'=64,'dp'=8] {'dp'}, dimensions={0} | all-to-all | bytes 2097152 | tf_op jit(solution)/shard_map/all_to_all | solution.py:179
  247.0 0.6 copy.73
  247.6 1.6 reshape.214
  249.2 13.0 %all-to-all-start.4 = ((bf16[64,2,4096]{2,1,0:T(2,128)(2,1)}), bf16[64,2,4096]{2,1,0:T(2,128)(2,1)S(1)}, u32[]{:S(2)}, u32[]{:S(2)}) async-start(bf16[64,2,4096]{2,1,0:T(2,128)(2,1)} %reshape.214), calls=%async_computation.4 | async-start | bytes 2097152 | tf_op jit(solution)/shard_map/all_to_all | solution.py:180
  262.2 4.9 %collective-permute-start.2 = (bf16[768,512]{1,0:T(8,128)(2,1)S(1)}, bf16[768,512]{1,0:T(8,128)(2,1)}, u32[]{:S(2)}, u32[]{:S(2)}) collective-permute-start(bf16[768,512]{1,0:T(8,128)(2,1)S(1)} %bitcast.102), channel_id=1, source_target_pairs={{0,256},{8,264},{16,272},{24,280},{32,288},{40,296},{48,304},{56,3... | collective-permute-start | bytes 2359304 | tf_op jit(solution)/shard_map/ppermute | solution.py:14
  267.2 1.9 collective-permute-start.1
  269.1 4.9 %collective-permute-start = (bf16[96,4096]{1,0:T(8,128)(2,1)}, bf16[96,4096]{1,0:T(8,128)(2,1)}, u32[]{:S(2)}, u32[]{:S(2)}) collective-permute-start(bf16[96,4096]{1,0:T(8,128)(2,1)} %bitcast.105), channel_id=1, source_target_pairs={{0,256},{8,264},{16,272},{24,280},{32,288},{40,296},{48,304},{56,3... | collective-permute-start | bytes 2359304 | tf_op jit(solution)/shard_map/ppermute | solution.py:14
  274.7 13.7 %collective-permute-done.2 = bf16[768,512]{1,0:T(8,128)(2,1)} collective-permute-done((bf16[768,512]{1,0:T(8,128)(2,1)S(1)}, bf16[768,512]{1,0:T(8,128)(2,1)}, u32[]{:S(2)}, u32[]{:S(2)}) %collective-permute-start.2) | collective-permute-done | bytes 786464 | tf_op jit(solution)/shard_map/ppermute | solution.py:14
  288.4 1.0 select_bitcast_fusion
  289.3 22.2 %collective-permute-done.1 = bf16[96,4096]{1,0:T(8,128)(2,1)} collective-permute-done((bf16[96,4096]{1,0:T(8,128)(2,1)S(1)}, bf16[96,4096]{1,0:T(8,128)(2,1)}, u32[]{:S(2)}, u32[]{:S(2)}) %collective-permute-start.1) | collective-permute-done | bytes 786464 | tf_op jit(solution)/shard_map/ppermute | solution.py:14
  311.5 1.0 select_bitcast_fusion.1
  312.5 16.2 %collective-permute-done = bf16[96,4096]{1,0:T(8,128)(2,1)} collective-permute-done((bf16[96,4096]{1,0:T(8,128)(2,1)}, bf16[96,4096]{1,0:T(8,128)(2,1)}, u32[]{:S(2)}, u32[]{:S(2)}) %collective-permute-start) | collective-permute-done | bytes 786464 | tf_op jit(solution)/shard_map/ppermute | solution.py:14
  328.7 1.0 select_bitcast_fusion.2
  329.7 1.9 fusion.17
  333.0 0.4 reshape.185
  333.4 0.9 gather_fusion.1
  334.3 0.4 fusion.6
  334.8 0.7 add_convert_fusion
  (59 shorter events, 2.0 us)
Async XLA Ops:
  0.6 4.1 %copy-start = (bf16[8,16,512]{2,1,0:T(8,128)(2,1)S(1)}, bf16[8,16,512]{2,1,0:T(8,128)(2,1)}, u32[]{:S(2)}) copy-start(bf16[8,16,512]{2,1,0:T(8,128)(2,1)} %param.18) | copy-start | bytes 393220
  0.6 4.3 %copy-start.6 = (bf16[8,4096]{1,0:T(8,128)(2,1)S(1)}, bf16[8,4096]{1,0:T(8,128)(2,1)}, u32[]{:S(2)}) copy-start(bf16[8,4096]{1,0:T(8,128)(2,1)} %param.15) | copy-start | bytes 196612
  0.7 4.5 %copy-start.7 = (s32[8,8]{1,0:T(8,128)S(1)}, s32[8,8]{1,0:T(8,128)}, u32[]{:S(2)}) copy-start(s32[8,8]{1,0:T(8,128)} %param.23) | copy-start | bytes 772
  0.7 5.1 %copy-start.8 = (f32[4096]{0:T(1024)S(1)}, f32[4096]{0:T(1024)}, u32[]{:S(2)}) copy-start(f32[4096]{0:T(1024)} %param.22) | copy-start | bytes 49156
  86.4 5.1 %copy-start.11 = (s32[64]{0:T(128)S(1)}, s32[64]{0:T(128)}, u32[]{:S(2)}) copy-start(s32[64]{0:T(128)} %param.26) | copy-start | bytes 772
  86.4 6.4 %copy-start.10 = (s32[64]{0:T(128)S(1)}, s32[64]{0:T(128)}, u32[]{:S(2)}) copy-start(s32[64]{0:T(128)} %param.25) | copy-start | bytes 772
  86.4 101.7 %all-to-all-start.1 = ((bf16[8,64,2,4224]{3,1,2,0:T(8,128)(2,1)}), bf16[8,64,2,4224]{3,1,2,0:T(8,128)(2,1)}, u32[]{:S(2)}, u32[]{:S(2)}) async-start(bf16[8,64,2,4224]{3,1,2,0:T(8,128)(2,1)} %broadcast_in_dim.106), calls=%async_computation.1 | async-start | bytes 17301504 | tf_op jit(solution)/shard_map/all_to_all | solution.py:134
  91.5 102.2 %copy-start.4 = (bf16[1,96,4096]{2,1,0:T(8,128)(2,1)S(1)}, bf16[1,96,4096]{2,1,0:T(8,128)(2,1)}, u32[]{:S(2)}) copy-start(bf16[1,96,4096]{2,1,0:T(8,128)(2,1)} %param.27) | copy-start | bytes 2359300
  193.7 5.9 %copy-start.2 = (bf16[1,96,4096]{2,1,0:T(8,128)(2,1)S(1)}, bf16[1,96,4096]{2,1,0:T(8,128)(2,1)}, u32[]{:S(2)}) copy-start(bf16[1,96,4096]{2,1,0:T(8,128)(2,1)} %param.28) | copy-start | bytes 2359300
  205.9 23.6 %copy-start.1 = (bf16[1,768,512]{2,1,0:T(8,128)(2,1)S(1)}, bf16[1,768,512]{2,1,0:T(8,128)(2,1)}, u32[]{:S(2)}) copy-start(bf16[1,768,512]{2,1,0:T(8,128)(2,1)} %param.29) | copy-start | bytes 2359300
  247.6 19.6 %copy-start.3 = (bf16[1,96,4096]{2,1,0:T(8,128)(2,1)S(1)}, bf16[1,96,4096]{2,1,0:T(8,128)(2,1)}, u32[]{:S(2)}) copy-start(bf16[1,96,4096]{2,1,0:T(8,128)(2,1)} %param.28) | copy-start | bytes 2359300
  249.2 83.8 %all-to-all-start.4 = ((bf16[64,2,4096]{2,1,0:T(2,128)(2,1)}), bf16[64,2,4096]{2,1,0:T(2,128)(2,1)S(1)}, u32[]{:S(2)}, u32[]{:S(2)}) async-start(bf16[64,2,4096]{2,1,0:T(2,128)(2,1)} %reshape.214), calls=%async_computation.4 | async-start | bytes 2097152 | tf_op jit(solution)/shard_map/all_to_all | solution.py:180
  262.2 26.1 %collective-permute-start.2 = (bf16[768,512]{1,0:T(8,128)(2,1)S(1)}, bf16[768,512]{1,0:T(8,128)(2,1)}, u32[]{:S(2)}, u32[]{:S(2)}) collective-permute-start(bf16[768,512]{1,0:T(8,128)(2,1)S(1)} %bitcast.102), channel_id=1, source_target_pairs={{0,256},{8,264},{16,272},{24,280},{32,288},{40,296},{48,304},{56,3... | collective-permute-start | bytes 2359304 | tf_op jit(solution)/shard_map/ppermute | solution.py:14
  267.2 44.3 %collective-permute-start.1 = (bf16[96,4096]{1,0:T(8,128)(2,1)S(1)}, bf16[96,4096]{1,0:T(8,128)(2,1)}, u32[]{:S(2)}, u32[]{:S(2)}) collective-permute-start(bf16[96,4096]{1,0:T(8,128)(2,1)S(1)} %bitcast.104), channel_id=1, source_target_pairs={{0,256},{8,264},{16,272},{24,280},{32,288},{40,296},{48,304},{56,3... | collective-permute-start | bytes 2359304 | tf_op jit(solution)/shard_map/ppermute | solution.py:14
  269.1 59.6 %collective-permute-start = (bf16[96,4096]{1,0:T(8,128)(2,1)}, bf16[96,4096]{1,0:T(8,128)(2,1)}, u32[]{:S(2)}, u32[]{:S(2)}) collective-permute-start(bf16[96,4096]{1,0:T(8,128)(2,1)} %bitcast.105), channel_id=1, source_target_pairs={{0,256},{8,264},{16,272},{24,280},{32,288},{40,296},{48,304},{56,3... | collective-permute-start | bytes 2359304 | tf_op jit(solution)/shard_map/ppermute | solution.py:14
  274.7 54.0 %copy-start.5 = (bf16[1,96,4096]{2,1,0:T(8,128)(2,1)S(1)}, bf16[1,96,4096]{2,1,0:T(8,128)(2,1)}, u32[]{:S(2)}) copy-start(bf16[1,96,4096]{2,1,0:T(8,128)(2,1)} %param.27) | copy-start | bytes 2359300
  333.4 0.9 copy-start.9
